TPU v7x, 32 devices: a whole 2x2x4 slice. The times are simulated.
32 devices in a mesh: groups: 2 (over y), slide: 4 (over z), rep: 2 (over x), section: 2 (over core).
Axes of the slice: x: 2, y: 2, z: 4, core: 2. Of those that a mesh axis runs over, the one named last changes fastest.
Arguments:
- tile_features: bfloat16 [8, 12, 49, 1536], P(('groups', 'rep', 'section'), 'slide'), parts along dimension 0, may hold values from -6 to 6
- depth_weight: float32 [49, 1536], replicated, may hold values from -0.875 to 0.875
- depth_bias: float32 [1536], replicated, may hold values from -3 to 3
- norm_gain: float32 [1536], replicated, may hold values from 0.1 to 1.9
- norm_bias: float32 [1536], replicated, may hold values from -3 to 3
- up_weight: bfloat16 [1536, 3072], P(None, 'rep'), may hold values from -0.15625 to 0.15625
- up_bias: float32 [3072], P('rep'), may hold values from -3 to 3
- down_weight: bfloat16 [3072, 1536], P('rep'), may hold values from -0.109375 to 0.109375
- down_bias: float32 [1536], replicated, may hold values from -3 to 3
- layer_scale: float32 [1536], replicated, may hold values from 0.3 to 3
- head_gain: float32 [1536], replicated, may hold values from 0.1 to 1.9
- head_bias: float32 [1536], replicated, may hold values from -3 to 3
- embed_store: bfloat16 [8, 512, 1536], P(('groups', 'rep', 'section'), 'slide'), parts along dimension 0, may hold values from -6 to 6
- in_weight: bfloat16 [1536, 1024], P('slide'), may hold values from -0.15625 to 0.15625
- slide_gain: float32 [1024], replicated, may hold values from 0.1 to 1.9
- qkv_weight: bfloat16 [1024, 3072], P(None, 'slide'), may hold values from -0.1875 to 0.1875
- head_slopes: float32 [16], replicated, may hold values from 0.004 to 0.4
- tile_coords: int32 [8, 2, 512], P(('groups', 'rep', 'section')), parts along dimension 0, may hold values from 0 to 95, as said below
- valid_counts: int32 [8], P(('groups', 'rep', 'section')), parts along dimension 0, may hold values from 128 to 512, as said below
Outputs:
- fresh_embed: bfloat16 [8, 12, 1536], P(('groups', 'rep', 'section'), 'slide'), parts along dimension 0
- context: bfloat16 [8, 512, 1024], P(('groups', 'rep', 'section'), 'slide'), parts along dimension 0
There are 2 independent parts, one for each index of `groups`. A program takes and returns all parts, laid end to end along the dimension named above; an argument that names none is the same for every part. Nothing has to cross between parts.
Inputs may be any that keep to these rules, and one draw needn't show every extreme that they name: `tile_coords`: each slide's 512 positions sit on distinct cells of a 96 by 96 grid, in raster order (by y, then x); the cells (0, 0) and (95, 95) are always among them. `valid_counts`: positions at or beyond a slide's count are padding.
All inputs are finite; a program needn't handle non-finite values.
Results may differ from a plain program's by a relative error of at most 0.0078.
Values may be sent and summed in bfloat16 or wider, within the bound.
No kernel may reach another device: no remote copies, remote signals or barrier semaphores. Data moves between devices by JAX's collectives and lax.ppermute only.
A program may use at most 64 MiB of HBM per device.

v0:
```python
import math

import jax
import jax.numpy as jnp
from jax import lax
from jax.sharding import PartitionSpec as P

SIDE = 7
KER = 7
HDIM = 64


def layer_norm(inputs, gain, shift, epsilon):
    center = jnp.mean(inputs, axis=-1, keepdims=True)
    centered = inputs - center
    spread = jnp.mean(centered * centered, axis=-1, keepdims=True)
    return centered * lax.rsqrt(spread + epsilon) * gain + shift


def depthwise(tile_data, depth_weight, depth_bias):
    tile_count = tile_data.shape[0]
    channels = tile_data.shape[-1]
    spatial = tile_data.reshape(tile_count, SIDE, SIDE, channels)
    margin = KER // 2
    padded = jnp.pad(spatial, ((0, 0), (margin, margin), (margin, margin), (0, 0)))
    running = jnp.zeros_like(spatial) + depth_bias
    for tap_row in range(KER):
        for tap_col in range(KER):
            running = (
                running
                + padded[:, tap_row : tap_row + SIDE, tap_col : tap_col + SIDE, :]
                * depth_weight[tap_row * KER + tap_col]
            )
    return running.reshape(tile_count, SIDE * SIDE, channels)


def normalize_heads(values):
    row_total = values.shape[0]
    grouped = values.reshape(row_total, -1, 3, HDIM)
    paired = grouped[:, :, :2]
    scaled = paired * lax.rsqrt(jnp.mean(paired * paired, axis=-1, keepdims=True) + 1e-06)
    joined = jnp.concatenate([scaled, grouped[:, :, 2:]], axis=2)
    return joined.astype(jnp.bfloat16).reshape(row_total, -1)


def on_device(
    tile_features,
    depth_weight,
    depth_bias,
    norm_gain,
    norm_bias,
    up_weight,
    up_bias,
    down_weight,
    down_bias,
    layer_scale,
    head_gain,
    head_bias,
    embed_store,
    in_weight,
    slide_gain,
    qkv_weight,
    head_slopes,
    tile_coords,
    valid_counts,
):
    tile_data = tile_features[0].astype(jnp.float32)
    fresh_count = tile_data.shape[0]
    channels = tile_data.shape[-1]
    convolved = depthwise(tile_data, depth_weight, depth_bias)
    normed = (
        layer_norm(convolved, norm_gain, norm_bias, 1e-06)
        .astype(jnp.bfloat16)
        .reshape(-1, channels)
    )
    hidden = jax.nn.gelu(
        jnp.dot(
            lax.all_gather(normed, "rep", axis=0, tiled=True),
            up_weight,
            preferred_element_type=jnp.float32,
        )
        + up_bias,
        approximate=False,
    ).astype(jnp.bfloat16)
    summed = lax.psum_scatter(
        jnp.dot(hidden, down_weight, preferred_element_type=jnp.float32).astype(jnp.bfloat16),
        "rep",
        scatter_dimension=0,
        tiled=True,
    ).astype(jnp.float32)
    updated = tile_data + layer_scale * (summed.reshape(tile_data.shape) + down_bias)
    pooled = jnp.mean(updated, axis=1)
    embedded = layer_norm(pooled, head_gain, head_bias, 1e-06).astype(jnp.bfloat16)
    seq_rows = jnp.concatenate([embedded, embed_store[0, fresh_count:]], axis=0)
    projected = jnp.dot(
        seq_rows,
        lax.all_gather(in_weight, "slide", axis=0, tiled=True),
        preferred_element_type=jnp.float32,
    )
    normed_seq = layer_norm(projected, slide_gain, 0.0, 1e-05).astype(jnp.bfloat16)
    full_weight = lax.all_gather(qkv_weight, "slide", axis=1, tiled=True)
    packed = normalize_heads(jnp.dot(normed_seq, full_weight, preferred_element_type=jnp.float32))
    local_heads = lax.all_to_all(packed, "slide", split_axis=1, concat_axis=0, tiled=True)
    seq_len = local_heads.shape[0]
    heads_here = local_heads.shape[1] // (3 * HDIM)
    arranged = local_heads.reshape(seq_len, heads_here, 3, HDIM)
    queries = arranged[:, :, 0]
    key_rows = arranged[:, :, 1]
    value_rows = arranged[:, :, 2]
    my_slopes = lax.dynamic_slice_in_dim(
        head_slopes, lax.axis_index("slide") * heads_here, heads_here, 0
    )
    coord_x = tile_coords[0, 0].astype(jnp.float32)
    coord_y = tile_coords[0, 1].astype(jnp.float32)
    valid = valid_counts[0]
    key_ok = jnp.arange(seq_len, dtype=jnp.int32) < valid
    inv_root = 1.0 / math.sqrt(HDIM)
    block_len = min(512, seq_len)
    block_count = seq_len // block_len

    def one_block(block_index):
        first_row = block_index * block_len
        query_block = lax.dynamic_slice_in_dim(queries, first_row, block_len, 0)
        query_x = lax.dynamic_slice_in_dim(coord_x, first_row, block_len, 0)
        query_y = lax.dynamic_slice_in_dim(coord_y, first_row, block_len, 0)
        distance = jnp.abs(query_x[:, None] - coord_x[None, :]) + jnp.abs(
            query_y[:, None] - coord_y[None, :]
        )
        scores = (
            jnp.einsum("qhd,khd->hqk", query_block, key_rows, preferred_element_type=jnp.float32)
            * inv_root
            - my_slopes[:, None, None] * distance[None]
        )
        weights = jnp.where(key_ok[None, None, :], jnp.exp(scores), 0.0).astype(jnp.bfloat16)
        totals = jnp.sum(weights, axis=-1, dtype=jnp.float32)
        weighted = jnp.einsum(
            "hqk,khd->qhd", weights, value_rows, preferred_element_type=jnp.float32
        )
        query_ok = first_row + jnp.arange(block_len, dtype=jnp.int32) < valid
        safe = jnp.where(query_ok[None, :], totals, 1.0)
        result = jnp.where(query_ok[:, None, None], weighted / safe.T[:, :, None], 0.0)
        return result.astype(jnp.bfloat16).reshape(block_len, heads_here * HDIM)

    attended = lax.map(one_block, jnp.arange(block_count, dtype=jnp.int32)).reshape(
        seq_len, heads_here * HDIM
    )
    context = lax.all_to_all(attended, "slide", split_axis=0, concat_axis=1, tiled=True)
    return (embedded[None], context[None])


def solution(mesh):
    in_specs = (
        P(("groups", "rep", "section"), "slide", None, None),
        P(),
        P(),
        P(),
        P(),
        P(None, "rep"),
        P("rep"),
        P("rep", None),
        P(),
        P(),
        P(),
        P(),
        P(("groups", "rep", "section"), "slide", None),
        P("slide", None),
        P(),
        P(None, "slide"),
        P(),
        P(("groups", "rep", "section"), None, None),
        P(("groups", "rep", "section")),
    )
    out_specs = (
        P(("groups", "rep", "section"), "slide", None),
        P(("groups", "rep", "section"), "slide", None),
    )
    return jax.shard_map(
        on_device, mesh=mesh, in_specs=in_specs, out_specs=out_specs, check_vma=False
    )
```

profile of v0, /device:TPU:0, one launch (start us, length us, event | category | flops | bytes accessed | tf_op | source)
XLA Modules:
  0.0 245.6 jit_solution(2592706791371269726)
XLA Ops:
  7.2 0.7 all-gather.4.cloned.1.call-update
  8.0 0.7 all-gather.6.cloned.1.call-update
  9.7 7.9 %fusion.187 = (f32[3,7,7]{2,1,0:T(8,128)S(1)}, f32[3,7,7,1536]{3,2,1,0:T(8,128)S(1)}) fusion(f32[1536]{0:T(1024)S(1)} %get-tuple-element.81, f32[1536]{0:T(1024)S(1)} %get-tuple-element.82, f32[1536]{0:T(1024)S(1)} %get-tuple-element.25, f32[1536]{0:T(1024)S(1)} %get-tuple-element.26, f32[1536]{0:T(1024)S(1)} %get-tuple-element.27, ...), kind=kLoop, calls=%fused_computation.327 | loop fusion | flops 22353260 | bytes 2114124 | tf_op jit(solution)/shard_map/reduce_sum | solution.py:14
  18.5 14.3 %all-gather = bf16[2,147,1536]{2,1,0:T(8,128)(2,1)S(1)} all-gather(bf16[1,147,1536]{2,1,0:T(8,128)(2,1)S(1)} %fusion.143), channel_id=1, replica_groups=mesh['groups'=2,'slide'=4,'rep'=2,'section'=2] {'rep'}, dimensions={0}, use_global_device_ids=true | all-gather | bytes 1354752 | tf_op jit(solution)/shard_map/all_gather | solution.py:78
  33.0 10.5 %convolution_convert_fusion = bf16[294,1536]{1,0:T(8,128)(2,1)S(1)} fusion(bf16[1536,1536]{1,0:T(8,128)(2,1)} %param.26, bf16[294,1536]{1,0:T(8,128)(2,1)S(1)} %reshape.375, bf16[1536,1536]{1,0:T(8,128)(2,1)} %param.24, f32[1536]{0:T(1024)S(1)} %copy-done.13), kind=kOutput, calls=%fused_computation.52 | convolution fusion | flops 2804788224 | bytes 11249664 | tf_op jit(solution)/shard_map/dot_general | solution.py:86
  43.6 14.9 %fusion = bf16[152,1536]{1,0:T(8,128)(2,1)S(1)} fusion(bf16[294,1536]{1,0:T(8,128)(2,1)S(1)} %convolution_convert_fusion), kind=kCustom, calls=%all-reduce-scatter | all-reduce-scatter fusion | flops 466945 | bytes 1370624
  58.6 2.7 %collective-permute-start = (bf16[5,1536]{1,0:T(8,128)(2,1)S(1)}, bf16[5,1536]{1,0:T(8,128)(2,1)S(1)}, u32[]{:S(2)}, u32[]{:S(2)}) collective-permute-start(bf16[5,1536]{1,0:T(8,128)(2,1)S(1)} %slice.427), channel_id=1, source_target_pairs={{0,2},{1,3},{4,6},{5,7},{8,10},{9,11},{12,14},{13,15},{16,18},{17,... | collective-permute-start | bytes 46088
  61.4 0.6 dynamic-slice.4
  62.6 0.6 concatenate.9
  64.6 11.2 %all-gather.4.cloned.1.call-done = bf16[1536,1024]{1,0:T(8,128)(2,1)} async-done(((bf16[384,1024]{1,0:T(8,128)(2,1)}), bf16[1536,1024]{1,0:T(8,128)(2,1)}) %all-gather.4.cloned.1.call-update) | async-done | bytes 3145744 | tf_op jit(solution)/shard_map/all_gather | solution.py:97
  75.8 2.6 %fusion.189 = (f32[128]{0:T(128)S(1)}, f32[128,1024]{1,0:T(8,128)S(1)}) fusion(bf16[1536,1024]{1,0:T(8,128)(2,1)} %all-gather.4.cloned.1.call-done, bf16[125,1536]{1,0:T(8,128)(2,1)S(1)} %slice_bitcast_fusion, bf16[3,1536]{1,0:T(4,128)(2,1)S(1)} %add_convert_fusion.1), kind=kOutput, calls=%fused_computation.328 | convolution fusion | flops 403570560 | bytes 4063744 | tf_op jit(solution)/shard_map/dot_general | solution.py:95
  78.6 112.8 %all-gather.6.cloned.1.call-done = bf16[1024,3072]{1,0:T(8,128)(2,1)} async-done(((bf16[1024,768]{1,0:T(8,128)(2,1)}), bf16[1024,3072]{1,0:T(8,128)(2,1)}) %all-gather.6.cloned.1.call-update) | async-done | bytes 6291472 | tf_op jit(solution)/shard_map/all_gather | solution.py:101
  191.4 5.4 %fusion.148 = f32[128,3072]{0,1:T(8,128)S(1)} fusion(bf16[1024,3072]{1,0:T(8,128)(2,1)} %all-gather.6.cloned.1.call-done, f32[128,1024]{1,0:T(8,128)S(1)} %get-tuple-element.88, f32[1024]{0:T(1024)S(1)} %copy-done.10, f32[128]{0:T(128)S(1)} %add_rsqrt_fusion.2, f32[128]{0:T(128)S(1)} %broadcast_multiply_fusion.1), kind=kOutput, calls=%fused_computation.221 | convolution fusion | flops 805830656 | bytes 8393728 | tf_op jit(solution)/shard_map/dot_general | solution.py:102
  197.2 1.0 pad_maximum_fusion
  198.2 3.5 %all-to-all-start = ((bf16[128,4,768]{0,2,1:T(8,128)(2,1)}), bf16[128,4,768]{0,2,1:T(8,128)(2,1)S(1)}, u32[]{:S(2)}, u32[]{:S(2)}) async-start(bf16[128,4,768]{0,2,1:T(8,128)(2,1)} %bitcast.6), calls=%async_computation | async-start | bytes 1572864 | tf_op jit(solution)/shard_map/all_to_all | solution.py:103
  202.7 19.6 %all-to-all-done = bf16[128,4,768]{0,2,1:T(8,128)(2,1)S(1)} async-done(((bf16[128,4,768]{0,2,1:T(8,128)(2,1)}), bf16[128,4,768]{0,2,1:T(8,128)(2,1)S(1)}, u32[]{:S(2)}, u32[]{:S(2)}) %all-to-all-start) | async-done | bytes 786464 | tf_op jit(solution)/shard_map/all_to_all | solution.py:103
  222.2 0.6 copy.31
  223.2 1.5 convert_reduce_fusion
  224.7 0.5 fusion.13
  225.2 0.7 copy.36
  225.9 3.4 %all-to-all-start.1 = ((bf16[4,128,256]{1,2,0:T(8,128)(2,1)}), bf16[4,128,256]{1,2,0:T(8,128)(2,1)S(1)}, u32[]{:S(2)}, u32[]{:S(2)}) async-start(bf16[4,128,256]{1,2,0:T(8,128)(2,1)} %copy.36), calls=%async_computation.1 | async-start | bytes 524288 | tf_op jit(solution)/shard_map/all_to_all | solution.py:147
  229.4 0.7 fusion.155
  230.0 7.8 %all-to-all-done.1 = bf16[4,128,256]{1,2,0:T(8,128)(2,1)S(1)} async-done(((bf16[4,128,256]{1,2,0:T(8,128)(2,1)}), bf16[4,128,256]{1,2,0:T(8,128)(2,1)S(1)}, u32[]{:S(2)}, u32[]{:S(2)}) %all-to-all-start.1) | async-done | bytes 262176 | tf_op jit(solution)/shard_map/all_to_all | solution.py:147
  237.9 0.8 copy.37
  (69 shorter events, 4.8 us)
Async XLA Ops:
  7.2 1.5 copy-start
  7.2 1.7 copy-start.2
  7.2 68.7 %all-gather.4.cloned.1.call-start = ((), (), s32[]{:S(2)}) async-start(), calls=%async_computation.2 | async-start | bytes 3932160 | tf_op jit(solution)/shard_map/all_gather | solution.py:97
  7.9 1.8 copy-start.5
  7.9 183.5 %all-gather.6.cloned.1.call-start = ((), (), s32[]{:S(2)}) async-start(), calls=%async_computation.3 | async-start | bytes 7864320 | tf_op jit(solution)/shard_map/all_gather | solution.py:101
  17.5 0.7 copy-start.6
  17.5 0.7 copy-start.7
  18.5 14.5 %copy-start.13 = (f32[1536]{0:T(1024)S(1)}, f32[1536]{0:T(1024)}, u32[]{:S(2)}) copy-start(f32[1536]{0:T(1024)} %param.25) | copy-start | bytes 18436
  33.0 28.2 %copy-start.1 = (bf16[1,128,1536]{2,1,0:T(8,128)(2,1)S(1)}, bf16[1,128,1536]{2,1,0:T(8,128)(2,1)}, u32[]{:S(2)}) copy-start(bf16[1,128,1536]{2,1,0:T(8,128)(2,1)} %param.31) | copy-start | bytes 1179652
  43.6 17.8 %copy-start.12 = (u32[32]{0:T(128)S(1)}, u32[32]{0:T(128)}, u32[]{:S(2)}) copy-start(u32[32]{0:T(128)} %constant.125) | copy-start | bytes 388
  58.6 4.1 %collective-permute-start = (bf16[5,1536]{1,0:T(8,128)(2,1)S(1)}, bf16[5,1536]{1,0:T(8,128)(2,1)S(1)}, u32[]{:S(2)}, u32[]{:S(2)}) collective-permute-start(bf16[5,1536]{1,0:T(8,128)(2,1)S(1)} %slice.427), channel_id=1, source_target_pairs={{0,2},{1,3},{4,6},{5,7},{8,10},{9,11},{12,14},{13,15},{16,18},{17,... | collective-permute-start | bytes 46088
  63.2 0.7 copy-start.8
  63.2 0.7 copy-start.9
  63.4 1.1 copy-start.3
  63.4 1.1 copy-start.4
  64.6 126.9 %copy-start.10 = (f32[1024]{0:T(1024)S(1)}, f32[1024]{0:T(1024)}, u32[]{:S(2)}) copy-start(f32[1024]{0:T(1024)} %param.33) | copy-start | bytes 12292
  197.2 5.1 %copy-start.14 = (f32[16]{0:T(128)S(1)}, f32[16]{0:T(128)}, u32[]{:S(2)}) copy-start(f32[16]{0:T(128)} %param.35) | copy-start | bytes 196
  197.2 5.2 %copy-start.11 = (s32[1,2,512]{2,1,0:T(2,128)S(1)}, s32[1,2,512]{2,1,0:T(2,128)}, u32[]{:S(2)}) copy-start(s32[1,2,512]{2,1,0:T(2,128)} %param.36) | copy-start | bytes 12292
  198.2 24.1 %all-to-all-start = ((bf16[128,4,768]{0,2,1:T(8,128)(2,1)}), bf16[128,4,768]{0,2,1:T(8,128)(2,1)S(1)}, u32[]{:S(2)}, u32[]{:S(2)}) async-start(bf16[128,4,768]{0,2,1:T(8,128)(2,1)} %bitcast.6), calls=%async_computation | async-start | bytes 1572864 | tf_op jit(solution)/shard_map/all_to_all | solution.py:103
  225.9 11.9 %all-to-all-start.1 = ((bf16[4,128,256]{1,2,0:T(8,128)(2,1)}), bf16[4,128,256]{1,2,0:T(8,128)(2,1)S(1)}, u32[]{:S(2)}, u32[]{:S(2)}) async-start(bf16[4,128,256]{1,2,0:T(8,128)(2,1)} %copy.36), calls=%async_computation.1 | async-start | bytes 524288 | tf_op jit(solution)/shard_map/all_to_all | solution.py:147
Sparse Core Ops, SparseCore 0:
  9.6 66.2 all-gather.3
  77.4 113.9 all-gather.5
where the time goes:
time: 246 us
  waiting for transfers between devices  153 us (62%)
  blocking collectives  29.3 us (12%)
  matrix products  20.5 us (8%)
  between operations  15.7 us (6%)
  other arithmetic  11.5 us (5%)
  starting transfers between devices  9.67 us (4%)
  local copies, waits for them, and re-layouts  6.05 us (2%)
    all_gather x1, waiting for transfers between devices, on_device(): full_weight = lax.all_gather(qkv_weight, 'slide', axis=1, tiled=True)  113 us
    all_to_all x1, waiting for transfers between devices, on_device(): lax.all_to_all(packed, 'slide', split_axis=1, concat_axis=0, tiled=True)  19.6 us
    unnamed x1, blocking collectives  14.9 us
    all_gather x1, blocking collectives, on_device(): lax.all_gather(normed, 'rep', axis=0, tiled=True)  14.3 us
    all_gather x1, waiting for transfers between devices, on_device(): lax.all_gather(in_weight, 'slide', axis=0, tiled=True)  11.2 us
    dot_general x1, matrix products, on_device(): jnp.dot(hidden, down_weight, preferred_element_type=jnp.float32)  10.5 us
    reduce_sum x2, other arithmetic, layer_norm(): center = jnp.mean(inputs, axis=-1, keepdims=True)  8 us
    all_to_all x1, waiting for transfers between devices, on_device(): lax.all_to_all(attended, 'slide', split_axis=0, concat_axis=1, tiled=True)  7.82 us
  transfers between devices with their start and end apart: 5, of which 4 were waited for; matrix products, arithmetic and copies ran while one was open for 17% of the time, Pallas kernels for 0%

commit v1 on v0

--- a/solution.py
+++ b/solution.py
@@ -35,12 +35,19 @@
 
 
 def normalize_heads(values):
-    row_total = values.shape[0]
-    grouped = values.reshape(row_total, -1, 3, HDIM)
-    paired = grouped[:, :, :2]
+    lead = values.shape[:-1]
+    grouped = values.reshape(lead + (-1, 3, HDIM))
+    paired = grouped[..., :2, :]
     scaled = paired * lax.rsqrt(jnp.mean(paired * paired, axis=-1, keepdims=True) + 1e-06)
-    joined = jnp.concatenate([scaled, grouped[:, :, 2:]], axis=2)
-    return joined.astype(jnp.bfloat16).reshape(row_total, -1)
+    joined = jnp.concatenate([scaled, grouped[..., 2:, :]], axis=-2)
+    return joined.astype(jnp.bfloat16).reshape(lead + (-1,))
+
+
+def project(rows, weight_parts, slide_gain):
+    projected = jnp.einsum(
+        "nk,skc->nsc", rows, weight_parts, preferred_element_type=jnp.float32
+    ).reshape(rows.shape[0], -1)
+    return layer_norm(projected, slide_gain, 0.0, 1e-05).astype(jnp.bfloat16)
 
 
 def on_device(
@@ -64,8 +71,22 @@
     tile_coords,
     valid_counts,
 ):
+    n_sec = lax.axis_size("section")
+    col_part = in_weight.shape[1] // n_sec
+    my_cols = lax.dynamic_slice_in_dim(
+        in_weight, lax.axis_index("section") * col_part, col_part, 1
+    )
+    cols_full = lax.all_gather(my_cols, "slide", axis=0, tiled=True)
+    weight_parts = lax.all_gather(cols_full, "section", axis=0, tiled=False)
+
+    fresh_count = tile_features.shape[1]
+    stale_normed = project(embed_store[0], weight_parts, slide_gain)
+    stale_all = lax.all_gather(stale_normed, "slide", axis=0, tiled=False)
+    stale_mixed = normalize_heads(
+        jnp.einsum("rnk,kc->rnc", stale_all, qkv_weight, preferred_element_type=jnp.float32)
+    )
+
     tile_data = tile_features[0].astype(jnp.float32)
-    fresh_count = tile_data.shape[0]
     channels = tile_data.shape[-1]
     convolved = depthwise(tile_data, depth_weight, depth_bias)
     normed = (
@@ -91,17 +112,17 @@
     updated = tile_data + layer_scale * (summed.reshape(tile_data.shape) + down_bias)
     pooled = jnp.mean(updated, axis=1)
     embedded = layer_norm(pooled, head_gain, head_bias, 1e-06).astype(jnp.bfloat16)
-    seq_rows = jnp.concatenate([embedded, embed_store[0, fresh_count:]], axis=0)
-    projected = jnp.dot(
-        seq_rows,
-        lax.all_gather(in_weight, "slide", axis=0, tiled=True),
-        preferred_element_type=jnp.float32,
+
+    fresh_normed = project(embedded, weight_parts, slide_gain)
+    fresh_all = lax.all_gather(fresh_normed, "slide", axis=0, tiled=False)
+    fresh_mixed = normalize_heads(
+        jnp.einsum("rnk,kc->rnc", fresh_all, qkv_weight, preferred_element_type=jnp.float32)
     )
-    normed_seq = layer_norm(projected, slide_gain, 0.0, 1e-05).astype(jnp.bfloat16)
-    full_weight = lax.all_gather(qkv_weight, "slide", axis=1, tiled=True)
-    packed = normalize_heads(jnp.dot(normed_seq, full_weight, preferred_element_type=jnp.float32))
-    local_heads = lax.all_to_all(packed, "slide", split_axis=1, concat_axis=0, tiled=True)
-    seq_len = local_heads.shape[0]
+    local_heads = jnp.concatenate([fresh_mixed, stale_mixed[:, fresh_count:]], axis=1)
+    n_slide = local_heads.shape[0]
+    seq_len = n_slide * local_heads.shape[1]
+    local_heads = local_heads.reshape(seq_len, -1)
+
     heads_here = local_heads.shape[1] // (3 * HDIM)
     arranged = local_heads.reshape(seq_len, heads_here, 3, HDIM)
     queries = arranged[:, :, 0]
@@ -115,35 +136,21 @@
     valid = valid_counts[0]
     key_ok = jnp.arange(seq_len, dtype=jnp.int32) < valid
     inv_root = 1.0 / math.sqrt(HDIM)
-    block_len = min(512, seq_len)
-    block_count = seq_len // block_len
 
-    def one_block(block_index):
-        first_row = block_index * block_len
-        query_block = lax.dynamic_slice_in_dim(queries, first_row, block_len, 0)
-        query_x = lax.dynamic_slice_in_dim(coord_x, first_row, block_len, 0)
-        query_y = lax.dynamic_slice_in_dim(coord_y, first_row, block_len, 0)
-        distance = jnp.abs(query_x[:, None] - coord_x[None, :]) + jnp.abs(
-            query_y[:, None] - coord_y[None, :]
-        )
-        scores = (
-            jnp.einsum("qhd,khd->hqk", query_block, key_rows, preferred_element_type=jnp.float32)
-            * inv_root
-            - my_slopes[:, None, None] * distance[None]
-        )
-        weights = jnp.where(key_ok[None, None, :], jnp.exp(scores), 0.0).astype(jnp.bfloat16)
-        totals = jnp.sum(weights, axis=-1, dtype=jnp.float32)
-        weighted = jnp.einsum(
-            "hqk,khd->qhd", weights, value_rows, preferred_element_type=jnp.float32
-        )
-        query_ok = first_row + jnp.arange(block_len, dtype=jnp.int32) < valid
-        safe = jnp.where(query_ok[None, :], totals, 1.0)
-        result = jnp.where(query_ok[:, None, None], weighted / safe.T[:, :, None], 0.0)
-        return result.astype(jnp.bfloat16).reshape(block_len, heads_here * HDIM)
-
-    attended = lax.map(one_block, jnp.arange(block_count, dtype=jnp.int32)).reshape(
-        seq_len, heads_here * HDIM
+    distance = jnp.abs(coord_x[:, None] - coord_x[None, :]) + jnp.abs(
+        coord_y[:, None] - coord_y[None, :]
     )
+    scores = (
+        jnp.einsum("qhd,khd->hqk", queries, key_rows, preferred_element_type=jnp.float32)
+        * inv_root
+        - my_slopes[:, None, None] * distance[None]
+    )
+    weights = jnp.where(key_ok[None, None, :], jnp.exp(scores), 0.0).astype(jnp.bfloat16)
+    totals = jnp.sum(weights, axis=-1, dtype=jnp.float32)
+    weighted = jnp.einsum("hqk,khd->qhd", weights, value_rows, preferred_element_type=jnp.float32)
+    safe = jnp.where(key_ok[None, :], totals, 1.0)
+    attended = jnp.where(key_ok[:, None, None], weighted / safe.T[:, :, None], 0.0)
+    attended = attended.astype(jnp.bfloat16).reshape(seq_len, heads_here * HDIM)
     context = lax.all_to_all(attended, "slide", split_axis=0, concat_axis=1, tiled=True)
     return (embedded[None], context[None])
 

time: 246 us -> 163 us (0.66)
  waiting for transfers between devices: 153 us -> 19.2 us
  other arithmetic: 11.5 us -> 40.4 us
  blocking collectives: 29.3 us -> 42.8 us
  local copies, waits for them, and re-layouts: 6.05 us -> 15.5 us
  starting transfers between devices: 9.67 us -> 6.21 us
    all_gather x2 -> x3, waiting for transfers between devices: 124 us -> 10.8 us  [the longest x1 10.7 us: on_device(): stale_all = lax.all_gather(stale_normed, 'slide', axis=0, tiled=False)]
    reduce_sum x2, other arithmetic: 8 us -> 31.9 us  [layer_norm(): center = jnp.mean(inputs, axis=-1, keepdims=True)]
    all_to_all x1 -> x0, waiting for transfers between devices: 19.6 us -> none  [on_device(): lax.all_to_all(packed, 'slide', split_axis=1, concat_axis=0, tiled=True)]
    all_gather x0 -> x1, blocking collectives: none -> 13.5 us  [on_device(): fresh_all = lax.all_gather(fresh_normed, 'slide', axis=0, tiled=False)]
    slice x3, local copies, waits for them, and re-layouts: 0.82 us -> 4.82 us  [depthwise(): depth_weight[tap_row * KER + tap_col]]
    all_to_all x1 -> x0, starting transfers between devices: 3.49 us -> none  [on_device(): lax.all_to_all(packed, 'slide', split_axis=1, concat_axis=0, tiled=True)]
    dot_general x4 -> x6, matrix products: 9.93 us -> 12 us  [the longest x2 5.54 us: project(): jnp.einsum('nk,skc->nsc', rows, weight_parts, preferred_element_type=jnp....]
  transfers between devices with their start and end apart: 5 -> 5, of which waited for: 4 -> 2; matrix products, arithmetic and copies ran while one was open for 17% -> 47% of each run, Pallas kernels for 0% -> 0%
where the time goes in v1:
time: 163 us; the launch traced here: 162 us
  blocking collectives  42.8 us (26%)
  other arithmetic  40.4 us (25%)
  matrix products  22.5 us (14%)
  waiting for transfers between devices  19.2 us (12%)
  local copies, waits for them, and re-layouts  15.5 us (10%)
  between operations  15.5 us (10%)
  starting transfers between devices  6.21 us (4%)
    reduce_sum x2, other arithmetic, layer_norm(): center = jnp.mean(inputs, axis=-1, keepdims=True)  31.9 us
    unnamed x1, blocking collectives  15 us
    all_gather x1, blocking collectives, on_device(): lax.all_gather(normed, 'rep', axis=0, tiled=True)  14.3 us
    all_gather x1, blocking collectives, on_device(): fresh_all = lax.all_gather(fresh_normed, 'slide', axis=0, tiled=False)  13.5 us
    all_gather x1, waiting for transfers between devices, on_device(): stale_all = lax.all_gather(stale_normed, 'slide', axis=0, tiled=False)  10.7 us
    dot_general x1, matrix products, on_device(): jnp.dot(hidden, down_weight, preferred_element_type=jnp.float32)  10.4 us
    all_to_all x1, waiting for transfers between devices, on_device(): lax.all_to_all(attended, 'slide', split_axis=0, concat_axis=1, tiled=True)  8.38 us
    dot_general x2, matrix products, project(): jnp.einsum('nk,skc->nsc', rows, weight_parts, preferred_element_type=jnp....  5.54 us
  transfers between devices with their start and end apart: 5, of which 2 were waited for; matrix products, arithmetic and copies ran while one was open for 47% of the time, Pallas kernels for 0%

profile of v1, /device:TPU:0, one launch (start us, length us, event | category | flops | bytes accessed | tf_op | source)
XLA Modules:
  0.0 162.0 jit_solution(1673579185459483674)
XLA Ops:
  7.3 1.9 %constant_dynamic-slice_fusion = bf16[384,512]{1,0:T(8,128)(2,1)} fusion(bf16[384,1024]{1,0:T(8,128)(2,1)} %param.32, s32[]{:T(128)S(6)} %select_n.22), kind=kLoop, calls=%fused_computation.311 | loop fusion | bytes 786436 | tf_op jit(solution)/shard_map/dynamic_slice | solution.py:76
  9.2 1.8 %slice_reduce_fusion.48 = (f32[1536]{0:T(1024)S(1)}, f32[1536]{0:T(1024)S(1)}, f32[1536]{0:T(1024)S(1)}, f32[1536]{0:T(1024)S(1)}, f32[1536]{0:T(1024)S(1)}, /*i...) fusion(f32[49,1536]{1,0:T(8,128)} %param.20), kind=kLoop, calls=%fused_computation.302 | loop fusion | bytes 233472 | tf_op jit(solution)/shard_map/slice | solution.py:32
  11.1 1.7 %slice_reduce_fusion.47 = (f32[1536]{0:T(1024)S(1)}, f32[1536]{0:T(1024)S(1)}, f32[1536]{0:T(1024)S(1)}, f32[1536]{0:T(1024)S(1)}, f32[1536]{0:T(1024)S(1)}, /*i...) fusion(f32[49,1536]{1,0:T(8,128)} %param.20), kind=kLoop, calls=%fused_computation.301 | loop fusion | bytes 233472 | tf_op jit(solution)/shard_map/slice | solution.py:32
  12.8 1.3 slice_reduce_fusion.46
  14.1 1.1 reshape.558
  15.2 31.7 %fusion.194 = (f32[3,7,7]{2,1,0:T(8,128)}, f32[3,7,7,1536]{3,2,1,0:T(8,128)S(1)}) fusion(f32[1536]{0:T(1024)S(1)} %get-tuple-element.51, f32[1536]{0:T(1024)S(1)} %get-tuple-element.52, f32[1536]{0:T(1024)S(1)} %get-tuple-element.5, f32[1536]{0:T(1024)S(1)} %get-tuple-element.6, f32[1536]{0:T(1024)S(1)} %get-tuple-element.7, f32[1536]{0:T(1024)S(1)} %get-tuple-element.8, ...), kind=kLoop, calls=%fused_computation.344 | loop fusion | flops 22353260 | bytes 2114124 | tf_op jit(solution)/shard_map/reduce_sum | solution.py:14
  48.3 0.9 fusion.149
  49.2 14.3 %all-gather.1 = bf16[2,147,1536]{2,1,0:T(8,128)(2,1)S(1)} all-gather(bf16[1,147,1536]{2,1,0:T(8,128)(2,1)S(1)} %fusion.149), channel_id=1, replica_groups=mesh['groups'=2,'slide'=4,'rep'=2,'section'=2] {'rep'}, dimensions={0}, use_global_device_ids=true | all-gather | bytes 1354752 | tf_op jit(solution)/shard_map/all_gather | solution.py:99
  64.2 10.4 %convolution_convert_fusion = bf16[294,1536]{1,0:T(8,128)(2,1)S(1)} fusion(bf16[1536,1536]{1,0:T(8,128)(2,1)} %param.26, bf16[294,1536]{1,0:T(8,128)(2,1)S(1)} %reshape.563, bf16[1536,1536]{1,0:T(8,128)(2,1)} %param.24, f32[1536]{0:T(1024)S(1)} %copy-done.12), kind=kOutput, calls=%fused_computation.52 | convolution fusion | flops 2804788224 | bytes 11249664 | tf_op jit(solution)/shard_map/dot_general | solution.py:107
  74.7 15.0 %fusion = bf16[152,1536]{1,0:T(8,128)(2,1)S(1)} fusion(bf16[294,1536]{1,0:T(8,128)(2,1)S(1)} %convolution_convert_fusion), kind=kCustom, calls=%all-reduce-scatter | all-reduce-scatter fusion | flops 466945 | bytes 1370624
  89.7 2.5 %collective-permute-start = (bf16[5,1536]{1,0:T(8,128)(2,1)S(1)}, bf16[5,1536]{1,0:T(8,128)(2,1)S(1)}, u32[]{:S(2)}, u32[]{:S(2)}) collective-permute-start(bf16[5,1536]{1,0:T(8,128)(2,1)S(1)} %slice.439), channel_id=1, source_target_pairs={{0,2},{1,3},{4,6},{5,7},{8,10},{9,11},{12,14},{13,15},{16,18},{17,... | collective-permute-start | bytes 46088
  92.9 1.3 abs_add_fusion
  97.9 1.3 fusion.115
  99.5 3.0 %fusion.196 = (f32[128]{0:T(128)S(1)}, f32[2,512,128]{2,1,0:T(8,128)S(1)}) fusion(bf16[2,1536,512]{2,1,0:T(8,128)(2,1)} %bitcast.97, bf16[1,128,1536]{2,1,0:T(8,128)(2,1)} %param.31), kind=kOutput, calls=%fused_computation.345 | convolution fusion | flops 402784128 | bytes 4063744 | tf_op jit(solution)/shard_map/nk,skc->nsc/dot_general | solution.py:47
  103.8 2.6 %fusion.197 = (f32[3]{0:T(128)S(1)}, f32[3,2,512]{2,0,1:T(4,128)S(1)}) fusion(bf16[2,1536,512]{2,1,0:T(8,128)(2,1)} %bitcast.98, f32[1536]{0:T(1024)S(1)} %copy-done.3, f32[3,1536]{1,0:T(4,128)S(1)} %fusion.115, f32[1536]{0:T(1024)S(1)} %copy-done.4, f32[3]{0:T(128)S(1)} %add_rsqrt_fusion.5, f32[3]{0:T(128)S(1)} %broadcast_multiply_fusion.3), kind=kOutput, calls=%fused_computation.346 | convolution fusion | flops 9467901 | bytes 3188772 | tf_op jit(solution)/shard_map/nk,skc->nsc/dot_general | solution.py:47
  106.6 13.5 %all_gather.24 = bf16[4,3,1024]{2,1,0:T(4,128)(2,1)S(1)} all-gather(bf16[1,3,1024]{2,1,0:T(4,128)(2,1)S(1)} %multiply_convert_fusion.3), channel_id=1, replica_groups=mesh['groups'=2,'slide'=4,'rep'=2,'section'=2] {'slide'}, dimensions={0}, use_global_device_ids=true | all-gather | bytes 30720 | tf_op jit(solution)/shard_map/all_gather | solution.py:117
  121.5 10.7 %all-gather.8.cloned.1.call-done = bf16[4,128,1024]{2,1,0:T(8,128)(2,1)} async-done(((bf16[1,128,1024]{2,1,0:T(8,128)(2,1)}), bf16[4,128,1024]{2,1,0:T(8,128)(2,1)}) %all-gather.8.cloned.1.call-update) | async-done | bytes 1048592 | tf_op jit(solution)/shard_map/all_gather | solution.py:84
  132.2 2.2 %fusion.11 = f32[4,128,768]{1,2,0:T(8,128)S(1)} fusion(bf16[4,128,1024]{2,1,0:T(8,128)(2,1)} %all-gather.8.cloned.1.call-done, bf16[1024,768]{1,0:T(8,128)(2,1)S(1)} %copy-done), kind=kOutput, calls=%fused_computation.71 | convolution fusion | flops 805306368 | bytes 4194304 | tf_op jit(solution)/shard_map/rnk,kc->rnc/dot_general | solution.py:86
  136.2 1.2 reshape_reshape.3
  137.4 2.5 %convert_reduce_fusion = (f32[4,512]{1,0:T(4,128)S(1)}, bf16[4,512,512]{1,2,0:T(8,128)(2,1)S(1)}) fusion(f32[512,512]{0,1:T(8,128)S(1)} %copy-done.2, f32[4]{0:T(128)S(1)} %copy-done.14, bf16[512,4,3,64]{0,3,2,1:T(8,128)(2,1)} %reshape_reshape.3, pred[512]{0:T(512)(128)(4,1)S(1)} %copy-done.11), kind=kOutput, calls=%fused_computation.48 | convolution fusion | flops 141555712 | bytes 3678736 | tf_op jit(solution)/shard_map/qhd,khd->hqk/dot_general | solution.py:144
  139.9 1.4 fusion.17
  142.2 3.4 %all-to-all-start = ((bf16[4,128,256]{1,2,0:T(8,128)(2,1)}), bf16[4,128,256]{1,2,0:T(8,128)(2,1)S(1)}, u32[]{:S(2)}, u32[]{:S(2)}) async-start(bf16[4,128,256]{1,2,0:T(8,128)(2,1)} %copy.47), calls=%async_computation | async-start | bytes 524288 | tf_op jit(solution)/shard_map/all_to_all | solution.py:154
  146.3 8.4 %all-to-all-done = bf16[4,128,256]{1,2,0:T(8,128)(2,1)S(1)} async-done(((bf16[4,128,256]{1,2,0:T(8,128)(2,1)}), bf16[4,128,256]{1,2,0:T(8,128)(2,1)S(1)}, u32[]{:S(2)}, u32[]{:S(2)}) %all-to-all-start) | async-done | bytes 262176 | tf_op jit(solution)/shard_map/all_to_all | solution.py:154
  154.6 0.8 copy.48
  (87 shorter events, 11.5 us)
Async XLA Ops:
  7.2 113.0 %copy-start = (bf16[1024,768]{1,0:T(8,128)(2,1)S(1)}, bf16[1024,768]{1,0:T(8,128)(2,1)}, u32[]{:S(2)}) copy-start(bf16[1024,768]{1,0:T(8,128)(2,1)} %param.34) | copy-start | bytes 4718596
  7.2 6.9 %copy-start.1 = (bf16[1,3,49,1536]{3,2,1,0:T(8,128)(2,1)S(1)}, bf16[1,3,49,1536]{3,2,1,0:T(8,128)(2,1)}, u32[]{:S(2)}) copy-start(bf16[1,3,49,1536]{3,2,1,0:T(8,128)(2,1)} %param.19) | copy-start | bytes 1354756
  7.2 8.0 %copy-start.6 = (f32[1536]{0:T(1024)S(1)}, f32[1536]{0:T(1024)}, u32[]{:S(2)}) copy-start(f32[1536]{0:T(1024)} %param.21) | copy-start | bytes 18436
  7.2 56.5 %all-gather.6.cloned.1.call-start = ((), (), s32[]{:S(2)}) async-start(), calls=%async_computation.1 | async-start | bytes 1966080 | tf_op jit(solution)/shard_map/all_gather | solution.py:79
  9.2 90.3 %all-gather.10.cloned.1.call-start = ((), (), s32[]{:S(2)}) async-start(), calls=%async_computation.3 | async-start | bytes 4718592 | tf_op jit(solution)/shard_map/all_gather | solution.py:80
  63.5 0.7 copy-start.12
  63.8 29.1 %copy-start.9 = (s32[1,2,512]{2,1,0:T(2,128)S(1)}, s32[1,2,512]{2,1,0:T(2,128)}, u32[]{:S(2)}) copy-start(s32[1,2,512]{2,1,0:T(2,128)} %param.36) | copy-start | bytes 12292
  63.8 68.4 %all-gather.8.cloned.1.call-start = ((), (), s32[]{:S(2)}) async-start(), calls=%async_computation.2 | async-start | bytes 1310720 | tf_op jit(solution)/shard_map/all_gather | solution.py:84
  74.7 20.1 %copy-start.10 = (u32[32]{0:T(128)S(1)}, u32[32]{0:T(128)}, u32[]{:S(2)}) copy-start(u32[32]{0:T(128)} %constant.122) | copy-start | bytes 388
  74.7 21.3 %copy-start.13 = (f32[16]{0:T(128)S(1)}, f32[16]{0:T(128)}, u32[]{:S(2)}) copy-start(f32[16]{0:T(128)} %param.35) | copy-start | bytes 196
  89.7 6.9 %collective-permute-start = (bf16[5,1536]{1,0:T(8,128)(2,1)S(1)}, bf16[5,1536]{1,0:T(8,128)(2,1)S(1)}, u32[]{:S(2)}, u32[]{:S(2)}) collective-permute-start(bf16[5,1536]{1,0:T(8,128)(2,1)S(1)} %slice.439), channel_id=1, source_target_pairs={{0,2},{1,3},{4,6},{5,7},{8,10},{9,11},{12,14},{13,15},{16,18},{17,... | collective-permute-start | bytes 46088
  97.1 0.7 copy-start.7
  97.2 0.7 copy-start.8
  99.5 3.4 %copy-start.5 = (f32[1024]{0:T(1024)S(1)}, f32[1024]{0:T(1024)}, u32[]{:S(2)}) copy-start(f32[1024]{0:T(1024)} %param.33) | copy-start | bytes 12292
  102.5 1.3 copy-start.3
  102.5 1.3 copy-start.4
  135.6 1.8 %copy-start.2 = (f32[512,512]{0,1:T(8,128)S(1)}, f32[512,512]{0,1:T(8,128)}, u32[]{:S(2)}) copy-start(f32[512,512]{0,1:T(8,128)} %abs_add_fusion) | copy-start | bytes 3145732
  135.6 1.8 %copy-start.11 = (pred[512]{0:T(512)(128)(4,1)S(1)}, pred[512]{0:T(512)(128)(4,1)}, u32[]{:S(2)}) copy-start(pred[512]{0:T(512)(128)(4,1)} %iota_compare_fusion) | copy-start | bytes 1540
  135.6 1.8 %copy-start.14 = (f32[4]{0:T(128)S(1)}, f32[4]{0:T(128)}, u32[]{:S(2)}) copy-start(f32[4]{0:T(128)} %dynamic_slice.7) | copy-start | bytes 52
  142.2 12.5 %all-to-all-start = ((bf16[4,128,256]{1,2,0:T(8,128)(2,1)}), bf16[4,128,256]{1,2,0:T(8,128)(2,1)S(1)}, u32[]{:S(2)}, u32[]{:S(2)}) async-start(bf16[4,128,256]{1,2,0:T(8,128)(2,1)} %copy.47), calls=%async_computation | async-start | bytes 524288 | tf_op jit(solution)/shard_map/all_to_all | solution.py:154
Sparse Core Ops, SparseCore 0:
  9.6 39.7 all-gather.5
  63.9 13.6 all-gather.9
  103.9 28.2 all-gather.7

commit v2 on v1

--- a/solution.py
+++ b/solution.py
@@ -3,11 +3,14 @@
 import jax
 import jax.numpy as jnp
 from jax import lax
+from jax.experimental import pallas as pl
+from jax.experimental.pallas import tpu as pltpu
 from jax.sharding import PartitionSpec as P
 
 SIDE = 7
 KER = 7
 HDIM = 64
+LANES = 128
 
 
 def layer_norm(inputs, gain, shift, epsilon):
@@ -17,21 +20,56 @@
     return centered * lax.rsqrt(spread + epsilon) * gain + shift
 
 
-def depthwise(tile_data, depth_weight, depth_bias):
-    tile_count = tile_data.shape[0]
-    channels = tile_data.shape[-1]
-    spatial = tile_data.reshape(tile_count, SIDE, SIDE, channels)
-    margin = KER // 2
-    padded = jnp.pad(spatial, ((0, 0), (margin, margin), (margin, margin), (0, 0)))
-    running = jnp.zeros_like(spatial) + depth_bias
-    for tap_row in range(KER):
-        for tap_col in range(KER):
-            running = (
-                running
-                + padded[:, tap_row : tap_row + SIDE, tap_col : tap_col + SIDE, :]
-                * depth_weight[tap_row * KER + tap_col]
-            )
-    return running.reshape(tile_count, SIDE * SIDE, channels)
+def dw_ln_kernel(x_ref, w_ref, b_ref, g_ref, nb_ref, o_ref, conv_ref):
+    C = x_ref.shape[-1]
+    jrow = lax.broadcasted_iota(jnp.int32, (8, LANES), 0)
+    masks = [((jrow + (bb - 3)) >= 0) & ((jrow + (bb - 3)) < SIDE) for bb in range(KER)]
+    def chunk(ci, carry):
+        c0 = pl.multiple_of(ci * LANES, LANES)
+        rows = [x_ref[0, i, :, pl.ds(c0, LANES)].astype(jnp.float32) for i in range(SIDE)]
+        bias = jnp.broadcast_to(b_ref[:, pl.ds(c0, LANES)], (8, LANES))
+        acc = [bias for _ in range(SIDE)]
+        for ip in range(SIDE):
+            for bb in range(KER):
+                s = bb - 3
+                sh = rows[ip] if s == 0 else pltpu.roll(rows[ip], shift=(-s) % 8, axis=0)
+                sh = jnp.where(masks[bb], sh, 0.0)
+                for a in range(KER):
+                    i = ip - (a - 3)
+                    if 0 <= i < SIDE:
+                        wv = jnp.broadcast_to(w_ref[pl.ds(a * KER + bb, 1), pl.ds(c0, LANES)], (8, LANES))
+                        acc[i] = acc[i] + sh * wv
+        for i in range(SIDE):
+            conv_ref[i, :, pl.ds(c0, LANES)] = acc[i]
+        return carry
+    lax.fori_loop(0, C // LANES, chunk, 0)
+    g = g_ref[...]
+    nb = nb_ref[...]
+    for i in range(SIDE):
+        v = conv_ref[i]
+        mean = jnp.mean(v, axis=-1, keepdims=True)
+        cen = v - mean
+        var = jnp.mean(cen * cen, axis=-1, keepdims=True)
+        o_ref[0, i] = (cen * lax.rsqrt(var + 1e-06) * g + nb).astype(o_ref.dtype)
+
+def dw_ln(tiles, depth_weight, depth_bias, norm_gain, norm_bias):
+    T, _, C = tiles.shape
+    x = jnp.pad(tiles.reshape(T, SIDE, SIDE, C), ((0, 0), (0, 0), (0, 1), (0, 0)))
+    out = pl.pallas_call(
+        dw_ln_kernel,
+        grid=(T,),
+        in_specs=[
+            pl.BlockSpec((1, SIDE, 8, C), lambda t: (t, 0, 0, 0)),
+            pl.BlockSpec((KER * KER, C), lambda t: (0, 0)),
+            pl.BlockSpec((1, C), lambda t: (0, 0)),
+            pl.BlockSpec((1, C), lambda t: (0, 0)),
+            pl.BlockSpec((1, C), lambda t: (0, 0)),
+        ],
+        out_specs=pl.BlockSpec((1, SIDE, 8, C), lambda t: (t, 0, 0, 0)),
+        out_shape=jax.ShapeDtypeStruct((T, SIDE, 8, C), jnp.bfloat16),
+        scratch_shapes=[pltpu.VMEM((SIDE, 8, C), jnp.float32)],
+    )(x, depth_weight, depth_bias[None], norm_gain[None], norm_bias[None])
+    return out[:, :, :SIDE].reshape(T * SIDE * SIDE, C)
 
 
 def normalize_heads(values):
@@ -87,13 +125,7 @@
     )
 
     tile_data = tile_features[0].astype(jnp.float32)
-    channels = tile_data.shape[-1]
-    convolved = depthwise(tile_data, depth_weight, depth_bias)
-    normed = (
-        layer_norm(convolved, norm_gain, norm_bias, 1e-06)
-        .astype(jnp.bfloat16)
-        .reshape(-1, channels)
-    )
+    normed = dw_ln(tile_features[0], depth_weight, depth_bias, norm_gain, norm_bias)
     hidden = jax.nn.gelu(
         jnp.dot(
             lax.all_gather(normed, "rep", axis=0, tiled=True),

time: 163 us -> 147 us (0.902)
  other arithmetic: 40.4 us -> 6.69 us
  waiting for transfers between devices: 19.2 us -> 32.3 us
  Pallas kernels: 0 us -> 5.74 us
    reduce_sum x2 -> x1, other arithmetic: 31.9 us -> 0.13 us  [layer_norm(): center = jnp.mean(inputs, axis=-1, keepdims=True)]
    all_gather x1, waiting for transfers between devices: 0.02 us -> 14.9 us  [on_device(): cols_full = lax.all_gather(my_cols, 'slide', axis=0, tiled=True)]
    pallas_call x0 -> x1, Pallas kernels: none -> 5.74 us  [dw_ln(): pl.pallas_call(dw_ln_kernel, grid=(T,), in_specs=[pl.BlockSpec((1, SIDE,...]
    slice x3 -> x0, local copies, waits for them, and re-layouts: 4.82 us -> none  [depthwise(): depth_weight[tap_row * KER + tap_col]]
    broadcast_in_dim x0 -> x3, local copies, waits for them, and re-layouts: none -> 1.79 us  [the longest x1 0.6 us: dw_ln(): depth_bias[None]]
    all_gather x1, waiting for transfers between devices: 10.7 us -> 8.95 us  [on_device(): stale_all = lax.all_gather(stale_normed, 'slide', axis=0, tiled=False)]
    unnamed x35 -> x38, local copies, waits for them, and re-layouts: 2.91 us -> 3.92 us
  transfers between devices with their start and end apart: 5 -> 5, of which waited for: 2 -> 3; matrix products, arithmetic and copies ran while one was open for 47% -> 28% of each run, Pallas kernels for 0% -> 4%
where the time goes in v2:
time: 147 us; the launch traced here: 146 us
  blocking collectives  43.2 us (29%)
  waiting for transfers between devices  32.3 us (22%)
  matrix products  22.4 us (15%)
  between operations  15.5 us (11%)
  local copies, waits for them, and re-layouts  14 us (10%)
  other arithmetic  6.69 us (5%)
  starting transfers between devices  5.96 us (4%)
  Pallas kernels  5.74 us (4%)
    unnamed x1, blocking collectives  15.5 us
    all_gather x1, waiting for transfers between devices, on_device(): cols_full = lax.all_gather(my_cols, 'slide', axis=0, tiled=True)  14.9 us
    all_gather x1, blocking collectives, on_device(): lax.all_gather(normed, 'rep', axis=0, tiled=True)  14.3 us
    all_gather x1, blocking collectives, on_device(): fresh_all = lax.all_gather(fresh_normed, 'slide', axis=0, tiled=False)  13.5 us
    dot_general x1, matrix products, on_device(): jnp.dot(hidden, down_weight, preferred_element_type=jnp.float32)  10.4 us
    all_gather x1, waiting for transfers between devices, on_device(): stale_all = lax.all_gather(stale_normed, 'slide', axis=0, tiled=False)  8.95 us
    all_to_all x1, waiting for transfers between devices, on_device(): lax.all_to_all(attended, 'slide', split_axis=0, concat_axis=1, tiled=True)  8.38 us
    pallas_call x1, Pallas kernels, dw_ln(): pl.pallas_call(dw_ln_kernel, grid=(T,), in_specs=[pl.BlockSpec((1, SIDE,...  5.74 us
  transfers between devices with their start and end apart: 5, of which 3 were waited for; matrix products, arithmetic and copies ran while one was open for 28% of the time, Pallas kernels for 4%

profile of v2, /device:TPU:0, one launch (start us, length us, event | category | flops | bytes accessed | tf_op | source)
XLA Modules:
  0.0 145.9 jit_solution(11029608558059528252)
XLA Ops:
  7.3 1.9 %constant_dynamic-slice_fusion = bf16[384,512]{1,0:T(8,128)(2,1)} fusion(bf16[384,1024]{1,0:T(8,128)(2,1)} %param.32, s32[]{:T(128)S(6)} %select_n.22), kind=kLoop, calls=%fused_computation.112 | loop fusion | bytes 786436 | tf_op jit(solution)/shard_map/dynamic_slice | solution.py:114
  9.2 1.2 reshape_squeeze.3
  12.2 0.9 pad.4.x_ref
  13.1 5.7 %shard_map.194 = bf16[3,7,8,1536]{3,2,1,0:T(8,128)(2,1)} custom-call(bf16[3,7,8,1536]{3,2,1,0:T(8,128)(2,1)} %pad.4.x_ref, f32[49,1536]{1,0:T(8,128)} %w_ref.1, f32[1,1536]{1,0:T(1,128)} %broadcast_in_dim.36.b_ref, f32[1,1536]{1,0:T(1,128)} %broadcast_in_dim.37.g_ref, f32[1,1536]{1,0:T(1,128)} %broadcast_in_dim.42.nb_ref), custom_call_target="tpu_custom_call" | custom-call | tf_op jit(solution)/shard_map/pallas_call | solution.py:58
  18.8 1.2 reshape.470
  20.1 14.3 %all-gather.1 = bf16[2,147,1536]{2,1,0:T(8,128)(2,1)S(1)} all-gather(bf16[1,147,1536]{2,1,0:T(8,128)(2,1)S(1)} %reshape.470), channel_id=1, replica_groups=mesh['groups'=2,'slide'=4,'rep'=2,'section'=2] {'rep'}, dimensions={0}, use_global_device_ids=true | all-gather | bytes 1354752 | tf_op jit(solution)/shard_map/all_gather | solution.py:131
  34.5 14.9 %all-gather.6.cloned.1.call-done = bf16[1536,512]{1,0:T(8,128)(2,1)} async-done(((bf16[384,512]{1,0:T(8,128)(2,1)}), bf16[1536,512]{1,0:T(8,128)(2,1)}) %all-gather.6.cloned.1.call-update) | async-done | bytes 1572880 | tf_op jit(solution)/shard_map/all_gather | solution.py:117
  49.5 10.4 %convolution_convert_fusion = bf16[294,1536]{1,0:T(8,128)(2,1)S(1)} fusion(bf16[1536,1536]{1,0:T(8,128)(2,1)} %param.26, bf16[294,1536]{1,0:T(8,128)(2,1)S(1)} %reshape.471, bf16[1536,1536]{1,0:T(8,128)(2,1)} %param.24, f32[1536]{0:T(1024)S(1)} %copy-done.13), kind=kOutput, calls=%fused_computation.4 | convolution fusion | flops 2804788224 | bytes 11249664 | tf_op jit(solution)/shard_map/dot_general | solution.py:139
  60.0 15.5 %fusion = bf16[152,1536]{1,0:T(8,128)(2,1)S(1)} fusion(bf16[294,1536]{1,0:T(8,128)(2,1)S(1)} %convolution_convert_fusion), kind=kCustom, calls=%all-reduce-scatter | all-reduce-scatter fusion | flops 466945 | bytes 1370624
  75.5 2.4 %collective-permute-start = (bf16[5,1536]{1,0:T(8,128)(2,1)S(1)}, bf16[5,1536]{1,0:T(8,128)(2,1)S(1)}, u32[]{:S(2)}, u32[]{:S(2)}) collective-permute-start(bf16[5,1536]{1,0:T(8,128)(2,1)S(1)} %slice.55), channel_id=1, source_target_pairs={{0,2},{1,3},{4,6},{5,7},{8,10},{9,11},{12,14},{13,15},{16,18},{17,... | collective-permute-start | bytes 46088
  78.6 1.3 abs_add_fusion
  83.6 1.3 fusion.18
  85.2 3.0 %fusion.96 = (f32[128]{0:T(128)S(1)}, f32[2,512,128]{2,1,0:T(8,128)S(1)}) fusion(bf16[2,1536,512]{2,1,0:T(8,128)(2,1)} %bitcast.95, bf16[1,128,1536]{2,1,0:T(8,128)(2,1)} %param.31), kind=kOutput, calls=%fused_computation.145 | convolution fusion | flops 402784128 | bytes 4063744 | tf_op jit(solution)/shard_map/nk,skc->nsc/dot_general | solution.py:85
  88.6 0.8 multiply_convert_fusion.1
  89.5 2.6 %fusion.97 = (f32[3]{0:T(128)S(1)}, f32[3,2,512]{2,0,1:T(4,128)S(1)}) fusion(bf16[2,1536,512]{2,1,0:T(8,128)(2,1)} %bitcast.96, f32[1536]{0:T(1024)S(1)} %copy-done.2, f32[3,1536]{1,0:T(4,128)S(1)} %fusion.18, f32[1536]{0:T(1024)S(1)} %copy-done.3, f32[3]{0:T(128)S(1)} %add_rsqrt_fusion.4, f32[3]{0:T(128)S(1)} %broadcast_multiply_fusion.2), kind=kOutput, calls=%fused_computation.146 | convolution fusion | flops 9467901 | bytes 3188772 | tf_op jit(solution)/shard_map/nk,skc->nsc/dot_general | solution.py:85
  92.4 13.5 %all_gather.24 = bf16[4,3,1024]{2,1,0:T(4,128)(2,1)S(1)} all-gather(bf16[1,3,1024]{2,1,0:T(4,128)(2,1)S(1)} %multiply_convert_fusion.3), channel_id=1, replica_groups=mesh['groups'=2,'slide'=4,'rep'=2,'section'=2] {'slide'}, dimensions={0}, use_global_device_ids=true | all-gather | bytes 30720 | tf_op jit(solution)/shard_map/all_gather | solution.py:149
  107.1 8.9 %all-gather.8.cloned.1.call-done = bf16[4,128,1024]{2,1,0:T(8,128)(2,1)} async-done(((bf16[1,128,1024]{2,1,0:T(8,128)(2,1)}), bf16[4,128,1024]{2,1,0:T(8,128)(2,1)}) %all-gather.8.cloned.1.call-update) | async-done | bytes 1048592 | tf_op jit(solution)/shard_map/all_gather | solution.py:122
  116.1 2.2 %fusion.11 = f32[4,128,768]{1,2,0:T(8,128)S(1)} fusion(bf16[4,128,1024]{2,1,0:T(8,128)(2,1)} %all-gather.8.cloned.1.call-done, bf16[1024,768]{1,0:T(8,128)(2,1)S(1)} %copy-done), kind=kOutput, calls=%fused_computation.23 | convolution fusion | flops 805306368 | bytes 4194304 | tf_op jit(solution)/shard_map/rnk,kc->rnc/dot_general | solution.py:124
  120.1 1.2 reshape_reshape.3
  121.3 2.5 %convert_reduce_fusion = (f32[4,512]{1,0:T(4,128)S(1)}, bf16[4,512,512]{1,2,0:T(8,128)(2,1)S(1)}) fusion(f32[512,512]{0,1:T(8,128)S(1)} %copy-done.1, f32[4]{0:T(128)S(1)} %copy-done.15, bf16[512,4,3,64]{0,3,2,1:T(8,128)(2,1)} %reshape_reshape.3, pred[512]{0:T(512)(128)(4,1)S(1)} %copy-done.11), kind=kOutput, calls=%fused_computation | convolution fusion | flops 141555712 | bytes 3678736 | tf_op jit(solution)/shard_map/qhd,khd->hqk/dot_general | solution.py:176
  123.8 1.4 fusion.17
  126.1 3.4 %all-to-all-start = ((bf16[4,128,256]{1,2,0:T(8,128)(2,1)}), bf16[4,128,256]{1,2,0:T(8,128)(2,1)S(1)}, u32[]{:S(2)}, u32[]{:S(2)}) async-start(bf16[4,128,256]{1,2,0:T(8,128)(2,1)} %copy.47), calls=%async_computation | async-start | bytes 524288 | tf_op jit(solution)/shard_map/all_to_all | solution.py:186
  130.2 8.4 %all-to-all-done = bf16[4,128,256]{1,2,0:T(8,128)(2,1)S(1)} async-done(((bf16[4,128,256]{1,2,0:T(8,128)(2,1)}), bf16[4,128,256]{1,2,0:T(8,128)(2,1)S(1)}, u32[]{:S(2)}, u32[]{:S(2)}) %all-to-all-start) | async-done | bytes 262176 | tf_op jit(solution)/shard_map/all_to_all | solution.py:186
  138.5 0.8 copy.48
  (84 shorter events, 10.7 us)
Async XLA Ops:
  7.2 98.7 %copy-start = (bf16[1024,768]{1,0:T(8,128)(2,1)S(1)}, bf16[1024,768]{1,0:T(8,128)(2,1)}, u32[]{:S(2)}) copy-start(bf16[1024,768]{1,0:T(8,128)(2,1)} %param.34) | copy-start | bytes 4718596
  7.2 3.2 %copy-start.7 = (f32[1536]{0:T(1024)S(1)}, f32[1536]{0:T(1024)}, u32[]{:S(2)}) copy-start(f32[1536]{0:T(1024)} %param.21) | copy-start | bytes 18436
  7.2 3.8 %copy-start.8 = (f32[1536]{0:T(1024)S(1)}, f32[1536]{0:T(1024)}, u32[]{:S(2)}) copy-start(f32[1536]{0:T(1024)} %param.22) | copy-start | bytes 18436
  7.2 4.4 %copy-start.9 = (f32[1536]{0:T(1024)S(1)}, f32[1536]{0:T(1024)}, u32[]{:S(2)}) copy-start(f32[1536]{0:T(1024)} %param.23) | copy-start | bytes 18436
  7.2 42.2 %all-gather.6.cloned.1.call-start = ((), (), s32[]{:S(2)}) async-start(), calls=%async_computation.1 | async-start | bytes 1966080 | tf_op jit(solution)/shard_map/all_gather | solution.py:117
  9.2 76.0 %all-gather.10.cloned.1.call-start = ((), (), s32[]{:S(2)}) async-start(), calls=%async_computation.3 | async-start | bytes 4718592 | tf_op jit(solution)/shard_map/all_gather | solution.py:118
  34.4 15.2 %copy-start.13 = (f32[1536]{0:T(1024)S(1)}, f32[1536]{0:T(1024)}, u32[]{:S(2)}) copy-start(f32[1536]{0:T(1024)} %param.25) | copy-start | bytes 18436
  49.5 29.1 %copy-start.10 = (s32[1,2,512]{2,1,0:T(2,128)S(1)}, s32[1,2,512]{2,1,0:T(2,128)}, u32[]{:S(2)}) copy-start(s32[1,2,512]{2,1,0:T(2,128)} %param.36) | copy-start | bytes 12292
  49.5 66.6 %all-gather.8.cloned.1.call-start = ((), (), s32[]{:S(2)}) async-start(), calls=%async_computation.2 | async-start | bytes 1310720 | tf_op jit(solution)/shard_map/all_gather | solution.py:122
  60.0 20.5 %copy-start.12 = (u32[32]{0:T(128)S(1)}, u32[32]{0:T(128)}, u32[]{:S(2)}) copy-start(u32[32]{0:T(128)} %constant.119) | copy-start | bytes 388
  60.0 21.7 %copy-start.14 = (f32[16]{0:T(128)S(1)}, f32[16]{0:T(128)}, u32[]{:S(2)}) copy-start(f32[16]{0:T(128)} %param.35) | copy-start | bytes 196
  75.5 6.8 %collective-permute-start = (bf16[5,1536]{1,0:T(8,128)(2,1)S(1)}, bf16[5,1536]{1,0:T(8,128)(2,1)S(1)}, u32[]{:S(2)}, u32[]{:S(2)}) collective-permute-start(bf16[5,1536]{1,0:T(8,128)(2,1)S(1)} %slice.55), channel_id=1, source_target_pairs={{0,2},{1,3},{4,6},{5,7},{8,10},{9,11},{12,14},{13,15},{16,18},{17,... | collective-permute-start | bytes 46088
  82.9 0.7 copy-start.5
  82.9 0.7 copy-start.6
  85.2 3.4 %copy-start.4 = (f32[1024]{0:T(1024)S(1)}, f32[1024]{0:T(1024)}, u32[]{:S(2)}) copy-start(f32[1024]{0:T(1024)} %param.33) | copy-start | bytes 12292
  88.2 1.3 copy-start.2
  88.2 1.3 copy-start.3
  119.5 1.8 %copy-start.1 = (f32[512,512]{0,1:T(8,128)S(1)}, f32[512,512]{0,1:T(8,128)}, u32[]{:S(2)}) copy-start(f32[512,512]{0,1:T(8,128)} %abs_add_fusion) | copy-start | bytes 3145732
  119.5 1.8 %copy-start.11 = (pred[512]{0:T(512)(128)(4,1)S(1)}, pred[512]{0:T(512)(128)(4,1)}, u32[]{:S(2)}) copy-start(pred[512]{0:T(512)(128)(4,1)} %iota_compare_fusion) | copy-start | bytes 1540
  119.5 1.8 %copy-start.15 = (f32[4]{0:T(128)S(1)}, f32[4]{0:T(128)}, u32[]{:S(2)}) copy-start(f32[4]{0:T(128)} %dynamic_slice.7) | copy-start | bytes 52
  126.1 12.5 %all-to-all-start = ((bf16[4,128,256]{1,2,0:T(8,128)(2,1)}), bf16[4,128,256]{1,2,0:T(8,128)(2,1)S(1)}, u32[]{:S(2)}, u32[]{:S(2)}) async-start(bf16[4,128,256]{1,2,0:T(8,128)(2,1)} %copy.47), calls=%async_computation | async-start | bytes 524288 | tf_op jit(solution)/shard_map/all_to_all | solution.py:186
Sparse Core Ops, SparseCore 0:
  9.6 39.7 all-gather.5
  51.0 11.0 all-gather.9
  89.6 26.4 all-gather.7

commit v3 on v2

--- a/solution.py
+++ b/solution.py
@@ -125,31 +125,48 @@
     )
 
     tile_data = tile_features[0].astype(jnp.float32)
+    fresh_count = tile_data.shape[0]
+    n_rep = lax.axis_size("rep")
+    my_rep = lax.axis_index("rep")
+    n_slide = lax.axis_size("slide")
+    my_slide = lax.axis_index("slide")
     normed = dw_ln(tile_features[0], depth_weight, depth_bias, norm_gain, norm_bias)
-    hidden = jax.nn.gelu(
-        jnp.dot(
-            lax.all_gather(normed, "rep", axis=0, tiled=True),
-            up_weight,
-            preferred_element_type=jnp.float32,
+
+    def block_sums(rows):
+        hidden = jax.nn.gelu(
+            jnp.dot(rows, up_weight, preferred_element_type=jnp.float32) + up_bias,
+            approximate=False,
+        ).astype(jnp.bfloat16)
+        part = jnp.dot(hidden, down_weight, preferred_element_type=jnp.float32).astype(
+            jnp.bfloat16
         )
-        + up_bias,
-        approximate=False,
-    ).astype(jnp.bfloat16)
-    summed = lax.psum_scatter(
-        jnp.dot(hidden, down_weight, preferred_element_type=jnp.float32).astype(jnp.bfloat16),
-        "rep",
-        scatter_dimension=0,
-        tiled=True,
-    ).astype(jnp.float32)
-    updated = tile_data + layer_scale * (summed.reshape(tile_data.shape) + down_bias)
-    pooled = jnp.mean(updated, axis=1)
-    embedded = layer_norm(pooled, head_gain, head_bias, 1e-06).astype(jnp.bfloat16)
-
-    fresh_normed = project(embedded, weight_parts, slide_gain)
-    fresh_all = lax.all_gather(fresh_normed, "slide", axis=0, tiled=False)
+        return jnp.sum(part.astype(jnp.float32).reshape(tile_data.shape), axis=1)
+
+    received = [
+        lax.ppermute(normed, "rep", perm=[(r, (r + k) % n_rep) for r in range(n_rep)])
+        for k in range(1, n_rep)
+    ]
+    positions = tile_data.shape[1]
+    own_term = jnp.mean(tile_data, axis=1) + layer_scale * (
+        block_sums(normed) / positions + down_bias
+    )
+    slots = jnp.zeros((n_rep, n_slide) + own_term.shape, jnp.float32)
+    slots = lax.dynamic_update_slice(slots, own_term[None, None], (my_rep, my_slide, 0, 0))
+    for k, rows in enumerate(received, start=1):
+        term = layer_scale * (block_sums(rows) / positions)
+        slots = lax.dynamic_update_slice(
+            slots, term[None, None], ((my_rep - k) % n_rep, my_slide, 0, 0)
+        )
+    pooled_all = lax.psum(slots, ("slide", "rep"))
+    pooled = lax.dynamic_index_in_dim(pooled_all, my_rep, 0, keepdims=False)
+    pooled = pooled.reshape(n_slide * fresh_count, -1)
+    embedded_all = layer_norm(pooled, head_gain, head_bias, 1e-06).astype(jnp.bfloat16)
+    embedded = lax.dynamic_slice_in_dim(embedded_all, my_slide * fresh_count, fresh_count, 0)
+
+    fresh_normed = project(embedded_all, weight_parts, slide_gain)
     fresh_mixed = normalize_heads(
-        jnp.einsum("rnk,kc->rnc", fresh_all, qkv_weight, preferred_element_type=jnp.float32)
-    )
+        jnp.dot(fresh_normed, qkv_weight, preferred_element_type=jnp.float32)
+    ).reshape(n_slide, fresh_count, -1)
     local_heads = jnp.concatenate([fresh_mixed, stale_mixed[:, fresh_count:]], axis=1)
     n_slide = local_heads.shape[0]
     seq_len = n_slide * local_heads.shape[1]

time: 147 us -> 191 us (1.30)
  waiting for transfers between devices: 32.3 us -> 105 us
  blocking collectives: 43.2 us -> 0 us
  local copies, waits for them, and re-layouts: 14 us -> 20.5 us
  matrix products: 22.4 us -> 27.3 us
  other arithmetic: 6.69 us -> 8.67 us
    psum x0 -> x1, waiting for transfers between devices: none -> 54.3 us  [on_device(): pooled_all = lax.psum(slots, ('slide', 'rep'))]
    all_gather x2 -> x0, blocking collectives: 27.8 us -> none  [the longest x1 14.3 us: on_device(): lax.all_gather(normed, 'rep', axis=0, tiled=True)]
    unnamed x1 -> x0, blocking collectives: 15.5 us -> none
    all_gather x1, waiting for transfers between devices: 8.95 us -> 22.4 us  [on_device(): stale_all = lax.all_gather(stale_normed, 'slide', axis=0, tiled=False)]
    all_gather x1, waiting for transfers between devices: 14.9 us -> 19.8 us  [on_device(): cols_full = lax.all_gather(my_cols, 'slide', axis=0, tiled=True)]
    dot_general x0 -> x1, local copies, waits for them, and re-layouts: none -> 4.74 us  [project(): jnp.einsum('nk,skc->nsc', rows, weight_parts, preferred_element_type=jnp....]
    dot_general x2 -> x3, matrix products: 10.7 us -> 15.2 us  [the longest x2 14.9 us: block_sums(): jnp.dot(hidden, down_weight, preferred_element_type=jnp.float32)]
    ppermute x0 -> x1, starting transfers between devices: none -> 2.94 us  [on_device(): lax.ppermute(normed, 'rep', perm=[(r, (r + k) % n_rep) for r in range(n_r...]
  transfers between devices with their start and end apart: 5 -> 6, of which waited for: 3 -> 5; matrix products, arithmetic and copies ran while one was open for 28% -> 15% of each run, Pallas kernels for 4% -> 0%
where the time goes in v3:
time: 191 us; the launch traced here: 190 us
  waiting for transfers between devices  105 us (55%)
  matrix products  27.3 us (14%)
  local copies, waits for them, and re-layouts  20.5 us (11%)
  between operations  16.2 us (8%)
  other arithmetic  8.67 us (5%)
  starting transfers between devices  6.69 us (4%)
  Pallas kernels  5.73 us (3%)
    psum x1, waiting for transfers between devices, on_device(): pooled_all = lax.psum(slots, ('slide', 'rep'))  54.3 us
    all_gather x1, waiting for transfers between devices, on_device(): stale_all = lax.all_gather(stale_normed, 'slide', axis=0, tiled=False)  22.4 us
    all_gather x1, waiting for transfers between devices, on_device(): cols_full = lax.all_gather(my_cols, 'slide', axis=0, tiled=True)  19.8 us
    dot_general x2, matrix products, block_sums(): jnp.dot(hidden, down_weight, preferred_element_type=jnp.float32)  14.9 us
    all_to_all x1, waiting for transfers between devices, on_device(): lax.all_to_all(attended, 'slide', split_axis=0, concat_axis=1, tiled=True)  8.34 us
    dot_general x2, matrix products, project(): jnp.einsum('nk,skc->nsc', rows, weight_parts, preferred_element_type=jnp....  5.86 us
    pallas_call x1, Pallas kernels, dw_ln(): pl.pallas_call(dw_ln_kernel, grid=(T,), in_specs=[pl.BlockSpec((1, SIDE,...  5.73 us
    dot_general x1, local copies, waits for them, and re-layouts, project(): jnp.einsum('nk,skc->nsc', rows, weight_parts, preferred_element_type=jnp....  4.74 us
  transfers between devices with their start and end apart: 6, of which 5 were waited for; matrix products, arithmetic and copies ran while one was open for 15% of the time, Pallas kernels for 0%

profile of v3, /device:TPU:0, one launch (start us, length us, event | category | flops | bytes accessed | tf_op | source)
XLA Modules:
  0.0 190.1 jit_solution(6769663029132704399)
XLA Ops:
  8.1 1.3 reshape_squeeze.3
  9.4 1.3 broadcast_in_dim.41.b_ref
  10.7 1.3 broadcast_in_dim.42.g_ref
  12.0 1.3 broadcast_in_dim.47.nb_ref
  13.3 0.9 pad.4.x_ref
  14.2 5.7 %shard_map.194 = bf16[3,7,8,1536]{3,2,1,0:T(8,128)(2,1)} custom-call(bf16[3,7,8,1536]{3,2,1,0:T(8,128)(2,1)} %pad.4.x_ref, f32[49,1536]{1,0:T(8,128)} %w_ref.1, f32[1,1536]{1,0:T(1,128)} %broadcast_in_dim.41.b_ref, f32[1,1536]{1,0:T(1,128)} %broadcast_in_dim.42.g_ref, f32[1,1536]{1,0:T(1,128)} %broadcast_in_dim.47.nb_ref), custom_call_target="tpu_custom_call" | custom-call | tf_op jit(solution)/shard_map/pallas_call | solution.py:58
  19.9 2.0 %reshape.420 = bf16[147,1536]{1,0:T(8,128)(2,1)} reshape(bf16[3,7,7,1536]{3,2,1,0:T(8,128)(2,1)} %bitcast.100) | data formatting | bytes 903168 | tf_op jit(solution)/shard_map/reshape | solution.py:72
  21.9 2.9 %collective-permute-start = (bf16[147,1536]{1,0:T(8,128)(2,1)}, bf16[147,1536]{1,0:T(8,128)(2,1)}, u32[]{:S(2)}, u32[]{:S(2)}) collective-permute-start(bf16[147,1536]{1,0:T(8,128)(2,1)} %reshape.420), channel_id=1, source_target_pairs={{0,2},{2,0},{1,3},{3,1},{4,6},{6,4},{5,7},{7,5},{8,10},{10,8},{9,1... | collective-permute-start | bytes 1354760 | tf_op jit(solution)/shard_map/ppermute | solution.py:146
  25.8 7.4 %fusion.1 = f32[147,1536]{1,0:T(8,128)S(1)} fusion(bf16[1536,1536]{1,0:T(8,128)(2,1)} %param.26, bf16[147,1536]{1,0:T(8,128)(2,1)} %reshape.420, bf16[1536,1536]{1,0:T(8,128)(2,1)} %param.24, f32[1536]{0:T(1024)S(1)} %copy-done.10), kind=kOutput, calls=%fused_computation.7 | convolution fusion | flops 1402619904 | bytes 10798080 | tf_op jit(solution)/shard_map/dot_general | solution.py:140
  35.9 7.4 %fusion = f32[147,1536]{1,0:T(8,128)S(1)} fusion(bf16[1536,1536]{1,0:T(8,128)(2,1)} %param.26, bf16[147,1536]{1,0:T(8,128)(2,1)} %collective-permute-done, bf16[1536,1536]{1,0:T(8,128)(2,1)} %param.24, f32[1536]{0:T(1024)} %param.25), kind=kOutput, calls=%fused_computation.5 | convolution fusion | flops 1402619904 | bytes 10798080 | tf_op jit(solution)/shard_map/dot_general | solution.py:140
  44.2 19.8 %all-gather.5.cloned.1.call-done = bf16[1536,512]{1,0:T(8,128)(2,1)} async-done(((bf16[384,512]{1,0:T(8,128)(2,1)}), bf16[1536,512]{1,0:T(8,128)(2,1)}) %all-gather.5.cloned.1.call-update) | async-done | bytes 1572880 | tf_op jit(solution)/shard_map/all_gather | solution.py:117
  66.4 1.2 abs_add_fusion
  67.7 54.3 %all-reduce.3.cloned.1.call-done = f32[2,4,3,1536]{3,2,1,0:T(4,128)} async-done(((f32[2,4,3,1536]{3,2,1,0:T(4,128)}), f32[2,4,3,1536]{3,2,1,0:T(4,128)}) %all-reduce.3.cloned.1.call-update) | async-done | bytes 147472 | tf_op jit(solution)/shard_map/psum | solution.py:160
  122.0 1.0 fusion.166
  123.7 4.7 %copy.70 = bf16[2,512,1536]{2,1,0:T(8,128)(2,1)} copy(bf16[2,512,1536]{1,2,0:T(8,128)(2,1)} %bitcast.92) | data formatting | bytes 6291456 | tf_op jit(solution)/shard_map/nk,skc->nsc/dot_general | solution.py:85
  128.4 2.9 %fusion.167 = (f32[128]{0:T(128)S(1)}, f32[2,512,128]{2,1,0:T(8,128)S(1)}) fusion(bf16[2,1536,512]{2,1,0:T(8,128)(2,1)} %bitcast.93, bf16[1,128,1536]{2,1,0:T(8,128)(2,1)S(1)} %copy-done.4), kind=kOutput, calls=%fused_computation.230 | convolution fusion | flops 402784128 | bytes 4063744 | tf_op jit(solution)/shard_map/nk,skc->nsc/dot_general | solution.py:85
  132.6 2.9 %fusion.168 = (f32[12]{0:T(128)S(1)}, f32[12,1024]{1,0:T(8,128)S(1)}) fusion(bf16[12,1536]{1,0:T(8,128)(2,1)S(1)} %convert_element_type.95, bf16[1024,1536]{1,0:T(8,128)(2,1)} %bitcast.94), kind=kOutput, calls=%fused_computation.231 | convolution fusion | flops 37761012 | bytes 3231792 | tf_op jit(solution)/shard_map/nk,skc->nsc/dot_general | solution.py:85
  137.4 22.4 %all-gather.7.cloned.1.call-done = bf16[4,128,1024]{2,1,0:T(8,128)(2,1)} async-done(((bf16[1,128,1024]{2,1,0:T(8,128)(2,1)}), bf16[4,128,1024]{2,1,0:T(8,128)(2,1)}) %all-gather.7.cloned.1.call-update) | async-done | bytes 1048592 | tf_op jit(solution)/shard_map/all_gather | solution.py:122
  159.8 2.2 %fusion.2 = f32[4,128,768]{1,2,0:T(8,128)S(1)} fusion(bf16[4,128,1024]{2,1,0:T(8,128)(2,1)} %all-gather.7.cloned.1.call-done, bf16[1024,768]{1,0:T(8,128)(2,1)S(1)} %copy-done), kind=kOutput, calls=%fused_computation.8 | convolution fusion | flops 805306368 | bytes 4194304 | tf_op jit(solution)/shard_map/rnk,kc->rnc/dot_general | solution.py:124
  163.8 1.2 reshape_reshape.4
  165.0 2.5 %convert_reduce_fusion = (f32[4,512]{1,0:T(4,128)S(1)}, bf16[4,512,512]{1,2,0:T(8,128)(2,1)S(1)}) fusion(f32[512,512]{0,1:T(8,128)S(1)} %copy-done.2, f32[4]{0:T(128)S(1)} %dynamic_slice.16, bf16[512,4,3,64]{0,3,2,1:T(8,128)(2,1)} %reshape_reshape.4, pred[512]{0:T(512)(128)(4,1)S(1)} %iota_compare_fusion), kind=kOutput, calls=%fused_computation | convolution fusion | flops 141555712 | bytes 3678736 | tf_op jit(solution)/shard_map/qhd,khd->hqk/dot_general | solution.py:193
  167.5 1.4 fusion.6
  169.7 3.4 %all-to-all-start = ((bf16[4,128,256]{1,2,0:T(8,128)(2,1)}), bf16[4,128,256]{1,2,0:T(8,128)(2,1)S(1)}, u32[]{:S(2)}, u32[]{:S(2)}) async-start(bf16[4,128,256]{1,2,0:T(8,128)(2,1)} %copy.82), calls=%async_computation | async-start | bytes 524288 | tf_op jit(solution)/shard_map/all_to_all | solution.py:203
  173.8 8.3 %all-to-all-done = bf16[4,128,256]{1,2,0:T(8,128)(2,1)S(1)} async-done(((bf16[4,128,256]{1,2,0:T(8,128)(2,1)}), bf16[4,128,256]{1,2,0:T(8,128)(2,1)S(1)}, u32[]{:S(2)}, u32[]{:S(2)}) %all-to-all-start) | async-done | bytes 262176 | tf_op jit(solution)/shard_map/all_to_all | solution.py:203
  (87 shorter events, 13.9 us)
Async XLA Ops:
  8.0 127.8 %copy-start = (bf16[1024,768]{1,0:T(8,128)(2,1)S(1)}, bf16[1024,768]{1,0:T(8,128)(2,1)}, u32[]{:S(2)}) copy-start(bf16[1024,768]{1,0:T(8,128)(2,1)} %param.34) | copy-start | bytes 4718596
  8.0 16.8 %copy-start.5 = (bf16[384,1024]{1,0:T(8,128)(2,1)S(1)}, bf16[384,1024]{1,0:T(8,128)(2,1)}, u32[]{:S(2)}) copy-start(bf16[384,1024]{1,0:T(8,128)(2,1)} %param.32) | copy-start | bytes 2359300
  8.0 17.7 %copy-start.10 = (f32[1536]{0:T(1024)S(1)}, f32[1536]{0:T(1024)}, u32[]{:S(2)}) copy-start(f32[1536]{0:T(1024)} %param.25) | copy-start | bytes 18436
  8.0 56.0 %all-gather.5.cloned.1.call-start = ((), (), s32[]{:S(2)}) async-start(), calls=%async_computation.2 | async-start | bytes 1966080 | tf_op jit(solution)/shard_map/all_gather | solution.py:117
  21.9 13.9 %collective-permute-start = (bf16[147,1536]{1,0:T(8,128)(2,1)}, bf16[147,1536]{1,0:T(8,128)(2,1)}, u32[]{:S(2)}, u32[]{:S(2)}) collective-permute-start(bf16[147,1536]{1,0:T(8,128)(2,1)} %reshape.420), channel_id=1, source_target_pairs={{0,2},{2,0},{1,3},{3,1},{4,6},{6,4},{5,7},{7,5},{8,10},{10,8},{9,1... | collective-permute-start | bytes 1354760 | tf_op jit(solution)/shard_map/ppermute | solution.py:146
  25.7 96.3 %all-reduce.3.cloned.1.call-start = ((), (), s32[]{:S(2)}) async-start(), calls=%async_computation.1 | async-start | bytes 393216 | tf_op jit(solution)/shard_map/psum | solution.py:160
  25.7 7.5 %copy-start.1 = (bf16[1,3,49,1536]{3,2,1,0:T(8,128)(2,1)S(1)}, bf16[1,3,49,1536]{3,2,1,0:T(8,128)(2,1)}, u32[]{:S(2)}) copy-start(bf16[1,3,49,1536]{3,2,1,0:T(8,128)(2,1)} %param.19) | copy-start | bytes 1354756
  25.7 8.2 %copy-start.6 = (f32[1536]{0:T(1024)S(1)}, f32[1536]{0:T(1024)}, u32[]{:S(2)}) copy-start(f32[1536]{0:T(1024)} %param.28) | copy-start | bytes 18436
  35.0 0.7 copy-start.3
  43.3 80.1 %copy-start.7 = (f32[1536]{0:T(1024)S(1)}, f32[1536]{0:T(1024)}, u32[]{:S(2)}) copy-start(f32[1536]{0:T(1024)} %param.30) | copy-start | bytes 18436
  43.4 80.0 %copy-start.8 = (f32[1536]{0:T(1024)S(1)}, f32[1536]{0:T(1024)}, u32[]{:S(2)}) copy-start(f32[1536]{0:T(1024)} %param.29) | copy-start | bytes 18436
  44.2 79.5 %all-gather.9.cloned.1.call-start = ((), (), s32[]{:S(2)}) async-start(), calls=%async_computation.4 | async-start | bytes 4718592 | tf_op jit(solution)/shard_map/all_gather | solution.py:118
  64.0 95.7 %all-gather.7.cloned.1.call-start = ((), (), s32[]{:S(2)}) async-start(), calls=%async_computation.3 | async-start | bytes 1310720 | tf_op jit(solution)/shard_map/all_gather | solution.py:122
  123.7 4.7 %copy-start.4 = (bf16[1,128,1536]{2,1,0:T(8,128)(2,1)S(1)}, bf16[1,128,1536]{2,1,0:T(8,128)(2,1)}, u32[]{:S(2)}) copy-start(bf16[1,128,1536]{2,1,0:T(8,128)(2,1)} %param.31) | copy-start | bytes 1179652
  128.4 3.3 %copy-start.9 = (f32[1024]{0:T(1024)S(1)}, f32[1024]{0:T(1024)}, u32[]{:S(2)}) copy-start(f32[1024]{0:T(1024)} %param.33) | copy-start | bytes 12292
  162.4 2.5 %copy-start.2 = (f32[512,512]{0,1:T(8,128)S(1)}, f32[512,512]{0,1:T(8,128)}, u32[]{:S(2)}) copy-start(f32[512,512]{0,1:T(8,128)} %abs_add_fusion) | copy-start | bytes 3145732
  169.7 12.4 %all-to-all-start = ((bf16[4,128,256]{1,2,0:T(8,128)(2,1)}), bf16[4,128,256]{1,2,0:T(8,128)(2,1)S(1)}, u32[]{:S(2)}, u32[]{:S(2)}) async-start(bf16[4,128,256]{1,2,0:T(8,128)(2,1)} %copy.82), calls=%async_computation | async-start | bytes 524288 | tf_op jit(solution)/shard_map/all_to_all | solution.py:203
Sparse Core Ops, SparseCore 0:
  25.8 38.1 all-gather.4
  65.6 11.1 all-gather.8
  132.8 26.9 all-gather.6
Sparse Core Ops, SparseCore 1:
  44.2 77.7 all-reduce.2

commit v4 on v3

--- a/solution.py
+++ b/solution.py
@@ -150,18 +150,19 @@
     own_term = jnp.mean(tile_data, axis=1) + layer_scale * (
         block_sums(normed) / positions + down_bias
     )
-    slots = jnp.zeros((n_rep, n_slide) + own_term.shape, jnp.float32)
-    slots = lax.dynamic_update_slice(slots, own_term[None, None], (my_rep, my_slide, 0, 0))
-    for k, rows in enumerate(received, start=1):
-        term = layer_scale * (block_sums(rows) / positions)
-        slots = lax.dynamic_update_slice(
-            slots, term[None, None], ((my_rep - k) % n_rep, my_slide, 0, 0)
+    returned = [
+        lax.ppermute(
+            layer_scale * (block_sums(rows) / positions),
+            "rep",
+            perm=[(r, (r - k) % n_rep) for r in range(n_rep)],
         )
-    pooled_all = lax.psum(slots, ("slide", "rep"))
-    pooled = lax.dynamic_index_in_dim(pooled_all, my_rep, 0, keepdims=False)
-    pooled = pooled.reshape(n_slide * fresh_count, -1)
-    embedded_all = layer_norm(pooled, head_gain, head_bias, 1e-06).astype(jnp.bfloat16)
-    embedded = lax.dynamic_slice_in_dim(embedded_all, my_slide * fresh_count, fresh_count, 0)
+        for k, rows in enumerate(received, start=1)
+    ]
+    pooled = own_term
+    for term in returned:
+        pooled = pooled + term
+    embedded = layer_norm(pooled, head_gain, head_bias, 1e-06).astype(jnp.bfloat16)
+    embedded_all = lax.all_gather(embedded, "slide", axis=0, tiled=True)
 
     fresh_normed = project(embedded_all, weight_parts, slide_gain)
     fresh_mixed = normalize_heads(

time: 191 us -> 137 us (0.72)
  waiting for transfers between devices: 105 us -> 41 us
  blocking collectives: 0 us -> 25.2 us
  local copies, waits for them, and re-layouts: 20.5 us -> 15.5 us
  other arithmetic: 8.67 us -> 4.31 us
  matrix products: 27.3 us -> 24.7 us
  starting transfers between devices: 6.69 us -> 4.78 us
    psum x1 -> x0, waiting for transfers between devices: 54.3 us -> none  [on_device(): pooled_all = lax.psum(slots, ('slide', 'rep'))]
    all_gather x0 -> x1, blocking collectives: none -> 13.3 us  [on_device(): embedded_all = lax.all_gather(embedded, 'slide', axis=0, tiled=True)]
    all_to_all x0 -> x1, blocking collectives: none -> 11.8 us  [on_device(): lax.all_to_all(attended, 'slide', split_axis=0, concat_axis=1, tiled=True)]
    all_to_all x1 -> x0, waiting for transfers between devices: 8.34 us -> none  [on_device(): lax.all_to_all(attended, 'slide', split_axis=0, concat_axis=1, tiled=True)]
    dot_general x1 -> x0, local copies, waits for them, and re-layouts: 4.74 us -> none  [project(): jnp.einsum('nk,skc->nsc', rows, weight_parts, preferred_element_type=jnp....]
    all_gather x1, waiting for transfers between devices: 19.8 us -> 15.7 us  [on_device(): cols_full = lax.all_gather(my_cols, 'slide', axis=0, tiled=True)]
    all_to_all x1 -> x0, starting transfers between devices: 3.41 us -> none  [on_device(): lax.all_to_all(attended, 'slide', split_axis=0, concat_axis=1, tiled=True)]
    all_gather x1, waiting for transfers between devices: 22.4 us -> 25.1 us  [on_device(): stale_all = lax.all_gather(stale_normed, 'slide', axis=0, tiled=False)]
  transfers between devices with their start and end apart: 6 -> 5, of which waited for: 5 -> 3; matrix products, arithmetic and copies ran while one was open for 15% -> 22% of each run, Pallas kernels for 0% -> 4%
where the time goes in v4:
time: 137 us; the launch traced here: 136 us
  waiting for transfers between devices  41 us (30%)
  blocking collectives  25.2 us (18%)
  matrix products  24.7 us (18%)
  local copies, waits for them, and re-layouts  15.5 us (11%)
  between operations  14.8 us (11%)
  Pallas kernels  5.74 us (4%)
  starting transfers between devices  4.78 us (3%)
  other arithmetic  4.31 us (3%)
    all_gather x1, waiting for transfers between devices, on_device(): stale_all = lax.all_gather(stale_normed, 'slide', axis=0, tiled=False)  25.1 us
    all_gather x1, waiting for transfers between devices, on_device(): cols_full = lax.all_gather(my_cols, 'slide', axis=0, tiled=True)  15.7 us
    dot_general x2, matrix products, block_sums(): jnp.dot(hidden, down_weight, preferred_element_type=jnp.float32)  15.6 us
    all_gather x1, blocking collectives, on_device(): embedded_all = lax.all_gather(embedded, 'slide', axis=0, tiled=True)  13.3 us
    all_to_all x1, blocking collectives, on_device(): lax.all_to_all(attended, 'slide', split_axis=0, concat_axis=1, tiled=True)  11.8 us
    pallas_call x1, Pallas kernels, dw_ln(): pl.pallas_call(dw_ln_kernel, grid=(T,), in_specs=[pl.BlockSpec((1, SIDE,...  5.74 us
    unnamed x31, local copies, waits for them, and re-layouts  3.92 us
    dot_general x2, matrix products, project(): jnp.einsum('nk,skc->nsc', rows, weight_parts, preferred_element_type=jnp....  3.7 us
  transfers between devices with their start and end apart: 5, of which 3 were waited for; matrix products, arithmetic and copies ran while one was open for 22% of the time, Pallas kernels for 4%

profile of v4, /device:TPU:0, one launch (start us, length us, event | category | flops | bytes accessed | tf_op | source)
XLA Modules:
  0.0 136.0 jit_solution(5958011780595691485)
XLA Ops:
  7.3 1.1 copy-done
  9.1 1.2 reshape_squeeze.3
  10.3 1.3 broadcast_in_dim.38.b_ref
  11.6 1.3 broadcast_in_dim.39.g_ref
  12.9 1.3 broadcast_in_dim.44.nb_ref
  14.2 0.9 pad.4.x_ref
  15.1 5.7 %shard_map.194 = bf16[3,7,8,1536]{3,2,1,0:T(8,128)(2,1)} custom-call(bf16[3,7,8,1536]{3,2,1,0:T(8,128)(2,1)} %pad.4.x_ref, f32[49,1536]{1,0:T(8,128)} %w_ref.1, f32[1,1536]{1,0:T(1,128)} %broadcast_in_dim.38.b_ref, f32[1,1536]{1,0:T(1,128)} %broadcast_in_dim.39.g_ref, f32[1,1536]{1,0:T(1,128)} %broadcast_in_dim.44.nb_ref), custom_call_target="tpu_custom_call" | custom-call | tf_op jit(solution)/shard_map/pallas_call | solution.py:58
  20.9 1.2 reshape.294
  22.1 3.0 %collective-permute-start = (bf16[147,1536]{1,0:T(8,128)(2,1)S(1)}, bf16[147,1536]{1,0:T(8,128)(2,1)S(1)}, u32[]{:S(2)}, u32[]{:S(2)}) collective-permute-start(bf16[147,1536]{1,0:T(8,128)(2,1)S(1)} %reshape.294), channel_id=1, source_target_pairs={{0,2},{2,0},{1,3},{3,1},{4,6},{6,4},{5,7},{7,5},{8,10},{10,8},{9,1... | collective-permute-start | bytes 1354760 | tf_op jit(solution)/shard_map/ppermute | solution.py:146
  25.1 7.4 %fusion.1 = f32[147,1536]{1,0:T(8,128)S(1)} fusion(bf16[1536,1536]{1,0:T(8,128)(2,1)} %param.26, bf16[147,1536]{1,0:T(8,128)(2,1)S(1)} %reshape.294, bf16[1536,1536]{1,0:T(8,128)(2,1)} %param.24, f32[1536]{0:T(1024)S(1)} %copy-done.12), kind=kOutput, calls=%fused_computation.7 | convolution fusion | flops 1402619904 | bytes 10798080 | tf_op jit(solution)/shard_map/dot_general | solution.py:140
  32.5 1.3 abs_add_fusion
  33.7 15.7 %all-gather.6.cloned.1.call-done = bf16[1536,512]{1,0:T(8,128)(2,1)} async-done(((bf16[384,512]{1,0:T(8,128)(2,1)}), bf16[1536,512]{1,0:T(8,128)(2,1)}) %all-gather.6.cloned.1.call-update) | async-done | bytes 1572880 | tf_op jit(solution)/shard_map/all_gather | solution.py:117
  50.3 8.2 %fusion = f32[147,1536]{1,0:T(8,128)} fusion(bf16[1536,1536]{1,0:T(8,128)(2,1)} %param.26, bf16[147,1536]{1,0:T(8,128)(2,1)S(1)} %collective-permute-done, bf16[1536,1536]{1,0:T(8,128)(2,1)} %param.24, f32[1536]{0:T(1024)S(1)} %copy-done.12), kind=kOutput, calls=%fused_computation.5 | convolution fusion | flops 1402619904 | bytes 10798080 | tf_op jit(solution)/shard_map/dot_general | solution.py:140
  58.5 1.3 reshape.304
  60.0 1.7 %collective-permute-start.1 = (f32[3,1536]{1,0:T(4,128)S(1)}, f32[3,1536]{1,0:T(4,128)S(1)}, u32[]{:S(2)}, u32[]{:S(2)}) collective-permute-start(f32[3,1536]{1,0:T(4,128)S(1)} %broadcast_multiply_fusion), channel_id=1, source_target_pairs={{0,2},{2,0},{1,3},{3,1},{4,6},{6,4},{5,7},{7,5},{8,10},{10,8},{9,1... | collective-permute-start | bytes 55304 | tf_op jit(solution)/shard_map/ppermute | solution.py:154
  61.9 1.8 %copy.40 = bf16[1024,768]{0,1:T(8,128)(2,1)S(1)} copy(bf16[1024,768]{1,0:T(8,128)(2,1)} %param.34) | data formatting | bytes 3145728 | tf_op args[15]
  64.3 13.3 %all-gather.1 = bf16[4,3,1536]{2,1,0:T(4,128)(2,1)S(1)} all-gather(bf16[1,3,1536]{2,1,0:T(4,128)(2,1)S(1)} %fusion.95), channel_id=1, replica_groups=mesh['groups'=2,'slide'=4,'rep'=2,'section'=2] {'slide'}, dimensions={0}, use_global_device_ids=true | all-gather | bytes 46080 | tf_op jit(solution)/shard_map/all_gather | solution.py:165
  77.8 2.7 %fusion.158 = (f32[12]{0:T(128)S(1)}, f32[12,2,512]{2,0,1:T(8,128)S(1)}) fusion(bf16[12,1536,1]{1,0,2:T(8,128)(2,1)S(1)} %reshape.308, bf16[2,1536,512]{2,1,0:T(8,128)(2,1)} %bitcast.81), kind=kOutput, calls=%fused_computation.219 | convolution fusion | flops 37761012 | bytes 3231792 | tf_op jit(solution)/shard_map/nk,skc->nsc/dot_general | solution.py:85
  80.6 1.0 fusion.157
  84.8 25.1 %all-gather.8.cloned.1.call-done = bf16[4,128,1024]{2,1,0:T(8,128)(2,1)} async-done(((bf16[1,128,1024]{2,1,0:T(8,128)(2,1)}), bf16[4,128,1024]{2,1,0:T(8,128)(2,1)}) %all-gather.8.cloned.1.call-update) | async-done | bytes 1048592 | tf_op jit(solution)/shard_map/all_gather | solution.py:122
  109.9 2.7 %fusion.2 = f32[4,128,768]{1,2,0:T(8,128)S(1)} fusion(bf16[4,128,1024]{2,1,0:T(8,128)(2,1)} %all-gather.8.cloned.1.call-done, bf16[1024,768]{1,0:T(8,128)(2,1)} %param.34), kind=kOutput, calls=%fused_computation.8 | convolution fusion | flops 805306368 | bytes 4194304 | tf_op jit(solution)/shard_map/rnk,kc->rnc/dot_general | solution.py:124
  114.7 1.5 %convert_reduce_fusion = (f32[4,512]{1,0:T(4,128)S(1)}, bf16[4,512,512]{1,2,0:T(8,128)(2,1)S(1)}) fusion(f32[512,512]{0,1:T(8,128)S(1)} %copy-done.3, f32[4]{0:T(128)S(1)} %dynamic_slice.7, bf16[512,4,3,64]{0,3,2,1:T(8,128)(2,1)S(1)} %reshape_reshape.4, pred[512]{0:T(512)(128)(4,1)S(1)} %iota_compare_fusion), kind=kOutput, calls=%fused_computation | convolution fusion | flops 141555712 | bytes 3679232 | tf_op jit(solution)/shard_map/qhd,khd->hqk/dot_general | solution.py:194
  116.8 11.8 %all_to_all.16 = bf16[4,128,256]{1,2,0:T(8,128)(2,1)S(1)} all-to-all(bf16[4,128,256]{1,2,0:T(8,128)(2,1)S(1)} %copy.51), channel_id=1, replica_groups=mesh['groups'=2,'slide'=4,'rep'=2,'section'=2] {'slide'}, dimensions={0} | all-to-all | bytes 524288 | tf_op jit(solution)/shard_map/all_to_all | solution.py:204
  128.6 0.8 copy.52
  (86 shorter events, 7.9 us)
Async XLA Ops:
  7.2 1.1 copy-start
  7.2 17.9 %copy-start.11 = (s32[1,2,512]{2,1,0:T(2,128)S(1)}, s32[1,2,512]{2,1,0:T(2,128)}, u32[]{:S(2)}) copy-start(s32[1,2,512]{2,1,0:T(2,128)} %param.36) | copy-start | bytes 12292
  7.2 17.9 %copy-start.12 = (f32[1536]{0:T(1024)S(1)}, f32[1536]{0:T(1024)}, u32[]{:S(2)}) copy-start(f32[1536]{0:T(1024)} %param.25) | copy-start | bytes 18436
  7.2 42.2 %all-gather.6.cloned.1.call-start = ((), (), s32[]{:S(2)}) async-start(), calls=%async_computation.1 | async-start | bytes 1966080 | tf_op jit(solution)/shard_map/all_gather | solution.py:117
  9.1 68.6 %all-gather.10.cloned.1.call-start = ((), (), s32[]{:S(2)}) async-start(), calls=%async_computation.3 | async-start | bytes 4718592 | tf_op jit(solution)/shard_map/all_gather | solution.py:118
  22.1 28.2 %collective-permute-start = (bf16[147,1536]{1,0:T(8,128)(2,1)S(1)}, bf16[147,1536]{1,0:T(8,128)(2,1)S(1)}, u32[]{:S(2)}, u32[]{:S(2)}) collective-permute-start(bf16[147,1536]{1,0:T(8,128)(2,1)S(1)} %reshape.294), channel_id=1, source_target_pairs={{0,2},{2,0},{1,3},{3,1},{4,6},{6,4},{5,7},{7,5},{8,10},{10,8},{9,1... | collective-permute-start | bytes 1354760 | tf_op jit(solution)/shard_map/ppermute | solution.py:146
  25.1 24.4 %copy-start.6 = (f32[1536]{0:T(1024)S(1)}, f32[1536]{0:T(1024)}, u32[]{:S(2)}) copy-start(f32[1536]{0:T(1024)} %param.28) | copy-start | bytes 18436
  25.1 25.1 %copy-start.2 = (bf16[1,3,49,1536]{3,2,1,0:T(8,128)(2,1)S(1)}, bf16[1,3,49,1536]{3,2,1,0:T(8,128)(2,1)}, u32[]{:S(2)}) copy-start(bf16[1,3,49,1536]{3,2,1,0:T(8,128)(2,1)} %param.19) | copy-start | bytes 1354756
  49.5 60.4 %all-gather.8.cloned.1.call-start = ((), (), s32[]{:S(2)}) async-start(), calls=%async_computation.2 | async-start | bytes 1310720 | tf_op jit(solution)/shard_map/all_gather | solution.py:122
  58.5 3.3 %copy-start.7 = (f32[1024]{0:T(1024)S(1)}, f32[1024]{0:T(1024)}, u32[]{:S(2)}) copy-start(f32[1024]{0:T(1024)} %param.33) | copy-start | bytes 12292
  59.9 3.7 %copy-start.13 = (f32[16]{0:T(128)S(1)}, f32[16]{0:T(128)}, u32[]{:S(2)}) copy-start(f32[16]{0:T(128)} %param.35) | copy-start | bytes 196
  60.0 3.9 %copy-start.8 = (f32[1536]{0:T(1024)S(1)}, f32[1536]{0:T(1024)}, u32[]{:S(2)}) copy-start(f32[1536]{0:T(1024)} %param.27) | copy-start | bytes 18436
  60.0 3.9 %collective-permute-start.1 = (f32[3,1536]{1,0:T(4,128)S(1)}, f32[3,1536]{1,0:T(4,128)S(1)}, u32[]{:S(2)}, u32[]{:S(2)}) collective-permute-start(f32[3,1536]{1,0:T(4,128)S(1)} %broadcast_multiply_fusion), channel_id=1, source_target_pairs={{0,2},{2,0},{1,3},{3,1},{4,6},{6,4},{5,7},{7,5},{8,10},{10,8},{9,1... | collective-permute-start | bytes 55304 | tf_op jit(solution)/shard_map/ppermute | solution.py:154
  61.6 2.6 %copy-start.9 = (f32[1536]{0:T(1024)S(1)}, f32[1536]{0:T(1024)}, u32[]{:S(2)}) copy-start(f32[1536]{0:T(1024)} %param.30) | copy-start | bytes 18436
  61.6 2.6 %copy-start.10 = (f32[1536]{0:T(1024)S(1)}, f32[1536]{0:T(1024)}, u32[]{:S(2)}) copy-start(f32[1536]{0:T(1024)} %param.29) | copy-start | bytes 18436
  61.9 18.6 %copy-start.4 = (bf16[1,128,1536]{2,1,0:T(8,128)(2,1)S(1)}, bf16[1,128,1536]{2,1,0:T(8,128)(2,1)}, u32[]{:S(2)}) copy-start(bf16[1,128,1536]{2,1,0:T(8,128)(2,1)} %param.31) | copy-start | bytes 1179652
  64.3 17.3 %copy-start.5 = (bf16[1,3,1536]{2,1,0:T(4,128)(2,1)}, bf16[1,3,1536]{2,1,0:T(4,128)(2,1)S(1)}, u32[]{:S(2)}) copy-start(bf16[1,3,1536]{2,1,0:T(4,128)(2,1)S(1)} %fusion.95) | copy-start | bytes 27652
  77.7 2.8 %copy-start.1 = (bf16[3072,512]{1,0:T(8,128)(2,1)S(1)}, bf16[3072,512]{1,0:T(8,128)(2,1)}, u32[]{:S(2)}) copy-start(bf16[3072,512]{1,0:T(8,128)(2,1)} %all-gather.10.cloned.1.call-done) | copy-start | bytes 9437188
  113.3 1.4 %copy-start.3 = (f32[512,512]{0,1:T(8,128)S(1)}, f32[512,512]{0,1:T(8,128)}, u32[]{:S(2)}) copy-start(f32[512,512]{0,1:T(8,128)} %abs_add_fusion) | copy-start | bytes 3145732
Sparse Core Ops, SparseCore 0:
  9.6 39.7 all-gather.5
  51.0 10.9 all-gather.9
  83.0 26.8 all-gather.7

commit v5 on v4

--- a/solution.py
+++ b/solution.py
@@ -115,14 +115,6 @@
         in_weight, lax.axis_index("section") * col_part, col_part, 1
     )
     cols_full = lax.all_gather(my_cols, "slide", axis=0, tiled=True)
-    weight_parts = lax.all_gather(cols_full, "section", axis=0, tiled=False)
-
-    fresh_count = tile_features.shape[1]
-    stale_normed = project(embed_store[0], weight_parts, slide_gain)
-    stale_all = lax.all_gather(stale_normed, "slide", axis=0, tiled=False)
-    stale_mixed = normalize_heads(
-        jnp.einsum("rnk,kc->rnc", stale_all, qkv_weight, preferred_element_type=jnp.float32)
-    )
 
     tile_data = tile_features[0].astype(jnp.float32)
     fresh_count = tile_data.shape[0]
@@ -150,28 +142,27 @@
     own_term = jnp.mean(tile_data, axis=1) + layer_scale * (
         block_sums(normed) / positions + down_bias
     )
+    peer_terms = [layer_scale * (block_sums(rows) / positions) for rows in received]
+    cols_full, own_term, peer_terms = lax.optimization_barrier(
+        (cols_full, own_term, peer_terms)
+    )
+    weight_parts = lax.all_gather(cols_full, "section", axis=0, tiled=False)
     returned = [
-        lax.ppermute(
-            layer_scale * (block_sums(rows) / positions),
-            "rep",
-            perm=[(r, (r - k) % n_rep) for r in range(n_rep)],
-        )
-        for k, rows in enumerate(received, start=1)
+        lax.ppermute(term, "rep", perm=[(r, (r - k) % n_rep) for r in range(n_rep)])
+        for k, term in enumerate(peer_terms, start=1)
     ]
     pooled = own_term
     for term in returned:
         pooled = pooled + term
     embedded = layer_norm(pooled, head_gain, head_bias, 1e-06).astype(jnp.bfloat16)
-    embedded_all = lax.all_gather(embedded, "slide", axis=0, tiled=True)
-
-    fresh_normed = project(embedded_all, weight_parts, slide_gain)
-    fresh_mixed = normalize_heads(
-        jnp.dot(fresh_normed, qkv_weight, preferred_element_type=jnp.float32)
-    ).reshape(n_slide, fresh_count, -1)
-    local_heads = jnp.concatenate([fresh_mixed, stale_mixed[:, fresh_count:]], axis=1)
-    n_slide = local_heads.shape[0]
-    seq_len = n_slide * local_heads.shape[1]
-    local_heads = local_heads.reshape(seq_len, -1)
+
+    seq_rows = jnp.concatenate([embedded, embed_store[0, fresh_count:]], axis=0)
+    normed_seq = project(seq_rows, weight_parts, slide_gain)
+    normed_all = lax.all_gather(normed_seq, "slide", axis=0, tiled=True)
+    local_heads = normalize_heads(
+        jnp.dot(normed_all, qkv_weight, preferred_element_type=jnp.float32)
+    )
+    seq_len = local_heads.shape[0]
 
     heads_here = local_heads.shape[1] // (3 * HDIM)
     arranged = local_heads.reshape(seq_len, heads_here, 3, HDIM)

time: 137 us -> 122 us (0.89)
  blocking collectives: 25.2 us -> 0 us
  waiting for transfers between devices: 41 us -> 49.3 us
  starting transfers between devices: 4.78 us -> 8.59 us
  matrix products: 24.7 us -> 22.6 us
  other arithmetic: 4.31 us -> 5.79 us
    all_gather x1 -> x0, blocking collectives: 13.3 us -> none  [on_device(): embedded_all = lax.all_gather(embedded, 'slide', axis=0, tiled=True)]
    all_to_all x1 -> x0, blocking collectives: 11.8 us -> none  [on_device(): lax.all_to_all(attended, 'slide', split_axis=0, concat_axis=1, tiled=True)]
    all_gather x1, waiting for transfers between devices: 15.7 us -> 4 us  [on_device(): cols_full = lax.all_gather(my_cols, 'slide', axis=0, tiled=True)]
    all_gather x1, waiting for transfers between devices: 0.02 us -> 7.25 us  [on_device(): weight_parts = lax.all_gather(cols_full, 'section', axis=0, tiled=False)]
    all_to_all x0 -> x1, waiting for transfers between devices: none -> 6.2 us  [on_device(): lax.all_to_all(attended, 'slide', split_axis=0, concat_axis=1, tiled=True)]
    all_gather x1, waiting for transfers between devices: 25.1 us -> 30.5 us  [on_device(): normed_all = lax.all_gather(normed_seq, 'slide', axis=0, tiled=True)]
    all_to_all x0 -> x1, starting transfers between devices: none -> 3.81 us  [on_device(): lax.all_to_all(attended, 'slide', split_axis=0, concat_axis=1, tiled=True)]
    unnamed x31 -> x19, local copies, waits for them, and re-layouts: 3.92 us -> 0.91 us
  transfers between devices with their start and end apart: 5 -> 6, of which waited for: 3 -> 5; matrix products, arithmetic and copies ran while one was open for 22% -> 25% of each run, Pallas kernels for 4% -> 5%
where the time goes in v5:
time: 122 us; the launch traced here: 121 us
  waiting for transfers between devices  49.3 us (40%)
  matrix products  22.6 us (19%)
  between operations  14.6 us (12%)
  local copies, waits for them, and re-layouts  14.3 us (12%)
  starting transfers between devices  8.59 us (7%)
  other arithmetic  5.79 us (5%)
  Pallas kernels  5.73 us (5%)
    all_gather x1, waiting for transfers between devices, on_device(): normed_all = lax.all_gather(normed_seq, 'slide', axis=0, tiled=True)  30.5 us
    dot_general x2, matrix products, block_sums(): jnp.dot(hidden, down_weight, preferred_element_type=jnp.float32)  15.9 us
    all_gather x1, waiting for transfers between devices, on_device(): weight_parts = lax.all_gather(cols_full, 'section', axis=0, tiled=False)  7.25 us
    all_to_all x1, waiting for transfers between devices, on_device(): lax.all_to_all(attended, 'slide', split_axis=0, concat_axis=1, tiled=True)  6.2 us
    pallas_call x1, Pallas kernels, dw_ln(): pl.pallas_call(dw_ln_kernel, grid=(T,), in_specs=[pl.BlockSpec((1, SIDE,...  5.73 us
    all_gather x1, waiting for transfers between devices, on_device(): cols_full = lax.all_gather(my_cols, 'slide', axis=0, tiled=True)  4 us
    all_to_all x1, starting transfers between devices, on_device(): lax.all_to_all(attended, 'slide', split_axis=0, concat_axis=1, tiled=True)  3.81 us
    ppermute x1, starting transfers between devices, on_device(): lax.ppermute(normed, 'rep', perm=[(r, (r + k) % n_rep) for r in range(n_r...  2.94 us
  transfers between devices with their start and end apart: 6, of which 5 were waited for; matrix products, arithmetic and copies ran while one was open for 25% of the time, Pallas kernels for 5%

profile of v5, /device:TPU:0, one launch (start us, length us, event | category | flops | bytes accessed | tf_op | source)
XLA Modules:
  0.0 120.9 jit_solution(10197064919931339408)
XLA Ops:
  7.2 1.9 %constant_dynamic-slice_fusion = bf16[384,512]{1,0:T(8,128)(2,1)} fusion(bf16[384,1024]{1,0:T(8,128)(2,1)} %param.32, s32[]{:T(128)S(6)} %select_n.22), kind=kLoop, calls=%fused_computation.144 | loop fusion | bytes 786436 | tf_op jit(solution)/shard_map/dynamic_slice | solution.py:114
  9.2 1.3 %broadcast_in_dim.42.b_ref = f32[1,1536]{1,0:T(1,128)} reshape(f32[1536]{0:T(1024)} %param.21) | data formatting | bytes 12288 | tf_op jit(solution)/shard_map/broadcast_in_dim | solution.py:71
  10.5 1.3 %broadcast_in_dim.43.g_ref = f32[1,1536]{1,0:T(1,128)} reshape(f32[1536]{0:T(1024)} %param.22) | data formatting | bytes 12288 | tf_op jit(solution)/shard_map/broadcast_in_dim | solution.py:71
  11.8 1.3 %broadcast_in_dim.44.nb_ref = f32[1,1536]{1,0:T(1,128)} reshape(f32[1536]{0:T(1024)} %param.23) | data formatting | bytes 12288 | tf_op jit(solution)/shard_map/broadcast_in_dim | solution.py:71
  13.1 1.2 reshape_squeeze.3
  14.3 0.9 pad.4.x_ref
  15.2 5.7 %shard_map.194 = bf16[3,7,8,1536]{3,2,1,0:T(8,128)(2,1)} custom-call(bf16[3,7,8,1536]{3,2,1,0:T(8,128)(2,1)} %pad.4.x_ref, f32[49,1536]{1,0:T(8,128)} %w_ref.1, f32[1,1536]{1,0:T(1,128)} %broadcast_in_dim.42.b_ref, f32[1,1536]{1,0:T(1,128)} %broadcast_in_dim.43.g_ref, f32[1,1536]{1,0:T(1,128)} %broadcast_in_dim.44.nb_ref), custom_call_target="tpu_custom_call" | custom-call | tf_op jit(solution)/shard_map/pallas_call | solution.py:58
  20.9 2.0 %reshape.168 = bf16[147,1536]{1,0:T(8,128)(2,1)} reshape(bf16[3,7,7,1536]{3,2,1,0:T(8,128)(2,1)} %bitcast.66) | data formatting | bytes 903168 | tf_op jit(solution)/shard_map/reshape | solution.py:72
  22.9 2.9 %collective-permute-start = (bf16[147,1536]{1,0:T(8,128)(2,1)}, bf16[147,1536]{1,0:T(8,128)(2,1)}, u32[]{:S(2)}, u32[]{:S(2)}) collective-permute-start(bf16[147,1536]{1,0:T(8,128)(2,1)} %reshape.168), channel_id=1, source_target_pairs={{0,2},{2,0},{1,3},{3,1},{4,6},{6,4},{5,7},{7,5},{8,10},{10,8},{9,1... | collective-permute-start | bytes 1354760 | tf_op jit(solution)/shard_map/ppermute | solution.py:138
  25.8 8.4 %fusion.1 = f32[147,1536]{1,0:T(8,128)} fusion(bf16[1536,1536]{1,0:T(8,128)(2,1)} %param.26, bf16[147,1536]{1,0:T(8,128)(2,1)} %reshape.168, bf16[1536,1536]{1,0:T(8,128)(2,1)} %param.24, f32[1536]{0:T(1024)S(1)} %copy-done.7), kind=kOutput, calls=%fused_computation.7 | convolution fusion | flops 1402619904 | bytes 10798080 | tf_op jit(solution)/shard_map/dot_general | solution.py:132
  34.2 1.3 %reshape.176 = f32[3,49,1536]{2,1,0:T(8,128)S(1)} reshape(f32[147,1536]{1,0:T(8,128)} %fusion.1) | data formatting | bytes 1806336 | tf_op jit(solution)/shard_map/reshape | solution.py:135
  36.9 7.5 %fusion = f32[147,1536]{1,0:T(8,128)S(1)} fusion(bf16[1536,1536]{1,0:T(8,128)(2,1)} %param.26, bf16[147,1536]{1,0:T(8,128)(2,1)} %collective-permute-done, bf16[1536,1536]{1,0:T(8,128)(2,1)} %param.24, f32[1536]{0:T(1024)} %param.25), kind=kOutput, calls=%fused_computation.5 | convolution fusion | flops 1402619904 | bytes 10798080 | tf_op jit(solution)/shard_map/dot_general | solution.py:132
  45.4 4.0 %all-gather.5.cloned.1.call-done = bf16[1536,512]{1,0:T(8,128)(2,1)} async-done(((bf16[384,512]{1,0:T(8,128)(2,1)}), bf16[1536,512]{1,0:T(8,128)(2,1)}) %all-gather.5.cloned.1.call-update) | async-done | bytes 1572880 | tf_op jit(solution)/shard_map/all_gather | solution.py:117
  49.7 1.5 %collective-permute-start.1 = (f32[3,1536]{1,0:T(4,128)S(1)}, f32[3,1536]{1,0:T(4,128)S(1)}, u32[]{:S(2)}, u32[]{:S(2)}) collective-permute-start(f32[3,1536]{1,0:T(4,128)S(1)} %get-tuple-element.6), channel_id=1, source_target_pairs={{0,2},{2,0},{1,3},{3,1},{4,6},{6,4},{5,7},{7,5},{8,10},{10,8},{9,1... | collective-permute-start | bytes 55304 | tf_op jit(solution)/shard_map/ppermute | solution.py:151
  51.2 1.1 slice_bitcast_fusion
  52.3 1.3 %collective-permute-done.1 = f32[3,1536]{1,0:T(4,128)S(1)} collective-permute-done((f32[3,1536]{1,0:T(4,128)S(1)}, f32[3,1536]{1,0:T(4,128)S(1)}, u32[]{:S(2)}, u32[]{:S(2)}) %collective-permute-start.1) | collective-permute-done | bytes 18464 | tf_op jit(solution)/shard_map/ppermute | solution.py:151
  54.7 7.2 %all-gather.9.cloned.1.call-done = bf16[3072,512]{1,0:T(8,128)(2,1)} async-done(((bf16[1536,512]{1,0:T(8,128)(2,1)}), bf16[3072,512]{1,0:T(8,128)(2,1)}) %all-gather.9.cloned.1.call-update) | async-done | bytes 3145744 | tf_op jit(solution)/shard_map/all_gather | solution.py:149
  62.0 2.6 %fusion.157 = (f32[128]{0:T(128)S(1)}, f32[128,2,512]{2,0,1:T(8,128)S(1)}) fusion(bf16[2,1536,512]{2,1,0:T(8,128)(2,1)} %bitcast.62, bf16[125,1536]{1,0:T(8,128)(2,1)S(1)} %slice_bitcast_fusion, bf16[3,1536]{1,0:T(4,128)(2,1)S(1)} %add_convert_fusion), kind=kOutput, calls=%fused_computation.207 | convolution fusion | flops 403570560 | bytes 4063744 | tf_op jit(solution)/shard_map/nk,skc->nsc/dot_general | solution.py:85
  65.0 0.9 fusion.27
  66.9 30.5 %all-gather.7.cloned.1.call-done = bf16[512,1024]{0,1:T(8,128)(2,1)} async-done(((bf16[128,1024]{0,1:T(8,128)(2,1)}), bf16[512,1024]{0,1:T(8,128)(2,1)}) %all-gather.7.cloned.1.call-update) | async-done | bytes 1048592 | tf_op jit(solution)/shard_map/all_gather | solution.py:161
  97.4 2.2 %fusion.158 = f32[512,768]{0,1:T(8,128)S(1)} fusion(bf16[512,1024]{0,1:T(8,128)(2,1)} %all-gather.7.cloned.1.call-done, bf16[1024,768]{1,0:T(8,128)(2,1)S(1)} %copy-done), kind=kOutput, calls=%fused_computation.208 | convolution fusion | flops 805306368 | bytes 4194304 | tf_op jit(solution)/shard_map/dot_general | solution.py:163
  100.0 1.5 %convert_reduce_fusion = (f32[4,512]{1,0:T(4,128)S(1)}, bf16[4,512,512]{1,2,0:T(8,128)(2,1)S(1)}) fusion(f32[512,512]{0,1:T(8,128)S(1)} %abs_add_fusion, f32[4]{0:T(128)S(1)} %dynamic_slice.7, bf16[512,4,2,64]{0,3,1,2:T(8,128)(2,1)S(1)} %multiply_convert_fusion, pred[512]{0:T(512)(128)(4,1)S(1)} %iota_compare_fusion), kind=kOutput, calls=%fused_computation | convolution fusion | flops 141555712 | bytes 3678736 | tf_op jit(solution)/shard_map/qhd,khd->hqk/dot_general | solution.py:185
  102.8 3.8 %all-to-all-start = ((bf16[4,128,256]{1,2,0:T(8,128)(2,1)}), bf16[4,128,256]{1,2,0:T(8,128)(2,1)S(1)}, u32[]{:S(2)}, u32[]{:S(2)}) async-start(bf16[4,128,256]{1,2,0:T(8,128)(2,1)} %copy.36), calls=%async_computation | async-start | bytes 524288 | tf_op jit(solution)/shard_map/all_to_all | solution.py:195
  107.3 6.2 %all-to-all-done = bf16[4,128,256]{1,2,0:T(8,128)(2,1)S(1)} async-done(((bf16[4,128,256]{1,2,0:T(8,128)(2,1)}), bf16[4,128,256]{1,2,0:T(8,128)(2,1)S(1)}, u32[]{:S(2)}, u32[]{:S(2)}) %all-to-all-start) | async-done | bytes 262176 | tf_op jit(solution)/shard_map/all_to_all | solution.py:195
  (53 shorter events, 7.8 us)
Async XLA Ops:
  7.2 90.3 %copy-start = (bf16[1024,768]{1,0:T(8,128)(2,1)S(1)}, bf16[1024,768]{1,0:T(8,128)(2,1)}, u32[]{:S(2)}) copy-start(bf16[1024,768]{1,0:T(8,128)(2,1)} %param.34) | copy-start | bytes 4718596
  7.2 18.7 %copy-start.7 = (f32[1536]{0:T(1024)S(1)}, f32[1536]{0:T(1024)}, u32[]{:S(2)}) copy-start(f32[1536]{0:T(1024)} %param.25) | copy-start | bytes 18436
  7.2 42.2 %all-gather.5.cloned.1.call-start = ((), (), s32[]{:S(2)}) async-start(), calls=%async_computation.1 | async-start | bytes 1966080 | tf_op jit(solution)/shard_map/all_gather | solution.py:117
  9.2 52.8 %all-gather.9.cloned.1.call-start = ((), (), s32[]{:S(2)}) async-start(), calls=%async_computation.3 | async-start | bytes 4718592 | tf_op jit(solution)/shard_map/all_gather | solution.py:149
  22.9 13.3 %copy-start.1 = (bf16[1,3,49,1536]{3,2,1,0:T(8,128)(2,1)S(1)}, bf16[1,3,49,1536]{3,2,1,0:T(8,128)(2,1)}, u32[]{:S(2)}) copy-start(bf16[1,3,49,1536]{3,2,1,0:T(8,128)(2,1)} %param.19) | copy-start | bytes 1354756
  22.9 14.0 %copy-start.2 = (f32[1536]{0:T(1024)S(1)}, f32[1536]{0:T(1024)}, u32[]{:S(2)}) copy-start(f32[1536]{0:T(1024)} %param.28) | copy-start | bytes 18436
  22.9 14.0 %collective-permute-start = (bf16[147,1536]{1,0:T(8,128)(2,1)}, bf16[147,1536]{1,0:T(8,128)(2,1)}, u32[]{:S(2)}, u32[]{:S(2)}) collective-permute-start(bf16[147,1536]{1,0:T(8,128)(2,1)} %reshape.168), channel_id=1, source_target_pairs={{0,2},{2,0},{1,3},{3,1},{4,6},{6,4},{5,7},{7,5},{8,10},{10,8},{9,1... | collective-permute-start | bytes 1354760 | tf_op jit(solution)/shard_map/ppermute | solution.py:138
  44.6 20.4 %copy-start.5 = (f32[1024]{0:T(1024)S(1)}, f32[1024]{0:T(1024)}, u32[]{:S(2)}) copy-start(f32[1024]{0:T(1024)} %param.33) | copy-start | bytes 12292
  49.4 17.1 %copy-start.8 = (f32[16]{0:T(128)S(1)}, f32[16]{0:T(128)}, u32[]{:S(2)}) copy-start(f32[16]{0:T(128)} %param.35) | copy-start | bytes 196
  49.5 17.2 %copy-start.6 = (s32[1,2,512]{2,1,0:T(2,128)S(1)}, s32[1,2,512]{2,1,0:T(2,128)}, u32[]{:S(2)}) copy-start(s32[1,2,512]{2,1,0:T(2,128)} %param.36) | copy-start | bytes 12292
  49.5 48.0 %all-gather.7.cloned.1.call-start = ((), (), s32[]{:S(2)}) async-start(), calls=%async_computation.2 | async-start | bytes 1310720 | tf_op jit(solution)/shard_map/all_gather | solution.py:161
  49.7 3.9 %collective-permute-start.1 = (f32[3,1536]{1,0:T(4,128)S(1)}, f32[3,1536]{1,0:T(4,128)S(1)}, u32[]{:S(2)}, u32[]{:S(2)}) collective-permute-start(f32[3,1536]{1,0:T(4,128)S(1)} %get-tuple-element.6), channel_id=1, source_target_pairs={{0,2},{2,0},{1,3},{3,1},{4,6},{6,4},{5,7},{7,5},{8,10},{10,8},{9,1... | collective-permute-start | bytes 55304 | tf_op jit(solution)/shard_map/ppermute | solution.py:151
  101.5 5.1 %copy-start.3 = (f32[1536]{0:T(1024)S(1)}, f32[1536]{0:T(1024)}, u32[]{:S(2)}) copy-start(f32[1536]{0:T(1024)} %param.30) | copy-start | bytes 18436
  101.5 5.1 %copy-start.4 = (f32[1536]{0:T(1024)S(1)}, f32[1536]{0:T(1024)}, u32[]{:S(2)}) copy-start(f32[1536]{0:T(1024)} %param.29) | copy-start | bytes 18436
  102.8 10.7 %all-to-all-start = ((bf16[4,128,256]{1,2,0:T(8,128)(2,1)}), bf16[4,128,256]{1,2,0:T(8,128)(2,1)S(1)}, u32[]{:S(2)}, u32[]{:S(2)}) async-start(bf16[4,128,256]{1,2,0:T(8,128)(2,1)} %copy.36), calls=%async_computation | async-start | bytes 524288 | tf_op jit(solution)/shard_map/all_to_all | solution.py:195
Sparse Core Ops, SparseCore 0:
  9.6 39.7 all-gather.4
  51.0 10.9 all-gather.8
  66.0 31.3 all-gather.6

commit v6 on v5

--- a/solution.py
+++ b/solution.py
@@ -81,10 +81,32 @@
     return joined.astype(jnp.bfloat16).reshape(lead + (-1,))
 
 
+def line_gather(block, axis_name):
+    n = lax.axis_size(axis_name)
+    me = lax.axis_index(axis_name)
+    right = block
+    left = block
+    entries = [block]
+    for _ in range(1, n):
+        right = lax.ppermute(right, axis_name, [(j, j + 1) for j in range(n - 1)])
+        left = lax.ppermute(left, axis_name, [(j, j - 1) for j in range(1, n)])
+        entries += [right, left]
+    source = jnp.arange(n, dtype=jnp.int32)
+    pick = jnp.where(
+        source == me, 0, jnp.where(source < me, 2 * (me - source) - 1, 2 * (source - me))
+    )
+    return jnp.take(jnp.stack(entries), pick, axis=0)
+
+
 def project(rows, weight_parts, slide_gain):
-    projected = jnp.einsum(
-        "nk,skc->nsc", rows, weight_parts, preferred_element_type=jnp.float32
-    ).reshape(rows.shape[0], -1)
+    mine, other, first = weight_parts
+    mine_part = jnp.dot(rows, mine, preferred_element_type=jnp.float32)
+    other_part = jnp.dot(rows, other, preferred_element_type=jnp.float32)
+    projected = jnp.where(
+        first,
+        jnp.concatenate([mine_part, other_part], axis=-1),
+        jnp.concatenate([other_part, mine_part], axis=-1),
+    )
     return layer_norm(projected, slide_gain, 0.0, 1e-05).astype(jnp.bfloat16)
 
 
@@ -116,6 +138,8 @@
     )
     cols_full = lax.all_gather(my_cols, "slide", axis=0, tiled=True)
 
+    stored_all = line_gather(embed_store[0], "slide")
+
     tile_data = tile_features[0].astype(jnp.float32)
     fresh_count = tile_data.shape[0]
     n_rep = lax.axis_size("rep")
@@ -146,7 +170,11 @@
     cols_full, own_term, peer_terms = lax.optimization_barrier(
         (cols_full, own_term, peer_terms)
     )
-    weight_parts = lax.all_gather(cols_full, "section", axis=0, tiled=False)
+    other_cols = lax.ppermute(
+        cols_full, "section", perm=[(c, (c + 1) % n_sec) for c in range(n_sec)]
+    )
+    first = lax.axis_index("section") == 0
+    weight_parts = (cols_full, other_cols, first)
     returned = [
         lax.ppermute(term, "rep", perm=[(r, (r - k) % n_rep) for r in range(n_rep)])
         for k, term in enumerate(peer_terms, start=1)
@@ -156,9 +184,9 @@
         pooled = pooled + term
     embedded = layer_norm(pooled, head_gain, head_bias, 1e-06).astype(jnp.bfloat16)
 
-    seq_rows = jnp.concatenate([embedded, embed_store[0, fresh_count:]], axis=0)
-    normed_seq = project(seq_rows, weight_parts, slide_gain)
-    normed_all = lax.all_gather(normed_seq, "slide", axis=0, tiled=True)
+    embedded_all = lax.all_gather(embedded, "slide", axis=0, tiled=False)
+    seq_rows = jnp.concatenate([embedded_all, stored_all[:, fresh_count:]], axis=1)
+    normed_all = project(seq_rows.reshape(-1, seq_rows.shape[-1]), weight_parts, slide_gain)
     local_heads = normalize_heads(
         jnp.dot(normed_all, qkv_weight, preferred_element_type=jnp.float32)
     )

time: 122 us -> 127 us (1.041)
  waiting for transfers between devices: 49.3 us -> 8.13 us
  blocking collectives: 0 us -> 23.2 us
  starting transfers between devices: 8.59 us -> 21.8 us
  local copies, waits for them, and re-layouts: 14.3 us -> 24 us
  other arithmetic: 5.79 us -> 7.7 us
  matrix products: 22.6 us -> 21 us
    all_gather x2 -> x0, waiting for transfers between devices: 37.8 us -> none  [the longest x1 30.5 us: on_device(): normed_all = lax.all_gather(normed_seq, 'slide', axis=0, tiled=True)]
    ppermute x0 -> x7, starting transfers between devices: none -> 19.6 us  [the longest x3 15.8 us: line_gather(): right = lax.ppermute(right, axis_name, [(j, j + 1) for j in range(n - 1)])]
    all_gather x0 -> x1, blocking collectives: none -> 13.5 us  [on_device(): embedded_all = lax.all_gather(embedded, 'slide', axis=0, tiled=False)]
    unnamed x19 -> x47, local copies, waits for them, and re-layouts: 0.91 us -> 10.8 us
    all_to_all x0 -> x1, blocking collectives: none -> 9.67 us  [on_device(): lax.all_to_all(attended, 'slide', split_axis=0, concat_axis=1, tiled=True)]
    all_to_all x1 -> x0, waiting for transfers between devices: 6.2 us -> none  [on_device(): lax.all_to_all(attended, 'slide', split_axis=0, concat_axis=1, tiled=True)]
    ppermute x0 -> x7, waiting for transfers between devices: none -> 5.6 us  [the longest x3 3.27 us: line_gather(): left = lax.ppermute(left, axis_name, [(j, j - 1) for j in range(1, n)])]
    all_gather x1, waiting for transfers between devices: 4 us -> 0.02 us  [on_device(): cols_full = lax.all_gather(my_cols, 'slide', axis=0, tiled=True)]
  transfers between devices with their start and end apart: 6 -> 10, of which waited for: 5 -> 3; matrix products, arithmetic and copies ran while one was open for 25% -> 36% of each run, Pallas kernels for 5% -> 5%
where the time goes in v6:
time: 127 us
  local copies, waits for them, and re-layouts  24 us (19%)
  blocking collectives  23.2 us (18%)
  starting transfers between devices  21.8 us (17%)
  matrix products  21 us (17%)
  between operations  15 us (12%)
  waiting for transfers between devices  8.13 us (6%)
  other arithmetic  7.7 us (6%)
  Pallas kernels  5.74 us (5%)
    dot_general x2, matrix products, block_sums(): jnp.dot(hidden, down_weight, preferred_element_type=jnp.float32)  15.8 us
    ppermute x3, starting transfers between devices, line_gather(): right = lax.ppermute(right, axis_name, [(j, j + 1) for j in range(n - 1)])  15.8 us
    all_gather x1, blocking collectives, on_device(): embedded_all = lax.all_gather(embedded, 'slide', axis=0, tiled=False)  13.5 us
    unnamed x47, local copies, waits for them, and re-layouts  10.8 us
    all_to_all x1, blocking collectives, on_device(): lax.all_to_all(attended, 'slide', split_axis=0, concat_axis=1, tiled=True)  9.67 us
    pallas_call x1, Pallas kernels, dw_ln(): pl.pallas_call(dw_ln_kernel, grid=(T,), in_specs=[pl.BlockSpec((1, SIDE,...  5.74 us
    ppermute x3, starting transfers between devices, line_gather(): left = lax.ppermute(left, axis_name, [(j, j - 1) for j in range(1, n)])  3.85 us
    ppermute x3, waiting for transfers between devices, line_gather(): left = lax.ppermute(left, axis_name, [(j, j - 1) for j in range(1, n)])  3.27 us
  transfers between devices with their start and end apart: 10, of which 3 were waited for; matrix products, arithmetic and copies ran while one was open for 36% of the time, Pallas kernels for 5%

profile of v6, /device:TPU:0, one launch (start us, length us, event | category | flops | bytes accessed | tf_op | source)
XLA Modules:
  0.0 126.5 jit_solution(10666677133884387828)
XLA Ops:
  7.3 5.8 %collective-permute-start.2 = (bf16[128,1536]{1,0:T(8,128)(2,1)}, bf16[128,1536]{1,0:T(8,128)(2,1)}, u32[]{:S(2)}, u32[]{:S(2)}) collective-permute-start(bf16[128,1536]{1,0:T(8,128)(2,1)} %bitcast.71), channel_id=1, source_target_pairs={{0,4},{4,8},{8,12},{1,5},{5,9},{9,13},{2,6},{6,10},{10,14},{3,7},{... | collective-permute-start | bytes 1179656 | tf_op jit(solution)/shard_map/ppermute | solution.py:91
  13.1 1.3 %collective-permute-start.3 = (bf16[128,1536]{1,0:T(8,128)(2,1)}, bf16[128,1536]{1,0:T(8,128)(2,1)}, u32[]{:S(2)}, u32[]{:S(2)}) collective-permute-start(bf16[128,1536]{1,0:T(8,128)(2,1)} %bitcast.72), channel_id=1, source_target_pairs={{4,0},{8,4},{12,8},{5,1},{9,5},{13,9},{6,2},{10,6},{14,10},{7,3},{... | collective-permute-start | bytes 1179656 | tf_op jit(solution)/shard_map/ppermute | solution.py:92
  14.4 1.8 %constant_dynamic-slice_fusion = bf16[384,512]{1,0:T(8,128)(2,1)} fusion(bf16[384,1024]{1,0:T(8,128)(2,1)} %param.32, s32[]{:T(128)S(6)} %select_n.79), kind=kLoop, calls=%fused_computation.162 | loop fusion | bytes 786436 | tf_op jit(solution)/shard_map/dynamic_slice | solution.py:136
  20.1 5.7 %shard_map.194 = bf16[3,7,8,1536]{3,2,1,0:T(8,128)(2,1)} custom-call(bf16[3,7,8,1536]{3,2,1,0:T(8,128)(2,1)} %pad.4.x_ref, f32[49,1536]{1,0:T(8,128)} %w_ref.1, f32[1,1536]{1,0:T(1,128)} %broadcast_in_dim.90.b_ref, f32[1,1536]{1,0:T(1,128)} %broadcast_in_dim.91.g_ref, f32[1,1536]{1,0:T(1,128)} %broadcast_in_dim.92.nb_ref), custom_call_target="tpu_custom_call" | custom-call | tf_op jit(solution)/shard_map/pallas_call | solution.py:58
  25.9 2.0 %reshape.217 = bf16[147,1536]{1,0:T(8,128)(2,1)} reshape(bf16[3,7,7,1536]{3,2,1,0:T(8,128)(2,1)} %bitcast.67) | data formatting | bytes 903168 | tf_op jit(solution)/shard_map/reshape | solution.py:72
  27.9 1.5 %collective-permute-start = (bf16[147,1536]{1,0:T(8,128)(2,1)}, bf16[147,1536]{1,0:T(8,128)(2,1)}, u32[]{:S(2)}, u32[]{:S(2)}) collective-permute-start(bf16[147,1536]{1,0:T(8,128)(2,1)} %reshape.217), channel_id=1, source_target_pairs={{0,2},{2,0},{1,3},{3,1},{4,6},{6,4},{5,7},{7,5},{8,10},{10,8},{9,1... | collective-permute-start | bytes 1354760 | tf_op jit(solution)/shard_map/ppermute | solution.py:162
  32.0 8.4 %fusion.1 = f32[147,1536]{1,0:T(8,128)} fusion(bf16[1536,1536]{1,0:T(8,128)(2,1)} %param.26, bf16[147,1536]{1,0:T(8,128)(2,1)} %reshape.217, bf16[1536,1536]{1,0:T(8,128)(2,1)} %param.24, f32[1536]{0:T(1024)S(1)} %copy-done.15), kind=kOutput, calls=%fused_computation.8 | convolution fusion | flops 1402619904 | bytes 10798080 | tf_op jit(solution)/shard_map/dot_general | solution.py:156
  41.0 1.3 %reshape.225 = f32[3,49,1536]{2,1,0:T(8,128)S(1)} reshape(f32[147,1536]{1,0:T(8,128)} %fusion.1) | data formatting | bytes 1806336 | tf_op jit(solution)/shard_map/reshape | solution.py:159
  45.5 5.3 %collective-permute-start.4 = (bf16[128,1536]{1,0:T(8,128)(2,1)}, bf16[128,1536]{1,0:T(8,128)(2,1)}, u32[]{:S(2)}, u32[]{:S(2)}) collective-permute-start(bf16[128,1536]{1,0:T(8,128)(2,1)} %collective-permute-done.2), channel_id=1, source_target_pairs={{0,4},{4,8},{8,12},{1,5},{5,9},{9,13},{2,6},{6,10},{10,14},{3,7},{... | collective-permute-start | bytes 1179656 | tf_op jit(solution)/shard_map/ppermute | solution.py:91
  50.9 1.8 %bitcast_dynamic-update-slice_fusion.5 = bf16[7,128,1536]{2,1,0:T(8,128)(2,1)} fusion(bf16[7,128,1536]{2,1,0:T(8,128)(2,1)} %constant_dynamic-update-slice_fusion, bf16[128,1536]{1,0:T(8,128)(2,1)} %collective-permute-done.2), kind=kLoop, calls=%fused_computation.132 | loop fusion | bytes 786432
  52.6 1.3 %collective-permute-start.5 = (bf16[128,1536]{1,0:T(8,128)(2,1)}, bf16[128,1536]{1,0:T(8,128)(2,1)}, u32[]{:S(2)}, u32[]{:S(2)}) collective-permute-start(bf16[128,1536]{1,0:T(8,128)(2,1)} %collective-permute-done.3), channel_id=1, source_target_pairs={{4,0},{8,4},{12,8},{5,1},{9,5},{13,9},{6,2},{10,6},{14,10},{7,3},{... | collective-permute-start | bytes 1179656 | tf_op jit(solution)/shard_map/ppermute | solution.py:92
  53.9 1.8 %bitcast_dynamic-update-slice_fusion.4 = bf16[7,128,1536]{2,1,0:T(8,128)(2,1)} fusion(bf16[7,128,1536]{2,1,0:T(8,128)(2,1)} %bitcast_dynamic-update-slice_fusion.5, bf16[128,1536]{1,0:T(8,128)(2,1)} %collective-permute-done.3), kind=kLoop, calls=%fused_computation.131 | loop fusion | bytes 786432
  55.7 7.4 %fusion = f32[147,1536]{1,0:T(8,128)S(1)} fusion(bf16[1536,1536]{1,0:T(8,128)(2,1)} %param.26, bf16[147,1536]{1,0:T(8,128)(2,1)} %collective-permute-done, bf16[1536,1536]{1,0:T(8,128)(2,1)} %param.24, f32[1536]{0:T(1024)S(1)} %copy-done.16), kind=kOutput, calls=%fused_computation.6 | convolution fusion | flops 1402619904 | bytes 10798080 | tf_op jit(solution)/shard_map/dot_general | solution.py:156
  64.1 4.6 %collective-permute-start.6 = (bf16[128,1536]{1,0:T(8,128)(2,1)}, bf16[128,1536]{1,0:T(8,128)(2,1)S(1)}, u32[]{:S(2)}, u32[]{:S(2)}) collective-permute-start(bf16[128,1536]{1,0:T(8,128)(2,1)} %collective-permute-done.4), channel_id=1, source_target_pairs={{0,4},{4,8},{8,12},{1,5},{5,9},{9,13},{2,6},{6,10},{10,14},{3,7},{... | collective-permute-start | bytes 1179656 | tf_op jit(solution)/shard_map/ppermute | solution.py:91
  68.7 1.3 %collective-permute-start.7 = (bf16[128,1536]{1,0:T(8,128)(2,1)}, bf16[128,1536]{1,0:T(8,128)(2,1)S(1)}, u32[]{:S(2)}, u32[]{:S(2)}) collective-permute-start(bf16[128,1536]{1,0:T(8,128)(2,1)} %collective-permute-done.5), channel_id=1, source_target_pairs={{4,0},{8,4},{12,8},{5,1},{9,5},{13,9},{6,2},{10,6},{14,10},{7,3},{... | collective-permute-start | bytes 1179656 | tf_op jit(solution)/shard_map/ppermute | solution.py:92
  70.0 1.8 %bitcast_dynamic-update-slice_fusion.3 = bf16[7,128,1536]{2,1,0:T(8,128)(2,1)} fusion(bf16[7,128,1536]{2,1,0:T(8,128)(2,1)} %bitcast_dynamic-update-slice_fusion.4, bf16[128,1536]{1,0:T(8,128)(2,1)} %collective-permute-done.4), kind=kLoop, calls=%fused_computation.130 | loop fusion | bytes 786432
  71.8 1.8 %bitcast_dynamic-update-slice_fusion.2 = bf16[7,128,1536]{2,1,0:T(8,128)(2,1)} fusion(bf16[7,128,1536]{2,1,0:T(8,128)(2,1)} %bitcast_dynamic-update-slice_fusion.3, bf16[128,1536]{1,0:T(8,128)(2,1)} %collective-permute-done.5), kind=kLoop, calls=%fused_computation.129 | loop fusion | bytes 786432
  73.6 2.3 %collective-permute-done.6 = bf16[128,1536]{1,0:T(8,128)(2,1)S(1)} collective-permute-done((bf16[128,1536]{1,0:T(8,128)(2,1)}, bf16[128,1536]{1,0:T(8,128)(2,1)S(1)}, u32[]{:S(2)}, u32[]{:S(2)}) %collective-permute-start.6) | collective-permute-done | bytes 393248 | tf_op jit(solution)/shard_map/ppermute | solution.py:91
  76.7 3.3 %collective-permute-done.7 = bf16[128,1536]{1,0:T(8,128)(2,1)S(1)} collective-permute-done((bf16[128,1536]{1,0:T(8,128)(2,1)}, bf16[128,1536]{1,0:T(8,128)(2,1)S(1)}, u32[]{:S(2)}, u32[]{:S(2)}) %collective-permute-start.7) | collective-permute-done | bytes 393248 | tf_op jit(solution)/shard_map/ppermute | solution.py:92
  80.7 2.5 %gather_fusion = bf16[4,128,1536]{2,1,0:T(8,128)(2,1)S(1)} fusion(bf16[7,128,1536]{2,1,0:T(8,128)(2,1)} %bitcast_dynamic-update-slice_fusion, s32[1024]{0:T(1024)} %pad_clamp_fusion), kind=kCustom, calls=%fused_computation | custom fusion | bytes 3145744 | tf_op jit(solution)/shard_map/jit(_take)/gather | solution.py:98
  84.8 2.5 %collective-permute-done.1 = f32[3,1536]{1,0:T(4,128)S(1)} collective-permute-done((f32[3,1536]{1,0:T(4,128)S(1)}, f32[3,1536]{1,0:T(4,128)S(1)}, u32[]{:S(2)}, u32[]{:S(2)}) %collective-permute-start.1) | collective-permute-done | bytes 18464 | tf_op jit(solution)/shard_map/ppermute | solution.py:179
  87.7 13.5 %all-gather.1 = bf16[4,3,1536]{2,1,0:T(4,128)(2,1)S(1)} all-gather(bf16[1,3,1536]{2,1,0:T(4,128)(2,1)S(1)} %fusion.94), channel_id=2, replica_groups=mesh['groups'=2,'slide'=4,'rep'=2,'section'=2] {'slide'}, dimensions={0}, use_global_device_ids=true | all-gather | bytes 46080 | tf_op jit(solution)/shard_map/all_gather | solution.py:187
  107.1 1.5 %convert_reduce_fusion = (f32[4,512]{1,0:T(4,128)S(1)}, bf16[4,512,512]{1,2,0:T(8,128)(2,1)S(1)}) fusion(f32[512,512]{0,1:T(8,128)S(1)} %copy-done.2, f32[4]{0:T(128)S(1)} %copy-done.19, bf16[512,4,2,64]{0,3,1,2:T(8,128)(2,1)S(1)} %multiply_convert_fusion.2, pred[512]{0:T(512)(128)(4,1)S(1)} %copy-done.12), kind=kOutput, calls=%fused_computation.1 | convolution fusion | flops 141555712 | bytes 3678736 | tf_op jit(solution)/shard_map/qhd,khd->hqk/dot_general | solution.py:213
  109.2 9.7 %all_to_all.16 = bf16[4,128,256]{1,2,0:T(8,128)(2,1)S(1)} all-to-all(bf16[4,128,256]{1,2,0:T(8,128)(2,1)S(1)} %copy.34), channel_id=1, replica_groups=mesh['groups'=2,'slide'=4,'rep'=2,'section'=2] {'slide'}, dimensions={0} | all-to-all | bytes 524288 | tf_op jit(solution)/shard_map/all_to_all | solution.py:223
  (94 shorter events, 21.4 us)
Async XLA Ops:
  7.2 97.4 %copy-start = (bf16[1024,768]{1,0:T(8,128)(2,1)S(1)}, bf16[1024,768]{1,0:T(8,128)(2,1)}, u32[]{:S(2)}) copy-start(bf16[1024,768]{1,0:T(8,128)(2,1)} %param.34) | copy-start | bytes 4718596
  7.2 10.3 %copy-start.6 = (f32[1536]{0:T(1024)S(1)}, f32[1536]{0:T(1024)}, u32[]{:S(2)}) copy-start(f32[1536]{0:T(1024)} %param.21) | copy-start | bytes 18436
  7.2 10.9 %copy-start.7 = (f32[1536]{0:T(1024)S(1)}, f32[1536]{0:T(1024)}, u32[]{:S(2)}) copy-start(f32[1536]{0:T(1024)} %param.22) | copy-start | bytes 18436
  7.2 11.5 %copy-start.8 = (f32[1536]{0:T(1024)S(1)}, f32[1536]{0:T(1024)}, u32[]{:S(2)}) copy-start(f32[1536]{0:T(1024)} %param.23) | copy-start | bytes 18436
  7.2 76.1 %all-gather.4.cloned.1.call-start = ((), (), s32[]{:S(2)}) async-start(), calls=%async_computation.1 | async-start | bytes 1966080 | tf_op jit(solution)/shard_map/all_gather | solution.py:139
  7.3 38.3 %collective-permute-start.2 = (bf16[128,1536]{1,0:T(8,128)(2,1)}, bf16[128,1536]{1,0:T(8,128)(2,1)}, u32[]{:S(2)}, u32[]{:S(2)}) collective-permute-start(bf16[128,1536]{1,0:T(8,128)(2,1)} %bitcast.71), channel_id=1, source_target_pairs={{0,4},{4,8},{8,12},{1,5},{5,9},{9,13},{2,6},{6,10},{10,14},{3,7},{... | collective-permute-start | bytes 1179656 | tf_op jit(solution)/shard_map/ppermute | solution.py:91
  13.1 39.5 %collective-permute-start.3 = (bf16[128,1536]{1,0:T(8,128)(2,1)}, bf16[128,1536]{1,0:T(8,128)(2,1)}, u32[]{:S(2)}, u32[]{:S(2)}) collective-permute-start(bf16[128,1536]{1,0:T(8,128)(2,1)} %bitcast.72), channel_id=1, source_target_pairs={{4,0},{8,4},{12,8},{5,1},{9,5},{13,9},{6,2},{10,6},{14,10},{7,3},{... | collective-permute-start | bytes 1179656 | tf_op jit(solution)/shard_map/ppermute | solution.py:92
  16.2 13.2 %copy-start.3 = (bf16[1,128,1536]{2,1,0:T(8,128)(2,1)S(1)}, bf16[1,128,1536]{2,1,0:T(8,128)(2,1)}, u32[]{:S(2)}) copy-start(bf16[1,128,1536]{2,1,0:T(8,128)(2,1)} %param.31) | copy-start | bytes 1179652
  19.3 11.5 %copy-start.5 = (f32[1536]{0:T(1024)S(1)}, f32[1536]{0:T(1024)}, u32[]{:S(2)}) copy-start(f32[1536]{0:T(1024)} %param.28) | copy-start | bytes 18436
  19.3 12.1 %copy-start.11 = (s32[1,2,512]{2,1,0:T(2,128)S(1)}, s32[1,2,512]{2,1,0:T(2,128)}, u32[]{:S(2)}) copy-start(s32[1,2,512]{2,1,0:T(2,128)} %param.36) | copy-start | bytes 12292
  19.3 12.8 %copy-start.15 = (f32[1536]{0:T(1024)S(1)}, f32[1536]{0:T(1024)}, u32[]{:S(2)}) copy-start(f32[1536]{0:T(1024)} %param.25) | copy-start | bytes 18436
  27.9 27.8 %collective-permute-start = (bf16[147,1536]{1,0:T(8,128)(2,1)}, bf16[147,1536]{1,0:T(8,128)(2,1)}, u32[]{:S(2)}, u32[]{:S(2)}) collective-permute-start(bf16[147,1536]{1,0:T(8,128)(2,1)} %reshape.217), channel_id=1, source_target_pairs={{0,2},{2,0},{1,3},{3,1},{4,6},{6,4},{5,7},{7,5},{8,10},{10,8},{9,1... | collective-permute-start | bytes 1354760 | tf_op jit(solution)/shard_map/ppermute | solution.py:162
  40.4 3.2 %copy-start.1 = (bf16[1,3,49,1536]{3,2,1,0:T(8,128)(2,1)S(1)}, bf16[1,3,49,1536]{3,2,1,0:T(8,128)(2,1)}, u32[]{:S(2)}) copy-start(bf16[1,3,49,1536]{3,2,1,0:T(8,128)(2,1)} %param.19) | copy-start | bytes 1354756
  43.0 12.7 %copy-start.16 = (f32[1536]{0:T(1024)S(1)}, f32[1536]{0:T(1024)}, u32[]{:S(2)}) copy-start(f32[1536]{0:T(1024)} %param.25) | copy-start | bytes 18436
  45.5 18.6 %collective-permute-start.4 = (bf16[128,1536]{1,0:T(8,128)(2,1)}, bf16[128,1536]{1,0:T(8,128)(2,1)}, u32[]{:S(2)}, u32[]{:S(2)}) collective-permute-start(bf16[128,1536]{1,0:T(8,128)(2,1)} %collective-permute-done.2), channel_id=1, source_target_pairs={{0,4},{4,8},{8,12},{1,5},{5,9},{9,13},{2,6},{6,10},{10,14},{3,7},{... | collective-permute-start | bytes 1179656 | tf_op jit(solution)/shard_map/ppermute | solution.py:91
  52.6 16.1 %collective-permute-start.5 = (bf16[128,1536]{1,0:T(8,128)(2,1)}, bf16[128,1536]{1,0:T(8,128)(2,1)}, u32[]{:S(2)}, u32[]{:S(2)}) collective-permute-start(bf16[128,1536]{1,0:T(8,128)(2,1)} %collective-permute-done.3), channel_id=1, source_target_pairs={{4,0},{8,4},{12,8},{5,1},{9,5},{13,9},{6,2},{10,6},{14,10},{7,3},{... | collective-permute-start | bytes 1179656 | tf_op jit(solution)/shard_map/ppermute | solution.py:92
  64.1 11.8 %collective-permute-start.6 = (bf16[128,1536]{1,0:T(8,128)(2,1)}, bf16[128,1536]{1,0:T(8,128)(2,1)S(1)}, u32[]{:S(2)}, u32[]{:S(2)}) collective-permute-start(bf16[128,1536]{1,0:T(8,128)(2,1)} %collective-permute-done.4), channel_id=1, source_target_pairs={{0,4},{4,8},{8,12},{1,5},{5,9},{9,13},{2,6},{6,10},{10,14},{3,7},{... | collective-permute-start | bytes 1179656 | tf_op jit(solution)/shard_map/ppermute | solution.py:91
  68.7 11.2 %collective-permute-start.7 = (bf16[128,1536]{1,0:T(8,128)(2,1)}, bf16[128,1536]{1,0:T(8,128)(2,1)S(1)}, u32[]{:S(2)}, u32[]{:S(2)}) collective-permute-start(bf16[128,1536]{1,0:T(8,128)(2,1)} %collective-permute-done.5), channel_id=1, source_target_pairs={{4,0},{8,4},{12,8},{5,1},{9,5},{13,9},{6,2},{10,6},{14,10},{7,3},{... | collective-permute-start | bytes 1179656 | tf_op jit(solution)/shard_map/ppermute | solution.py:92
  76.7 7.3 %copy-start.13 = (pred[4]{0:T(512)(128)(4,1)S(1)}, pred[4]{0:T(512)(128)(4,1)}, u32[]{:S(2)}) copy-start(pred[4]{0:T(512)(128)(4,1)} %compare_and_fusion) | copy-start | bytes 16
  83.3 4.3 %copy-start.9 = (f32[1536]{0:T(1024)S(1)}, f32[1536]{0:T(1024)}, u32[]{:S(2)}) copy-start(f32[1536]{0:T(1024)} %param.30) | copy-start | bytes 18436
  83.3 4.3 %copy-start.10 = (f32[1536]{0:T(1024)S(1)}, f32[1536]{0:T(1024)}, u32[]{:S(2)}) copy-start(f32[1536]{0:T(1024)} %param.29) | copy-start | bytes 18436
  83.4 3.9 %collective-permute-start.1 = (f32[3,1536]{1,0:T(4,128)S(1)}, f32[3,1536]{1,0:T(4,128)S(1)}, u32[]{:S(2)}, u32[]{:S(2)}) collective-permute-start(f32[3,1536]{1,0:T(4,128)S(1)} %get-tuple-element.6), channel_id=1, source_target_pairs={{0,2},{2,0},{1,3},{3,1},{4,6},{6,4},{5,7},{7,5},{8,10},{10,8},{9,1... | collective-permute-start | bytes 55304 | tf_op jit(solution)/shard_map/ppermute | solution.py:179
  84.8 17.9 %collective-permute-start.8 = (bf16[1536,512]{1,0:T(8,128)(2,1)S(1)}, bf16[1536,512]{1,0:T(8,128)(2,1)S(1)}, u32[]{:S(2)}, u32[]{:S(2)}) collective-permute-start(bf16[1536,512]{1,0:T(8,128)(2,1)S(1)} %copy-done.14), channel_id=1, source_target_pairs={{0,1},{1,0},{2,3},{3,2},{4,5},{5,4},{6,7},{7,6},{8,9},{9,8},{10,11... | collective-permute-start | bytes 4718600 | tf_op jit(solution)/shard_map/ppermute | solution.py:173
  87.7 14.9 %copy-start.4 = (bf16[1,3,1536]{2,1,0:T(4,128)(2,1)}, bf16[1,3,1536]{2,1,0:T(4,128)(2,1)S(1)}, u32[]{:S(2)}) copy-start(bf16[1,3,1536]{2,1,0:T(4,128)(2,1)S(1)} %fusion.94) | copy-start | bytes 27652
  (6 other events, 8.5 us)
Sparse Core Ops, SparseCore 0:
  16.3 39.3 all-gather.3

commit v7 on v5

--- a/solution.py
+++ b/solution.py
@@ -82,9 +82,14 @@
 
 
 def project(rows, weight_parts, slide_gain):
-    projected = jnp.einsum(
-        "nk,skc->nsc", rows, weight_parts, preferred_element_type=jnp.float32
-    ).reshape(rows.shape[0], -1)
+    mine, other, first = weight_parts
+    mine_part = jnp.dot(rows, mine, preferred_element_type=jnp.float32)
+    other_part = jnp.dot(rows, other, preferred_element_type=jnp.float32)
+    projected = jnp.where(
+        first,
+        jnp.concatenate([mine_part, other_part], axis=-1),
+        jnp.concatenate([other_part, mine_part], axis=-1),
+    )
     return layer_norm(projected, slide_gain, 0.0, 1e-05).astype(jnp.bfloat16)
 
 
@@ -146,7 +151,11 @@
     cols_full, own_term, peer_terms = lax.optimization_barrier(
         (cols_full, own_term, peer_terms)
     )
-    weight_parts = lax.all_gather(cols_full, "section", axis=0, tiled=False)
+    other_cols = lax.ppermute(
+        cols_full, "section", perm=[(c, (c + 1) % n_sec) for c in range(n_sec)]
+    )
+    first = lax.axis_index("section") == 0
+    weight_parts = (cols_full, other_cols, first)
     returned = [
         lax.ppermute(term, "rep", perm=[(r, (r - k) % n_rep) for r in range(n_rep)])
         for k, term in enumerate(peer_terms, start=1)

time: 122 us -> 113 us (0.926)
  waiting for transfers between devices: 49.3 us -> 38.7 us
  other arithmetic: 5.79 us -> 7.19 us
    all_gather x1 -> x0, waiting for transfers between devices: 7.25 us -> none  [on_device(): weight_parts = lax.all_gather(cols_full, 'section', axis=0, tiled=False)]
    all_gather x1, waiting for transfers between devices: 30.5 us -> 25.3 us  [on_device(): normed_all = lax.all_gather(normed_seq, 'slide', axis=0, tiled=True)]
    all_to_all x1, waiting for transfers between devices: 6.2 us -> 8.32 us  [on_device(): lax.all_to_all(attended, 'slide', split_axis=0, concat_axis=1, tiled=True)]
    dot_general x1 -> x2, matrix products: 2.56 us -> 2.15 us  [the longest x1 1.78 us: project(): mine_part = jnp.dot(rows, mine, preferred_element_type=jnp.float32)]
  transfers between devices with their start and end apart: 6 -> 6, of which waited for: 5 -> 4; matrix products, arithmetic and copies ran while one was open for 25% -> 31% of each run, Pallas kernels for 5% -> 5%
where the time goes in v7:
time: 113 us; the launch traced here: 112 us
  waiting for transfers between devices  38.7 us (34%)
  matrix products  22.2 us (20%)
  local copies, waits for them, and re-layouts  15.1 us (13%)
  between operations  14.9 us (13%)
  starting transfers between devices  7.9 us (7%)
  other arithmetic  7.19 us (6%)
  Pallas kernels  5.74 us (5%)
    all_gather x1, waiting for transfers between devices, on_device(): normed_all = lax.all_gather(normed_seq, 'slide', axis=0, tiled=True)  25.3 us
    dot_general x2, matrix products, block_sums(): jnp.dot(hidden, down_weight, preferred_element_type=jnp.float32)  15.8 us
    all_to_all x1, waiting for transfers between devices, on_device(): lax.all_to_all(attended, 'slide', split_axis=0, concat_axis=1, tiled=True)  8.32 us
    pallas_call x1, Pallas kernels, dw_ln(): pl.pallas_call(dw_ln_kernel, grid=(T,), in_specs=[pl.BlockSpec((1, SIDE,...  5.74 us
    all_gather x1, waiting for transfers between devices, on_device(): cols_full = lax.all_gather(my_cols, 'slide', axis=0, tiled=True)  3.44 us
    all_to_all x1, starting transfers between devices, on_device(): lax.all_to_all(attended, 'slide', split_axis=0, concat_axis=1, tiled=True)  3.41 us
    ppermute x1, starting transfers between devices, on_device(): lax.ppermute(normed, 'rep', perm=[(r, (r + k) % n_rep) for r in range(n_r...  2.94 us
  transfers between devices with their start and end apart: 6, of which 4 were waited for; matrix products, arithmetic and copies ran while one was open for 31% of the time, Pallas kernels for 5%

profile of v7, /device:TPU:0, one launch (start us, length us, event | category | flops | bytes accessed | tf_op | source)
XLA Modules:
  0.0 111.7 jit_solution(14879873486658185746)
XLA Ops:
  7.2 1.9 %constant_dynamic-slice_fusion = bf16[384,512]{1,0:T(8,128)(2,1)} fusion(bf16[384,1024]{1,0:T(8,128)(2,1)} %param.32, s32[]{:T(128)S(6)} %select_n.30), kind=kLoop, calls=%fused_computation.142 | loop fusion | bytes 786436 | tf_op jit(solution)/shard_map/dynamic_slice | solution.py:119
  9.2 1.3 %broadcast_in_dim.42.b_ref = f32[1,1536]{1,0:T(1,128)} reshape(f32[1536]{0:T(1024)} %param.21) | data formatting | bytes 12288 | tf_op jit(solution)/shard_map/broadcast_in_dim | solution.py:71
  10.5 1.3 %broadcast_in_dim.43.g_ref = f32[1,1536]{1,0:T(1,128)} reshape(f32[1536]{0:T(1024)} %param.22) | data formatting | bytes 12288 | tf_op jit(solution)/shard_map/broadcast_in_dim | solution.py:71
  11.8 1.3 %broadcast_in_dim.44.nb_ref = f32[1,1536]{1,0:T(1,128)} reshape(f32[1536]{0:T(1024)} %param.23) | data formatting | bytes 12288 | tf_op jit(solution)/shard_map/broadcast_in_dim | solution.py:71
  13.1 1.2 %reshape_squeeze.3 = bf16[3,7,7,1536]{3,2,1,0:T(8,128)(2,1)S(1)} reshape(bf16[1,3,49,1536]{3,2,1,0:T(8,128)(2,1)} %param.19) | data formatting | bytes 903168 | tf_op jit(solution)/shard_map/reshape;squeeze | solution.py:57
  14.3 0.9 pad.4.x_ref
  15.2 5.7 %shard_map.194 = bf16[3,7,8,1536]{3,2,1,0:T(8,128)(2,1)} custom-call(bf16[3,7,8,1536]{3,2,1,0:T(8,128)(2,1)} %pad.4.x_ref, f32[49,1536]{1,0:T(8,128)} %w_ref.1, f32[1,1536]{1,0:T(1,128)} %broadcast_in_dim.42.b_ref, f32[1,1536]{1,0:T(1,128)} %broadcast_in_dim.43.g_ref, f32[1,1536]{1,0:T(1,128)} %broadcast_in_dim.44.nb_ref), custom_call_target="tpu_custom_call" | custom-call | tf_op jit(solution)/shard_map/pallas_call | solution.py:58
  20.9 2.0 %reshape.160 = bf16[147,1536]{1,0:T(8,128)(2,1)} reshape(bf16[3,7,7,1536]{3,2,1,0:T(8,128)(2,1)} %bitcast.52) | data formatting | bytes 903168 | tf_op jit(solution)/shard_map/reshape | solution.py:72
  22.9 2.9 %collective-permute-start = (bf16[147,1536]{1,0:T(8,128)(2,1)}, bf16[147,1536]{1,0:T(8,128)(2,1)}, u32[]{:S(2)}, u32[]{:S(2)}) collective-permute-start(bf16[147,1536]{1,0:T(8,128)(2,1)} %reshape.160), channel_id=1, source_target_pairs={{0,2},{2,0},{1,3},{3,1},{4,6},{6,4},{5,7},{7,5},{8,10},{10,8},{9,1... | collective-permute-start | bytes 1354760 | tf_op jit(solution)/shard_map/ppermute | solution.py:143
  25.8 8.4 %fusion.1 = f32[147,1536]{1,0:T(8,128)} fusion(bf16[1536,1536]{1,0:T(8,128)(2,1)} %param.26, bf16[147,1536]{1,0:T(8,128)(2,1)} %reshape.160, bf16[1536,1536]{1,0:T(8,128)(2,1)} %param.24, f32[1536]{0:T(1024)S(1)} %copy-done.9), kind=kOutput, calls=%fused_computation.7 | convolution fusion | flops 1402619904 | bytes 10798080 | tf_op jit(solution)/shard_map/dot_general | solution.py:137
  34.2 1.3 %reshape.167 = f32[3,49,1536]{2,1,0:T(8,128)S(1)} reshape(f32[147,1536]{1,0:T(8,128)} %fusion.1) | data formatting | bytes 1806336 | tf_op jit(solution)/shard_map/reshape | solution.py:140
  36.9 7.5 %fusion = f32[147,1536]{1,0:T(8,128)S(1)} fusion(bf16[1536,1536]{1,0:T(8,128)(2,1)} %param.26, bf16[147,1536]{1,0:T(8,128)(2,1)} %collective-permute-done, bf16[1536,1536]{1,0:T(8,128)(2,1)} %param.24, f32[1536]{0:T(1024)} %param.25), kind=kOutput, calls=%fused_computation.5 | convolution fusion | flops 1402619904 | bytes 10798080 | tf_op jit(solution)/shard_map/dot_general | solution.py:137
  44.6 1.4 %multiply_add_fusion = (f32[3,1536]{1,0:T(4,128)}, f32[3,1536]{1,0:T(4,128)}) fusion(f32[3,1536]{1,0:T(4,128)} %reduce_sum.82, f32[3,1536]{1,0:T(4,128)} %convert_reduce_fusion.1, f32[1536]{0:T(1024)} %param.27, f32[1536]{0:T(1024)S(1)} %copy-done.4, f32[3,1536]{1,0:T(4,128)S(1)} %reduce_sum.83, f32[1536]{0:T(1024)S(1)} %broadcast_multiply_fusion.1), kind=kLoop, calls=%fused_computation.130 | loop fusion | flops 27648 | bytes 110592 | tf_op jit(solution)/shard_map/add | solution.py:147
  46.0 3.4 %all-gather.3.cloned.1.call-done = bf16[1536,512]{1,0:T(8,128)(2,1)} async-done(((bf16[384,512]{1,0:T(8,128)(2,1)}), bf16[1536,512]{1,0:T(8,128)(2,1)}) %all-gather.3.cloned.1.call-update) | async-done | bytes 1572880 | tf_op jit(solution)/shard_map/all_gather | solution.py:122
  49.4 1.5 %collective-permute-start.1 = (f32[3,1536]{1,0:T(4,128)}, f32[3,1536]{1,0:T(4,128)}, u32[]{:S(2)}, u32[]{:S(2)}) collective-permute-start(f32[3,1536]{1,0:T(4,128)} %get-tuple-element.6), channel_id=1, source_target_pairs={{0,2},{2,0},{1,3},{3,1},{4,6},{6,4},{5,7},{7,5},{8,10},{10,8},{9,1... | collective-permute-start | bytes 55304 | tf_op jit(solution)/shard_map/ppermute | solution.py:160
  50.9 1.1 slice_bitcast_fusion
  52.0 1.6 %collective-permute-done.1 = f32[3,1536]{1,0:T(4,128)} collective-permute-done((f32[3,1536]{1,0:T(4,128)}, f32[3,1536]{1,0:T(4,128)}, u32[]{:S(2)}, u32[]{:S(2)}) %collective-permute-start.1) | collective-permute-done | bytes 18464 | tf_op jit(solution)/shard_map/ppermute | solution.py:160
  53.6 0.9 fusion.154
  55.8 1.8 %fusion.90 = f32[128,512]{1,0:T(8,128)S(1)} fusion(bf16[1536,512]{1,0:T(8,128)(2,1)} %all-gather.3.cloned.1.call-done, bf16[125,1536]{1,0:T(8,128)(2,1)S(1)} %slice_bitcast_fusion, bf16[3,1536]{1,0:T(4,128)(2,1)S(1)} %add_convert_fusion), kind=kOutput, calls=%fused_computation.126 | convolution fusion | flops 202113024 | bytes 2228224 | tf_op jit(solution)/shard_map/dot_general | solution.py:86
  60.9 25.3 %all-gather.5.cloned.1.call-done = bf16[512,1024]{1,0:T(8,128)(2,1)} async-done(((bf16[128,1024]{1,0:T(8,128)(2,1)}), bf16[512,1024]{1,0:T(8,128)(2,1)}) %all-gather.5.cloned.1.call-update) | async-done | bytes 1048592 | tf_op jit(solution)/shard_map/all_gather | solution.py:170
  86.2 2.2 %fusion.155 = f32[512,768]{0,1:T(8,128)S(1)} fusion(bf16[512,1024]{1,0:T(8,128)(2,1)} %all-gather.5.cloned.1.call-done, bf16[1024,768]{1,0:T(8,128)(2,1)S(1)} %copy-done), kind=kOutput, calls=%fused_computation.206 | convolution fusion | flops 805306368 | bytes 4194304 | tf_op jit(solution)/shard_map/dot_general | solution.py:172
  88.8 1.5 %convert_reduce_fusion = (f32[4,512]{1,0:T(4,128)S(1)}, bf16[4,512,512]{1,2,0:T(8,128)(2,1)S(1)}) fusion(f32[512,512]{0,1:T(8,128)S(1)} %abs_add_fusion, f32[4]{0:T(128)S(1)} %dynamic_slice.7, bf16[512,4,2,64]{0,3,1,2:T(8,128)(2,1)S(1)} %multiply_convert_fusion, pred[512]{0:T(512)(128)(4,1)S(1)} %iota_compare_fusion), kind=kOutput, calls=%fused_computation | convolution fusion | flops 141555712 | bytes 3678736 | tf_op jit(solution)/shard_map/qhd,khd->hqk/dot_general | solution.py:194
  91.6 3.4 %all-to-all-start = ((bf16[4,128,256]{1,2,0:T(8,128)(2,1)}), bf16[4,128,256]{1,2,0:T(8,128)(2,1)S(1)}, u32[]{:S(2)}, u32[]{:S(2)}) async-start(bf16[4,128,256]{1,2,0:T(8,128)(2,1)} %copy.34), calls=%async_computation | async-start | bytes 524288 | tf_op jit(solution)/shard_map/all_to_all | solution.py:204
  95.7 8.3 %all-to-all-done = bf16[4,128,256]{1,2,0:T(8,128)(2,1)S(1)} async-done(((bf16[4,128,256]{1,2,0:T(8,128)(2,1)}), bf16[4,128,256]{1,2,0:T(8,128)(2,1)S(1)}, u32[]{:S(2)}, u32[]{:S(2)}) %all-to-all-start) | async-done | bytes 262176 | tf_op jit(solution)/shard_map/all_to_all | solution.py:204
  (55 shorter events, 8.8 us)
Async XLA Ops:
  7.2 79.1 %copy-start = (bf16[1024,768]{1,0:T(8,128)(2,1)S(1)}, bf16[1024,768]{1,0:T(8,128)(2,1)}, u32[]{:S(2)}) copy-start(bf16[1024,768]{1,0:T(8,128)(2,1)} %param.34) | copy-start | bytes 4718596
  7.2 18.6 %copy-start.9 = (f32[1536]{0:T(1024)S(1)}, f32[1536]{0:T(1024)}, u32[]{:S(2)}) copy-start(f32[1536]{0:T(1024)} %param.25) | copy-start | bytes 18436
  7.2 42.2 %all-gather.3.cloned.1.call-start = ((), (), s32[]{:S(2)}) async-start(), calls=%async_computation.1 | async-start | bytes 1966080 | tf_op jit(solution)/shard_map/all_gather | solution.py:122
  9.2 77.1 %all-gather.5.cloned.1.call-start = ((), (), s32[]{:S(2)}) async-start(), calls=%async_computation.2 | async-start | bytes 1310720 | tf_op jit(solution)/shard_map/all_gather | solution.py:170
  22.9 13.3 %copy-start.1 = (bf16[1,3,49,1536]{3,2,1,0:T(8,128)(2,1)S(1)}, bf16[1,3,49,1536]{3,2,1,0:T(8,128)(2,1)}, u32[]{:S(2)}) copy-start(bf16[1,3,49,1536]{3,2,1,0:T(8,128)(2,1)} %param.19) | copy-start | bytes 1354756
  22.9 14.0 %copy-start.4 = (f32[1536]{0:T(1024)S(1)}, f32[1536]{0:T(1024)}, u32[]{:S(2)}) copy-start(f32[1536]{0:T(1024)} %param.28) | copy-start | bytes 18436
  22.9 14.0 %collective-permute-start = (bf16[147,1536]{1,0:T(8,128)(2,1)}, bf16[147,1536]{1,0:T(8,128)(2,1)}, u32[]{:S(2)}, u32[]{:S(2)}) collective-permute-start(bf16[147,1536]{1,0:T(8,128)(2,1)} %reshape.160), channel_id=1, source_target_pairs={{0,2},{2,0},{1,3},{3,1},{4,6},{6,4},{5,7},{7,5},{8,10},{10,8},{9,1... | collective-permute-start | bytes 1354760 | tf_op jit(solution)/shard_map/ppermute | solution.py:143
  46.0 12.4 %copy-start.7 = (f32[1024]{0:T(1024)S(1)}, f32[1024]{0:T(1024)}, u32[]{:S(2)}) copy-start(f32[1024]{0:T(1024)} %param.33) | copy-start | bytes 12292
  46.0 14.7 %copy-start.8 = (s32[1,2,512]{2,1,0:T(2,128)S(1)}, s32[1,2,512]{2,1,0:T(2,128)}, u32[]{:S(2)}) copy-start(s32[1,2,512]{2,1,0:T(2,128)} %param.36) | copy-start | bytes 12292
  49.4 4.1 %collective-permute-start.1 = (f32[3,1536]{1,0:T(4,128)}, f32[3,1536]{1,0:T(4,128)}, u32[]{:S(2)}, u32[]{:S(2)}) collective-permute-start(f32[3,1536]{1,0:T(4,128)} %get-tuple-element.6), channel_id=1, source_target_pairs={{0,2},{2,0},{1,3},{3,1},{4,6},{6,4},{5,7},{7,5},{8,10},{10,8},{9,1... | collective-permute-start | bytes 55304 | tf_op jit(solution)/shard_map/ppermute | solution.py:160
  50.9 6.7 %collective-permute-start.2 = (bf16[1536,512]{1,0:T(8,128)(2,1)}, bf16[1536,512]{1,0:T(8,128)(2,1)S(1)}, u32[]{:S(2)}, u32[]{:S(2)}) collective-permute-start(bf16[1536,512]{1,0:T(8,128)(2,1)} %all-gather.3.cloned.1.call-done), channel_id=1, source_target_pairs={{0,1},{1,0},{2,3},{3,2},{4,5},{5,4},{6,7},{7,6},{8,9},{9,8},{10,11... | collective-permute-start | bytes 4718600 | tf_op jit(solution)/shard_map/ppermute | solution.py:154
  54.4 0.6 copy-start.2
  90.3 4.7 %copy-start.3 = (f32[3,1536]{1,0:T(4,128)S(1)}, f32[3,1536]{1,0:T(4,128)}, u32[]{:S(2)}) copy-start(f32[3,1536]{1,0:T(4,128)} %copy-done.2) | copy-start | bytes 55300
  90.3 4.7 %copy-start.5 = (f32[1536]{0:T(1024)S(1)}, f32[1536]{0:T(1024)}, u32[]{:S(2)}) copy-start(f32[1536]{0:T(1024)} %param.30) | copy-start | bytes 18436
  90.3 4.7 %copy-start.6 = (f32[1536]{0:T(1024)S(1)}, f32[1536]{0:T(1024)}, u32[]{:S(2)}) copy-start(f32[1536]{0:T(1024)} %param.29) | copy-start | bytes 18436
  91.6 12.4 %all-to-all-start = ((bf16[4,128,256]{1,2,0:T(8,128)(2,1)}), bf16[4,128,256]{1,2,0:T(8,128)(2,1)S(1)}, u32[]{:S(2)}, u32[]{:S(2)}) async-start(bf16[4,128,256]{1,2,0:T(8,128)(2,1)} %copy.34), calls=%async_computation | async-start | bytes 524288 | tf_op jit(solution)/shard_map/all_to_all | solution.py:204
Sparse Core Ops, SparseCore 0:
  9.6 39.7 all-gather.2
  59.4 26.8 all-gather.4

commit v8 on v7

--- a/solution.py
+++ b/solution.py
@@ -148,14 +148,6 @@
         block_sums(normed) / positions + down_bias
     )
     peer_terms = [layer_scale * (block_sums(rows) / positions) for rows in received]
-    cols_full, own_term, peer_terms = lax.optimization_barrier(
-        (cols_full, own_term, peer_terms)
-    )
-    other_cols = lax.ppermute(
-        cols_full, "section", perm=[(c, (c + 1) % n_sec) for c in range(n_sec)]
-    )
-    first = lax.axis_index("section") == 0
-    weight_parts = (cols_full, other_cols, first)
     returned = [
         lax.ppermute(term, "rep", perm=[(r, (r - k) % n_rep) for r in range(n_rep)])
         for k, term in enumerate(peer_terms, start=1)
@@ -164,6 +156,12 @@
     for term in returned:
         pooled = pooled + term
     embedded = layer_norm(pooled, head_gain, head_bias, 1e-06).astype(jnp.bfloat16)
+    cols_full, embedded = lax.optimization_barrier((cols_full, embedded))
+    other_cols = lax.ppermute(
+        cols_full, "section", perm=[(c, (c + 1) % n_sec) for c in range(n_sec)]
+    )
+    first = lax.axis_index("section") == 0
+    weight_parts = (cols_full, other_cols, first)
 
     seq_rows = jnp.concatenate([embedded, embed_store[0, fresh_count:]], axis=0)
     normed_seq = project(seq_rows, weight_parts, slide_gain)

time: 113 us -> 111 us (0.982)
  blocking collectives: 0 us -> 11.8 us
  waiting for transfers between devices: 38.7 us -> 33.3 us
  other arithmetic: 7.19 us -> 3.89 us
  starting transfers between devices: 7.9 us -> 4.96 us
  local copies, waits for them, and re-layouts: 15.1 us -> 12.9 us
    all_to_all x0 -> x1, blocking collectives: none -> 11.8 us  [on_device(): lax.all_to_all(attended, 'slide', split_axis=0, concat_axis=1, tiled=True)]
    all_to_all x1 -> x0, waiting for transfers between devices: 8.32 us -> none  [on_device(): lax.all_to_all(attended, 'slide', split_axis=0, concat_axis=1, tiled=True)]
    all_gather x1, waiting for transfers between devices: 3.44 us -> 0.02 us  [on_device(): cols_full = lax.all_gather(my_cols, 'slide', axis=0, tiled=True)]
    all_to_all x1 -> x0, starting transfers between devices: 3.41 us -> none  [on_device(): lax.all_to_all(attended, 'slide', split_axis=0, concat_axis=1, tiled=True)]
    all_gather x1, waiting for transfers between devices: 25.3 us -> 28.6 us  [on_device(): normed_all = lax.all_gather(normed_seq, 'slide', axis=0, tiled=True)]
    ppermute x1, waiting for transfers between devices: 0.01 us -> 2.44 us  [on_device(): lax.ppermute(normed, 'rep', perm=[(r, (r + k) % n_rep) for r in range(n_r...]
    ppermute x1, waiting for transfers between devices: 0.01 us -> 1.66 us  [on_device(): lax.ppermute(cols_full, 'section', perm=[(c, (c + 1) % n_sec) for c in ra...]
    add x1 -> x0, other arithmetic: 1.39 us -> none  [on_device(): jnp.mean(tile_data, axis=1)]
  transfers between devices with their start and end apart: 6 -> 5, of which waited for: 4 -> 4; matrix products, arithmetic and copies ran while one was open for 31% -> 28% of each run, Pallas kernels for 5% -> 5%
where the time goes in v8:
time: 111 us; the launch traced here: 110 us
  waiting for transfers between devices  33.3 us (30%)
  matrix products  22.9 us (21%)
  between operations  14.9 us (13%)
  local copies, waits for them, and re-layouts  12.9 us (12%)
  blocking collectives  11.8 us (11%)
  Pallas kernels  5.74 us (5%)
  starting transfers between devices  4.96 us (4%)
  other arithmetic  3.89 us (4%)
    all_gather x1, waiting for transfers between devices, on_device(): normed_all = lax.all_gather(normed_seq, 'slide', axis=0, tiled=True)  28.6 us
    dot_general x2, matrix products, block_sums(): jnp.dot(hidden, down_weight, preferred_element_type=jnp.float32)  16.5 us
    all_to_all x1, blocking collectives, on_device(): lax.all_to_all(attended, 'slide', split_axis=0, concat_axis=1, tiled=True)  11.8 us
    pallas_call x1, Pallas kernels, dw_ln(): pl.pallas_call(dw_ln_kernel, grid=(T,), in_specs=[pl.BlockSpec((1, SIDE,...  5.74 us
    ppermute x1, starting transfers between devices, on_device(): lax.ppermute(normed, 'rep', perm=[(r, (r + k) % n_rep) for r in range(n_r...  3 us
    reshape x2, local copies, waits for them, and re-layouts, block_sums(): return jnp.sum(part.astype(jnp.float32).reshape(tile_data.shape), axis=1)  2.62 us
    ppermute x1, waiting for transfers between devices, on_device(): lax.ppermute(normed, 'rep', perm=[(r, (r + k) % n_rep) for r in range(n_r...  2.44 us
    dot_general x1, matrix products, on_device(): jnp.dot(normed_all, qkv_weight, preferred_element_type=jnp.float32)  2.24 us
  transfers between devices with their start and end apart: 5, of which 4 were waited for; matrix products, arithmetic and copies ran while one was open for 28% of the time, Pallas kernels for 5%

profile of v8, /device:TPU:0, one launch (start us, length us, event | category | flops | bytes accessed | tf_op | source)
XLA Modules:
  0.0 110.4 jit_solution(9747965976190211988)
XLA Ops:
  7.2 1.9 %constant_dynamic-slice_fusion = bf16[384,512]{1,0:T(8,128)(2,1)} fusion(bf16[384,1024]{1,0:T(8,128)(2,1)} %param.32, s32[]{:T(128)S(6)} %select_n.30), kind=kLoop, calls=%fused_computation.142 | loop fusion | bytes 786436 | tf_op jit(solution)/shard_map/dynamic_slice | solution.py:119
  9.2 1.3 %broadcast_in_dim.42.b_ref = f32[1,1536]{1,0:T(1,128)} reshape(f32[1536]{0:T(1024)} %param.21) | data formatting | bytes 12288 | tf_op jit(solution)/shard_map/broadcast_in_dim | solution.py:71
  10.5 1.3 %broadcast_in_dim.43.g_ref = f32[1,1536]{1,0:T(1,128)} reshape(f32[1536]{0:T(1024)} %param.22) | data formatting | bytes 12288 | tf_op jit(solution)/shard_map/broadcast_in_dim | solution.py:71
  11.8 1.3 %broadcast_in_dim.44.nb_ref = f32[1,1536]{1,0:T(1,128)} reshape(f32[1536]{0:T(1024)} %param.23) | data formatting | bytes 12288 | tf_op jit(solution)/shard_map/broadcast_in_dim | solution.py:71
  13.1 1.2 %reshape_squeeze.3 = bf16[3,7,7,1536]{3,2,1,0:T(8,128)(2,1)S(1)} reshape(bf16[1,3,49,1536]{3,2,1,0:T(8,128)(2,1)} %param.19) | data formatting | bytes 903168 | tf_op jit(solution)/shard_map/reshape;squeeze | solution.py:57
  14.3 0.9 pad.4.x_ref
  15.2 5.7 %shard_map.194 = bf16[3,7,8,1536]{3,2,1,0:T(8,128)(2,1)} custom-call(bf16[3,7,8,1536]{3,2,1,0:T(8,128)(2,1)} %pad.4.x_ref, f32[49,1536]{1,0:T(8,128)} %w_ref.1, f32[1,1536]{1,0:T(1,128)} %broadcast_in_dim.42.b_ref, f32[1,1536]{1,0:T(1,128)} %broadcast_in_dim.43.g_ref, f32[1,1536]{1,0:T(1,128)} %broadcast_in_dim.44.nb_ref), custom_call_target="tpu_custom_call" | custom-call | tf_op jit(solution)/shard_map/pallas_call | solution.py:58
  20.9 1.2 %reshape.160 = bf16[147,1536]{1,0:T(8,128)(2,1)S(1)} reshape(bf16[3,7,7,1536]{3,2,1,0:T(8,128)(2,1)} %bitcast.51) | data formatting | bytes 903168 | tf_op jit(solution)/shard_map/reshape | solution.py:72
  22.1 3.0 %collective-permute-start = (bf16[147,1536]{1,0:T(8,128)(2,1)S(1)}, bf16[147,1536]{1,0:T(8,128)(2,1)S(1)}, u32[]{:S(2)}, u32[]{:S(2)}) collective-permute-start(bf16[147,1536]{1,0:T(8,128)(2,1)S(1)} %reshape.160), channel_id=1, source_target_pairs={{0,2},{2,0},{1,3},{3,1},{4,6},{6,4},{5,7},{7,5},{8,10},{10,8},{9,1... | collective-permute-start | bytes 1354760 | tf_op jit(solution)/shard_map/ppermute | solution.py:143
  25.1 8.2 %fusion.1 = f32[147,1536]{1,0:T(8,128)} fusion(bf16[1536,1536]{1,0:T(8,128)(2,1)} %param.26, bf16[147,1536]{1,0:T(8,128)(2,1)S(1)} %reshape.160, bf16[1536,1536]{1,0:T(8,128)(2,1)} %param.24, f32[1536]{0:T(1024)S(1)} %copy-done.7), kind=kOutput, calls=%fused_computation.7 | convolution fusion | flops 1402619904 | bytes 10798080 | tf_op jit(solution)/shard_map/dot_general | solution.py:137
  33.4 2.4 %collective-permute-done = bf16[147,1536]{1,0:T(8,128)(2,1)S(1)} collective-permute-done((bf16[147,1536]{1,0:T(8,128)(2,1)S(1)}, bf16[147,1536]{1,0:T(8,128)(2,1)S(1)}, u32[]{:S(2)}, u32[]{:S(2)}) %collective-permute-start) | collective-permute-done | bytes 451616 | tf_op jit(solution)/shard_map/ppermute | solution.py:143
  35.8 8.2 %fusion = f32[147,1536]{1,0:T(8,128)} fusion(bf16[1536,1536]{1,0:T(8,128)(2,1)} %param.26, bf16[147,1536]{1,0:T(8,128)(2,1)S(1)} %collective-permute-done, bf16[1536,1536]{1,0:T(8,128)(2,1)} %param.24, f32[1536]{0:T(1024)S(1)} %copy-done.7), kind=kOutput, calls=%fused_computation.5 | convolution fusion | flops 1402619904 | bytes 10798080 | tf_op jit(solution)/shard_map/dot_general | solution.py:137
  44.1 1.3 %reshape.169 = f32[3,49,1536]{2,1,0:T(8,128)S(1)} reshape(f32[147,1536]{1,0:T(8,128)} %fusion) | data formatting | bytes 1806336 | tf_op jit(solution)/shard_map/reshape | solution.py:140
  45.5 1.8 %collective-permute-start.1 = (f32[3,1536]{1,0:T(4,128)S(1)}, f32[3,1536]{1,0:T(4,128)S(1)}, u32[]{:S(2)}, u32[]{:S(2)}) collective-permute-start(f32[3,1536]{1,0:T(4,128)S(1)} %broadcast_multiply_fusion), channel_id=1, source_target_pairs={{0,2},{2,0},{1,3},{3,1},{4,6},{6,4},{5,7},{7,5},{8,10},{10,8},{9,1... | collective-permute-start | bytes 55304 | tf_op jit(solution)/shard_map/ppermute | solution.py:152
  47.4 1.3 %reshape.167 = f32[3,49,1536]{2,1,0:T(8,128)S(1)} reshape(f32[147,1536]{1,0:T(8,128)} %fusion.1) | data formatting | bytes 1806336 | tf_op jit(solution)/shard_map/reshape | solution.py:140
  49.4 0.8 fusion.154
  51.5 1.8 %fusion.90 = f32[128,512]{1,0:T(8,128)S(1)} fusion(bf16[1536,512]{1,0:T(8,128)(2,1)} %all-gather.3.cloned.1.call-done, bf16[125,1536]{1,0:T(8,128)(2,1)S(1)} %slice_bitcast_fusion, bf16[3,1536]{1,0:T(4,128)(2,1)S(1)} %add_convert_fusion), kind=kOutput, calls=%fused_computation.126 | convolution fusion | flops 202113024 | bytes 2228224 | tf_op jit(solution)/shard_map/dot_general | solution.py:86
  53.3 1.7 %collective-permute-done.2 = bf16[1536,512]{1,0:T(8,128)(2,1)S(1)} collective-permute-done((bf16[1536,512]{1,0:T(8,128)(2,1)}, bf16[1536,512]{1,0:T(8,128)(2,1)S(1)}, u32[]{:S(2)}, u32[]{:S(2)}) %collective-permute-start.2) | collective-permute-done | bytes 1572896 | tf_op jit(solution)/shard_map/ppermute | solution.py:160
  55.7 0.8 multiply_convert_fusion.1
  57.6 28.6 %all-gather.5.cloned.1.call-done = bf16[512,1024]{1,0:T(8,128)(2,1)} async-done(((bf16[128,1024]{1,0:T(8,128)(2,1)}), bf16[512,1024]{1,0:T(8,128)(2,1)}) %all-gather.5.cloned.1.call-update) | async-done | bytes 1048592 | tf_op jit(solution)/shard_map/all_gather | solution.py:168
  86.2 2.2 %fusion.155 = f32[512,768]{0,1:T(8,128)S(1)} fusion(bf16[512,1024]{1,0:T(8,128)(2,1)} %all-gather.5.cloned.1.call-done, bf16[1024,768]{1,0:T(8,128)(2,1)S(1)} %copy-done), kind=kOutput, calls=%fused_computation.206 | convolution fusion | flops 805306368 | bytes 4194304 | tf_op jit(solution)/shard_map/dot_general | solution.py:170
  88.8 1.5 %convert_reduce_fusion = (f32[4,512]{1,0:T(4,128)S(1)}, bf16[4,512,512]{1,2,0:T(8,128)(2,1)S(1)}) fusion(f32[512,512]{0,1:T(8,128)S(1)} %abs_add_fusion, f32[4]{0:T(128)S(1)} %dynamic_slice.7, bf16[512,4,2,64]{0,3,1,2:T(8,128)(2,1)S(1)} %multiply_convert_fusion, pred[512]{0:T(512)(128)(4,1)S(1)} %iota_compare_fusion), kind=kOutput, calls=%fused_computation | convolution fusion | flops 141555712 | bytes 3678736 | tf_op jit(solution)/shard_map/qhd,khd->hqk/dot_general | solution.py:192
  90.8 11.8 %all_to_all.16 = bf16[4,128,256]{1,2,0:T(8,128)(2,1)S(1)} all-to-all(bf16[4,128,256]{1,2,0:T(8,128)(2,1)S(1)} %copy.34), channel_id=1, replica_groups=mesh['groups'=2,'slide'=4,'rep'=2,'section'=2] {'slide'}, dimensions={0} | all-to-all | bytes 524288 | tf_op jit(solution)/shard_map/all_to_all | solution.py:202
  102.7 0.8 copy.35
  (51 shorter events, 4.2 us)
Async XLA Ops:
  7.2 79.0 %copy-start = (bf16[1024,768]{1,0:T(8,128)(2,1)S(1)}, bf16[1024,768]{1,0:T(8,128)(2,1)}, u32[]{:S(2)}) copy-start(bf16[1024,768]{1,0:T(8,128)(2,1)} %param.34) | copy-start | bytes 4718596
  7.2 18.0 %copy-start.7 = (f32[1536]{0:T(1024)S(1)}, f32[1536]{0:T(1024)}, u32[]{:S(2)}) copy-start(f32[1536]{0:T(1024)} %param.25) | copy-start | bytes 18436
  7.2 44.1 %all-gather.3.cloned.1.call-start = ((), (), s32[]{:S(2)}) async-start(), calls=%async_computation.1 | async-start | bytes 1966080 | tf_op jit(solution)/shard_map/all_gather | solution.py:122
  9.2 77.0 %all-gather.5.cloned.1.call-start = ((), (), s32[]{:S(2)}) async-start(), calls=%async_computation.2 | async-start | bytes 1310720 | tf_op jit(solution)/shard_map/all_gather | solution.py:168
  22.1 11.3 %copy-start.4 = (f32[1536]{0:T(1024)S(1)}, f32[1536]{0:T(1024)}, u32[]{:S(2)}) copy-start(f32[1536]{0:T(1024)} %param.28) | copy-start | bytes 18436
  22.1 13.7 %collective-permute-start = (bf16[147,1536]{1,0:T(8,128)(2,1)S(1)}, bf16[147,1536]{1,0:T(8,128)(2,1)S(1)}, u32[]{:S(2)}, u32[]{:S(2)}) collective-permute-start(bf16[147,1536]{1,0:T(8,128)(2,1)S(1)} %reshape.160), channel_id=1, source_target_pairs={{0,2},{2,0},{1,3},{3,1},{4,6},{6,4},{5,7},{7,5},{8,10},{10,8},{9,1... | collective-permute-start | bytes 1354760 | tf_op jit(solution)/shard_map/ppermute | solution.py:143
  33.4 13.9 %copy-start.1 = (bf16[1,3,49,1536]{3,2,1,0:T(8,128)(2,1)S(1)}, bf16[1,3,49,1536]{3,2,1,0:T(8,128)(2,1)}, u32[]{:S(2)}) copy-start(bf16[1,3,49,1536]{3,2,1,0:T(8,128)(2,1)} %param.19) | copy-start | bytes 1354756
  44.1 7.3 %copy-start.2 = (bf16[1,128,1536]{2,1,0:T(8,128)(2,1)S(1)}, bf16[1,128,1536]{2,1,0:T(8,128)(2,1)}, u32[]{:S(2)}) copy-start(bf16[1,128,1536]{2,1,0:T(8,128)(2,1)} %param.31) | copy-start | bytes 1179652
  45.5 3.9 %collective-permute-start.1 = (f32[3,1536]{1,0:T(4,128)S(1)}, f32[3,1536]{1,0:T(4,128)S(1)}, u32[]{:S(2)}, u32[]{:S(2)}) collective-permute-start(f32[3,1536]{1,0:T(4,128)S(1)} %broadcast_multiply_fusion), channel_id=1, source_target_pairs={{0,2},{2,0},{1,3},{3,1},{4,6},{6,4},{5,7},{7,5},{8,10},{10,8},{9,1... | collective-permute-start | bytes 55304 | tf_op jit(solution)/shard_map/ppermute | solution.py:152
  48.7 7.0 %copy-start.5 = (f32[1024]{0:T(1024)S(1)}, f32[1024]{0:T(1024)}, u32[]{:S(2)}) copy-start(f32[1024]{0:T(1024)} %param.33) | copy-start | bytes 12292
  51.3 6.4 %copy-start.3 = (bf16[3,1536]{1,0:T(4,128)(2,1)}, bf16[3,1536]{1,0:T(4,128)(2,1)S(1)}, u32[]{:S(2)}) copy-start(bf16[3,1536]{1,0:T(4,128)(2,1)S(1)} %add_convert_fusion) | copy-start | bytes 27652
  51.3 3.7 %collective-permute-start.2 = (bf16[1536,512]{1,0:T(8,128)(2,1)}, bf16[1536,512]{1,0:T(8,128)(2,1)S(1)}, u32[]{:S(2)}, u32[]{:S(2)}) collective-permute-start(bf16[1536,512]{1,0:T(8,128)(2,1)} %all-gather.3.cloned.1.call-done), channel_id=1, source_target_pairs={{0,1},{1,0},{2,3},{3,2},{4,5},{5,4},{6,7},{7,6},{8,9},{9,8},{10,11... | collective-permute-start | bytes 4718600 | tf_op jit(solution)/shard_map/ppermute | solution.py:160
  51.5 5.8 %copy-start.8 = (f32[16]{0:T(128)S(1)}, f32[16]{0:T(128)}, u32[]{:S(2)}) copy-start(f32[16]{0:T(128)} %param.35) | copy-start | bytes 196
  51.5 5.8 %copy-start.6 = (s32[1,2,512]{2,1,0:T(2,128)S(1)}, s32[1,2,512]{2,1,0:T(2,128)}, u32[]{:S(2)}) copy-start(s32[1,2,512]{2,1,0:T(2,128)} %param.36) | copy-start | bytes 12292
Sparse Core Ops, SparseCore 0:
  9.6 39.7 all-gather.2
  56.7 29.4 all-gather.4

commit v9 on v8

--- a/solution.py
+++ b/solution.py
@@ -199,7 +199,25 @@
     safe = jnp.where(key_ok[None, :], totals, 1.0)
     attended = jnp.where(key_ok[:, None, None], weighted / safe.T[:, :, None], 0.0)
     attended = attended.astype(jnp.bfloat16).reshape(seq_len, heads_here * HDIM)
-    context = lax.all_to_all(attended, "slide", split_axis=0, concat_axis=1, tiled=True)
+    block = seq_len // n_slide
+    pieces = [lax.dynamic_slice_in_dim(attended, my_slide * block, block, 0)]
+    for k in range(1, n_slide):
+        target = (my_slide + k) % n_slide
+        pieces.append(
+            lax.ppermute(
+                lax.dynamic_slice_in_dim(attended, target * block, block, 0),
+                "slide",
+                perm=[(j, (j + k) % n_slide) for j in range(n_slide)],
+            )
+        )
+    columns = []
+    for group in range(n_slide):
+        shift = (my_slide - group) % n_slide
+        chosen = pieces[0]
+        for k in range(1, n_slide):
+            chosen = jnp.where(shift == k, pieces[k], chosen)
+        columns.append(chosen)
+    context = jnp.concatenate(columns, axis=1)
     return (embedded[None], context[None])
 
 

time: 111 us -> 116 us (1.045)
  waiting for transfers between devices: 33.3 us -> 46.9 us
  blocking collectives: 11.8 us -> 0 us
  starting transfers between devices: 4.96 us -> 8.99 us
  local copies, waits for them, and re-layouts: 12.9 us -> 11.4 us
    all_gather x1, waiting for transfers between devices: 0.02 us -> 12 us  [on_device(): cols_full = lax.all_gather(my_cols, 'slide', axis=0, tiled=True)]
    all_to_all x1 -> x0, blocking collectives: 11.8 us -> none  [on_device(): lax.all_to_all(attended, 'slide', split_axis=0, concat_axis=1, tiled=True)]
    ppermute x0 -> x3, waiting for transfers between devices: none -> 4.96 us  [on_device(): lax.ppermute(lax.dynamic_slice_in_dim(attended, target * block, block, 0)...]
    ppermute x0 -> x3, starting transfers between devices: none -> 4.1 us  [on_device(): lax.ppermute(lax.dynamic_slice_in_dim(attended, target * block, block, 0)...]
    all_gather x1, waiting for transfers between devices: 28.6 us -> 25.9 us  [on_device(): normed_all = lax.all_gather(normed_seq, 'slide', axis=0, tiled=True)]
  transfers between devices with their start and end apart: 5 -> 8, of which waited for: 4 -> 7; matrix products, arithmetic and copies ran while one was open for 28% -> 21% of each run, Pallas kernels for 5% -> 0%
where the time goes in v9:
time: 116 us
  waiting for transfers between devices  46.9 us (40%)
  matrix products  22.9 us (20%)
  between operations  15 us (13%)
  local copies, waits for them, and re-layouts  11.4 us (10%)
  starting transfers between devices  8.99 us (8%)
  Pallas kernels  5.74 us (5%)
  other arithmetic  4.66 us (4%)
    all_gather x1, waiting for transfers between devices, on_device(): normed_all = lax.all_gather(normed_seq, 'slide', axis=0, tiled=True)  25.9 us
    dot_general x2, matrix products, block_sums(): jnp.dot(hidden, down_weight, preferred_element_type=jnp.float32)  16.5 us
    all_gather x1, waiting for transfers between devices, on_device(): cols_full = lax.all_gather(my_cols, 'slide', axis=0, tiled=True)  12 us
    pallas_call x1, Pallas kernels, dw_ln(): pl.pallas_call(dw_ln_kernel, grid=(T,), in_specs=[pl.BlockSpec((1, SIDE,...  5.74 us
    ppermute x3, waiting for transfers between devices, on_device(): lax.ppermute(lax.dynamic_slice_in_dim(attended, target * block, block, 0)...  4.96 us
    ppermute x3, starting transfers between devices, on_device(): lax.ppermute(lax.dynamic_slice_in_dim(attended, target * block, block, 0)...  4.1 us
    ppermute x1, starting transfers between devices, on_device(): lax.ppermute(normed, 'rep', perm=[(r, (r + k) % n_rep) for r in range(n_r...  3 us
    reshape x2, local copies, waits for them, and re-layouts, block_sums(): return jnp.sum(part.astype(jnp.float32).reshape(tile_data.shape), axis=1)  2.63 us
  transfers between devices with their start and end apart: 8, of which 7 were waited for; matrix products, arithmetic and copies ran while one was open for 21% of the time, Pallas kernels for 0%

profile of v9, /device:TPU:0, one launch (start us, length us, event | category | flops | bytes accessed | tf_op | source)
XLA Modules:
  0.0 115.6 jit_solution(4343678676521352294)
XLA Ops:
  7.2 1.3 %reshape_squeeze.3 = bf16[3,7,7,1536]{3,2,1,0:T(8,128)(2,1)S(1)} reshape(bf16[1,3,49,1536]{3,2,1,0:T(8,128)(2,1)} %param.19) | data formatting | bytes 903168 | tf_op jit(solution)/shard_map/reshape;squeeze | solution.py:57
  8.6 1.3 %broadcast_in_dim.42.b_ref = f32[1,1536]{1,0:T(1,128)} reshape(f32[1536]{0:T(1024)} %param.21) | data formatting | bytes 12288 | tf_op jit(solution)/shard_map/broadcast_in_dim | solution.py:71
  9.9 1.3 %broadcast_in_dim.43.g_ref = f32[1,1536]{1,0:T(1,128)} reshape(f32[1536]{0:T(1024)} %param.22) | data formatting | bytes 12288 | tf_op jit(solution)/shard_map/broadcast_in_dim | solution.py:71
  11.2 1.3 %broadcast_in_dim.44.nb_ref = f32[1,1536]{1,0:T(1,128)} reshape(f32[1536]{0:T(1024)} %param.23) | data formatting | bytes 12288 | tf_op jit(solution)/shard_map/broadcast_in_dim | solution.py:71
  12.5 0.9 pad.4.x_ref
  13.4 5.7 %shard_map.194 = bf16[3,7,8,1536]{3,2,1,0:T(8,128)(2,1)} custom-call(bf16[3,7,8,1536]{3,2,1,0:T(8,128)(2,1)} %pad.4.x_ref, f32[49,1536]{1,0:T(8,128)} %w_ref.1, f32[1,1536]{1,0:T(1,128)} %broadcast_in_dim.42.b_ref, f32[1,1536]{1,0:T(1,128)} %broadcast_in_dim.43.g_ref, f32[1,1536]{1,0:T(1,128)} %broadcast_in_dim.44.nb_ref), custom_call_target="tpu_custom_call" | custom-call | tf_op jit(solution)/shard_map/pallas_call | solution.py:58
  19.1 1.2 %reshape.157 = bf16[147,1536]{1,0:T(8,128)(2,1)S(1)} reshape(bf16[3,7,7,1536]{3,2,1,0:T(8,128)(2,1)} %bitcast.49) | data formatting | bytes 903168 | tf_op jit(solution)/shard_map/reshape | solution.py:72
  20.3 3.0 %collective-permute-start = (bf16[147,1536]{1,0:T(8,128)(2,1)S(1)}, bf16[147,1536]{1,0:T(8,128)(2,1)}, u32[]{:S(2)}, u32[]{:S(2)}) collective-permute-start(bf16[147,1536]{1,0:T(8,128)(2,1)S(1)} %reshape.157), channel_id=1, source_target_pairs={{0,2},{2,0},{1,3},{3,1},{4,6},{6,4},{5,7},{7,5},{8,10},{10,8},{9,1... | collective-permute-start | bytes 1354760 | tf_op jit(solution)/shard_map/ppermute | solution.py:143
  24.2 8.2 %fusion.1 = f32[147,1536]{1,0:T(8,128)} fusion(bf16[1536,1536]{1,0:T(8,128)(2,1)} %param.26, bf16[147,1536]{1,0:T(8,128)(2,1)S(1)} %reshape.157, bf16[1536,1536]{1,0:T(8,128)(2,1)} %param.24, f32[1536]{0:T(1024)S(1)} %copy-done.8), kind=kOutput, calls=%fused_computation.7 | convolution fusion | flops 1402619904 | bytes 10798080 | tf_op jit(solution)/shard_map/dot_general | solution.py:137
  32.4 1.7 %collective-permute-done = bf16[147,1536]{1,0:T(8,128)(2,1)} collective-permute-done((bf16[147,1536]{1,0:T(8,128)(2,1)S(1)}, bf16[147,1536]{1,0:T(8,128)(2,1)}, u32[]{:S(2)}, u32[]{:S(2)}) %collective-permute-start) | collective-permute-done | bytes 451616 | tf_op jit(solution)/shard_map/ppermute | solution.py:143
  34.1 8.3 %fusion = f32[147,1536]{1,0:T(8,128)} fusion(bf16[1536,1536]{1,0:T(8,128)(2,1)} %param.26, bf16[147,1536]{1,0:T(8,128)(2,1)} %collective-permute-done, bf16[1536,1536]{1,0:T(8,128)(2,1)} %param.24, f32[1536]{0:T(1024)S(1)} %copy-done.8), kind=kOutput, calls=%fused_computation.5 | convolution fusion | flops 1402619904 | bytes 10798080 | tf_op jit(solution)/shard_map/dot_general | solution.py:137
  42.4 1.3 %reshape.167 = f32[3,49,1536]{2,1,0:T(8,128)S(1)} reshape(f32[147,1536]{1,0:T(8,128)} %fusion) | data formatting | bytes 1806336 | tf_op jit(solution)/shard_map/reshape | solution.py:140
  43.9 1.8 %collective-permute-start.1 = (f32[3,1536]{1,0:T(4,128)S(1)}, f32[3,1536]{1,0:T(4,128)S(1)}, u32[]{:S(2)}, u32[]{:S(2)}) collective-permute-start(f32[3,1536]{1,0:T(4,128)S(1)} %broadcast_multiply_fusion), channel_id=1, source_target_pairs={{0,2},{2,0},{1,3},{3,1},{4,6},{6,4},{5,7},{7,5},{8,10},{10,8},{9,1... | collective-permute-start | bytes 55304 | tf_op jit(solution)/shard_map/ppermute | solution.py:152
  45.8 1.3 %reshape.165 = f32[3,49,1536]{2,1,0:T(8,128)S(1)} reshape(f32[147,1536]{1,0:T(8,128)} %fusion.1) | data formatting | bytes 1806336 | tf_op jit(solution)/shard_map/reshape | solution.py:140
  49.7 12.0 %all-gather.3.cloned.1.call-done = bf16[1536,512]{1,0:T(8,128)(2,1)} async-done(((bf16[384,512]{1,0:T(8,128)(2,1)}), bf16[1536,512]{1,0:T(8,128)(2,1)}) %all-gather.3.cloned.1.call-update) | async-done | bytes 1572880 | tf_op jit(solution)/shard_map/all_gather | solution.py:122
  61.8 1.8 %fusion.90 = f32[128,512]{1,0:T(8,128)S(1)} fusion(bf16[1536,512]{1,0:T(8,128)(2,1)} %all-gather.3.cloned.1.call-done, bf16[125,1536]{1,0:T(8,128)(2,1)S(1)} %slice_bitcast_fusion, bf16[3,1536]{1,0:T(4,128)(2,1)S(1)} %add_convert_fusion), kind=kOutput, calls=%fused_computation.127 | convolution fusion | flops 202113024 | bytes 2228224 | tf_op jit(solution)/shard_map/dot_general | solution.py:86
  63.6 1.7 %collective-permute-done.2 = bf16[1536,512]{1,0:T(8,128)(2,1)S(1)} collective-permute-done((bf16[1536,512]{1,0:T(8,128)(2,1)}, bf16[1536,512]{1,0:T(8,128)(2,1)S(1)}, u32[]{:S(2)}, u32[]{:S(2)}) %collective-permute-start.2) | collective-permute-done | bytes 1572896 | tf_op jit(solution)/shard_map/ppermute | solution.py:160
  68.0 25.9 %all-gather.5.cloned.1.call-done = bf16[512,1024]{1,0:T(8,128)(2,1)} async-done(((bf16[128,1024]{1,0:T(8,128)(2,1)}), bf16[512,1024]{1,0:T(8,128)(2,1)}) %all-gather.5.cloned.1.call-update) | async-done | bytes 1048592 | tf_op jit(solution)/shard_map/all_gather | solution.py:168
  93.9 2.2 %fusion.155 = f32[512,768]{0,1:T(8,128)S(1)} fusion(bf16[512,1024]{1,0:T(8,128)(2,1)} %all-gather.5.cloned.1.call-done, bf16[1024,768]{1,0:T(8,128)(2,1)S(1)} %copy-done), kind=kOutput, calls=%fused_computation.215 | convolution fusion | flops 805306368 | bytes 4194304 | tf_op jit(solution)/shard_map/dot_general | solution.py:170
  96.4 1.5 %convert_reduce_fusion = (f32[4,512]{1,0:T(4,128)S(1)}, bf16[4,512,512]{1,2,0:T(8,128)(2,1)S(1)}) fusion(f32[512,512]{0,1:T(8,128)S(1)} %abs_add_fusion, f32[4]{0:T(128)S(1)} %dynamic_slice.19, bf16[512,4,2,64]{0,3,1,2:T(8,128)(2,1)S(1)} %multiply_convert_fusion, pred[512]{0:T(512)(128)(4,1)S(1)} %iota_compare_fusion), kind=kOutput, calls=%fused_computation | convolution fusion | flops 141555712 | bytes 3678736 | tf_op jit(solution)/shard_map/qhd,khd->hqk/dot_general | solution.py:192
  98.6 2.0 %collective-permute-start.3 = (bf16[128,256]{1,0:T(8,128)(2,1)S(1)}, bf16[128,256]{1,0:T(8,128)(2,1)S(1)}, u32[]{:S(2)}, u32[]{:S(2)}) collective-permute-start(bf16[128,256]{1,0:T(8,128)(2,1)S(1)} %copy.38), channel_id=1, source_target_pairs={{0,12},{4,0},{8,4},{12,8},{1,13},{5,1},{9,5},{13,9},{2,14},{6,2},{... | collective-permute-start | bytes 196616 | tf_op jit(solution)/shard_map/ppermute | solution.py:207
  100.7 1.1 collective-permute-start.4
  101.8 1.1 collective-permute-start.5
  103.0 4.3 %collective-permute-done.4 = bf16[128,256]{1,0:T(8,128)(2,1)S(1)} collective-permute-done((bf16[128,256]{1,0:T(8,128)(2,1)S(1)}, bf16[128,256]{1,0:T(8,128)(2,1)S(1)}, u32[]{:S(2)}, u32[]{:S(2)}) %collective-permute-start.4) | collective-permute-done | bytes 65568 | tf_op jit(solution)/shard_map/ppermute | solution.py:207
  (62 shorter events, 8.4 us)
Async XLA Ops:
  7.2 86.7 %copy-start = (bf16[1024,768]{1,0:T(8,128)(2,1)S(1)}, bf16[1024,768]{1,0:T(8,128)(2,1)}, u32[]{:S(2)}) copy-start(bf16[1024,768]{1,0:T(8,128)(2,1)} %param.34) | copy-start | bytes 4718596
  7.2 16.1 %copy-start.3 = (bf16[384,1024]{1,0:T(8,128)(2,1)S(1)}, bf16[384,1024]{1,0:T(8,128)(2,1)}, u32[]{:S(2)}) copy-start(bf16[384,1024]{1,0:T(8,128)(2,1)} %param.32) | copy-start | bytes 2359300
  7.2 17.0 %copy-start.8 = (f32[1536]{0:T(1024)S(1)}, f32[1536]{0:T(1024)}, u32[]{:S(2)}) copy-start(f32[1536]{0:T(1024)} %param.25) | copy-start | bytes 18436
  7.2 54.5 %all-gather.3.cloned.1.call-start = ((), (), s32[]{:S(2)}) async-start(), calls=%async_computation | async-start | bytes 1966080 | tf_op jit(solution)/shard_map/all_gather | solution.py:122
  20.3 13.8 %collective-permute-start = (bf16[147,1536]{1,0:T(8,128)(2,1)S(1)}, bf16[147,1536]{1,0:T(8,128)(2,1)}, u32[]{:S(2)}, u32[]{:S(2)}) collective-permute-start(bf16[147,1536]{1,0:T(8,128)(2,1)S(1)} %reshape.157), channel_id=1, source_target_pairs={{0,2},{2,0},{1,3},{3,1},{4,6},{6,4},{5,7},{7,5},{8,10},{10,8},{9,1... | collective-permute-start | bytes 1354760 | tf_op jit(solution)/shard_map/ppermute | solution.py:143
  24.1 8.3 %copy-start.5 = (f32[1536]{0:T(1024)S(1)}, f32[1536]{0:T(1024)}, u32[]{:S(2)}) copy-start(f32[1536]{0:T(1024)} %param.28) | copy-start | bytes 18436
  24.1 69.8 %all-gather.5.cloned.1.call-start = ((), (), s32[]{:S(2)}) async-start(), calls=%async_computation.1 | async-start | bytes 1310720 | tf_op jit(solution)/shard_map/all_gather | solution.py:168
  32.4 13.3 %copy-start.1 = (bf16[1,3,49,1536]{3,2,1,0:T(8,128)(2,1)S(1)}, bf16[1,3,49,1536]{3,2,1,0:T(8,128)(2,1)}, u32[]{:S(2)}) copy-start(bf16[1,3,49,1536]{3,2,1,0:T(8,128)(2,1)} %param.19) | copy-start | bytes 1354756
  42.4 19.2 %copy-start.2 = (bf16[1,128,1536]{2,1,0:T(8,128)(2,1)S(1)}, bf16[1,128,1536]{2,1,0:T(8,128)(2,1)}, u32[]{:S(2)}) copy-start(bf16[1,128,1536]{2,1,0:T(8,128)(2,1)} %param.31) | copy-start | bytes 1179652
  43.9 3.9 %collective-permute-start.1 = (f32[3,1536]{1,0:T(4,128)S(1)}, f32[3,1536]{1,0:T(4,128)S(1)}, u32[]{:S(2)}, u32[]{:S(2)}) collective-permute-start(f32[3,1536]{1,0:T(4,128)S(1)} %broadcast_multiply_fusion), channel_id=1, source_target_pairs={{0,2},{2,0},{1,3},{3,1},{4,6},{6,4},{5,7},{7,5},{8,10},{10,8},{9,1... | collective-permute-start | bytes 55304 | tf_op jit(solution)/shard_map/ppermute | solution.py:152
  47.1 18.9 %copy-start.6 = (f32[1024]{0:T(1024)S(1)}, f32[1024]{0:T(1024)}, u32[]{:S(2)}) copy-start(f32[1024]{0:T(1024)} %param.33) | copy-start | bytes 12292
  49.6 18.3 %copy-start.4 = (bf16[3,1536]{1,0:T(4,128)(2,1)}, bf16[3,1536]{1,0:T(4,128)(2,1)S(1)}, u32[]{:S(2)}) copy-start(bf16[3,1536]{1,0:T(4,128)(2,1)S(1)} %add_convert_fusion) | copy-start | bytes 27652
  61.7 3.6 %collective-permute-start.2 = (bf16[1536,512]{1,0:T(8,128)(2,1)}, bf16[1536,512]{1,0:T(8,128)(2,1)S(1)}, u32[]{:S(2)}, u32[]{:S(2)}) collective-permute-start(bf16[1536,512]{1,0:T(8,128)(2,1)} %all-gather.3.cloned.1.call-done), channel_id=1, source_target_pairs={{0,1},{1,0},{2,3},{3,2},{4,5},{5,4},{6,7},{7,6},{8,9},{9,8},{10,11... | collective-permute-start | bytes 4718600 | tf_op jit(solution)/shard_map/ppermute | solution.py:160
  61.8 5.8 %copy-start.9 = (f32[16]{0:T(128)S(1)}, f32[16]{0:T(128)}, u32[]{:S(2)}) copy-start(f32[16]{0:T(128)} %param.35) | copy-start | bytes 196
  61.8 5.9 %copy-start.7 = (s32[1,2,512]{2,1,0:T(2,128)S(1)}, s32[1,2,512]{2,1,0:T(2,128)}, u32[]{:S(2)}) copy-start(s32[1,2,512]{2,1,0:T(2,128)} %param.36) | copy-start | bytes 12292
  98.6 4.4 %collective-permute-start.3 = (bf16[128,256]{1,0:T(8,128)(2,1)S(1)}, bf16[128,256]{1,0:T(8,128)(2,1)S(1)}, u32[]{:S(2)}, u32[]{:S(2)}) collective-permute-start(bf16[128,256]{1,0:T(8,128)(2,1)S(1)} %copy.38), channel_id=1, source_target_pairs={{0,12},{4,0},{8,4},{12,8},{1,13},{5,1},{9,5},{13,9},{2,14},{6,2},{... | collective-permute-start | bytes 196616 | tf_op jit(solution)/shard_map/ppermute | solution.py:207
  100.7 6.7 %collective-permute-start.4 = (bf16[128,256]{1,0:T(8,128)(2,1)S(1)}, bf16[128,256]{1,0:T(8,128)(2,1)S(1)}, u32[]{:S(2)}, u32[]{:S(2)}) collective-permute-start(bf16[128,256]{1,0:T(8,128)(2,1)S(1)} %copy.39), channel_id=1, source_target_pairs={{0,8},{4,12},{8,0},{12,4},{1,9},{5,13},{9,1},{13,5},{2,10},{6,14},... | collective-permute-start | bytes 196616 | tf_op jit(solution)/shard_map/ppermute | solution.py:207
  101.8 6.2 %collective-permute-start.5 = (bf16[128,256]{1,0:T(8,128)(2,1)S(1)}, bf16[128,256]{1,0:T(8,128)(2,1)S(1)}, u32[]{:S(2)}, u32[]{:S(2)}) collective-permute-start(bf16[128,256]{1,0:T(8,128)(2,1)S(1)} %copy.40), channel_id=1, source_target_pairs={{0,4},{4,8},{8,12},{12,0},{1,5},{5,9},{9,13},{13,1},{2,6},{6,10},{... | collective-permute-start | bytes 196616 | tf_op jit(solution)/shard_map/ppermute | solution.py:207
Sparse Core Ops, SparseCore 0:
  24.2 37.4 all-gather.2
  67.0 26.7 all-gather.4

commit v10 on v9

--- a/solution.py
+++ b/solution.py
@@ -119,6 +119,7 @@
     my_cols = lax.dynamic_slice_in_dim(
         in_weight, lax.axis_index("section") * col_part, col_part, 1
     )
+    my_cols, tile_features = lax.optimization_barrier((my_cols, tile_features))
     cols_full = lax.all_gather(my_cols, "slide", axis=0, tiled=True)
 
     tile_data = tile_features[0].astype(jnp.float32)

time: 116 us -> 117 us (level)
  transfers between devices with their start and end apart: 8 -> 8, of which waited for: 7 -> 7; matrix products, arithmetic and copies ran while one was open for 21% -> 20% of each run, Pallas kernels for 0% -> 0%
where the time goes in v10:
time: 117 us
  waiting for transfers between devices  47 us (40%)
  matrix products  22.8 us (19%)
  between operations  15 us (13%)
  local copies, waits for them, and re-layouts  12.4 us (11%)
  starting transfers between devices  9.01 us (8%)
  Pallas kernels  5.74 us (5%)
  other arithmetic  4.66 us (4%)
    all_gather x1, waiting for transfers between devices, on_device(): normed_all = lax.all_gather(normed_seq, 'slide', axis=0, tiled=True)  25.9 us
    dot_general x2, matrix products, block_sums(): jnp.dot(hidden, down_weight, preferred_element_type=jnp.float32)  16.4 us
    all_gather x1, waiting for transfers between devices, on_device(): cols_full = lax.all_gather(my_cols, 'slide', axis=0, tiled=True)  11.5 us
    pallas_call x1, Pallas kernels, dw_ln(): pl.pallas_call(dw_ln_kernel, grid=(T,), in_specs=[pl.BlockSpec((1, SIDE,...  5.74 us
    ppermute x3, waiting for transfers between devices, on_device(): lax.ppermute(lax.dynamic_slice_in_dim(attended, target * block, block, 0)...  4.95 us
    ppermute x3, starting transfers between devices, on_device(): lax.ppermute(lax.dynamic_slice_in_dim(attended, target * block, block, 0)...  4.11 us
    ppermute x1, starting transfers between devices, on_device(): lax.ppermute(normed, 'rep', perm=[(r, (r + k) % n_rep) for r in range(n_r...  3 us
    reshape x2, local copies, waits for them, and re-layouts, block_sums(): return jnp.sum(part.astype(jnp.float32).reshape(tile_data.shape), axis=1)  2.63 us
  transfers between devices with their start and end apart: 8, of which 7 were waited for; matrix products, arithmetic and copies ran while one was open for 20% of the time, Pallas kernels for 0%

profile of v10, /device:TPU:0, one launch (start us, length us, event | category | flops | bytes accessed | tf_op | source)
XLA Modules:
  0.0 116.6 jit_solution(6866603335413112019)
XLA Ops:
  7.2 1.9 %constant_dynamic-slice_fusion.4 = bf16[384,512]{1,0:T(8,128)(2,1)} fusion(bf16[384,1024]{1,0:T(8,128)(2,1)} %param.32, s32[]{:T(128)S(6)} %select_n.147), kind=kLoop, calls=%fused_computation.147 | loop fusion | bytes 786436 | tf_op jit(solution)/shard_map/dynamic_slice | solution.py:119
  9.1 1.2 %reshape_squeeze.3 = bf16[3,7,7,1536]{3,2,1,0:T(8,128)(2,1)S(1)} reshape(bf16[1,3,49,1536]{3,2,1,0:T(8,128)(2,1)} %param.19) | data formatting | bytes 903168 | tf_op jit(solution)/shard_map/reshape;squeeze | solution.py:57
  10.3 1.3 %broadcast_in_dim.42.b_ref = f32[1,1536]{1,0:T(1,128)} reshape(f32[1536]{0:T(1024)} %param.21) | data formatting | bytes 12288 | tf_op jit(solution)/shard_map/broadcast_in_dim | solution.py:71
  11.6 1.3 %broadcast_in_dim.43.g_ref = f32[1,1536]{1,0:T(1,128)} reshape(f32[1536]{0:T(1024)} %param.22) | data formatting | bytes 12288 | tf_op jit(solution)/shard_map/broadcast_in_dim | solution.py:71
  12.9 1.3 %broadcast_in_dim.44.nb_ref = f32[1,1536]{1,0:T(1,128)} reshape(f32[1536]{0:T(1024)} %param.23) | data formatting | bytes 12288 | tf_op jit(solution)/shard_map/broadcast_in_dim | solution.py:71
  15.1 5.7 %shard_map.194 = bf16[3,7,8,1536]{3,2,1,0:T(8,128)(2,1)} custom-call(bf16[3,7,8,1536]{3,2,1,0:T(8,128)(2,1)} %pad.4.x_ref, f32[49,1536]{1,0:T(8,128)} %w_ref.1, f32[1,1536]{1,0:T(1,128)} %broadcast_in_dim.42.b_ref, f32[1,1536]{1,0:T(1,128)} %broadcast_in_dim.43.g_ref, f32[1,1536]{1,0:T(1,128)} %broadcast_in_dim.44.nb_ref), custom_call_target="tpu_custom_call" | custom-call | tf_op jit(solution)/shard_map/pallas_call | solution.py:58
  20.8 1.2 %reshape.157 = bf16[147,1536]{1,0:T(8,128)(2,1)S(1)} reshape(bf16[3,7,7,1536]{3,2,1,0:T(8,128)(2,1)} %bitcast.49) | data formatting | bytes 903168 | tf_op jit(solution)/shard_map/reshape | solution.py:72
  22.0 3.0 %collective-permute-start = (bf16[147,1536]{1,0:T(8,128)(2,1)S(1)}, bf16[147,1536]{1,0:T(8,128)(2,1)S(1)}, u32[]{:S(2)}, u32[]{:S(2)}) collective-permute-start(bf16[147,1536]{1,0:T(8,128)(2,1)S(1)} %reshape.157), channel_id=1, source_target_pairs={{0,2},{2,0},{1,3},{3,1},{4,6},{6,4},{5,7},{7,5},{8,10},{10,8},{9,1... | collective-permute-start | bytes 1354760 | tf_op jit(solution)/shard_map/ppermute | solution.py:144
  25.1 8.2 %fusion.1 = f32[147,1536]{1,0:T(8,128)} fusion(bf16[1536,1536]{1,0:T(8,128)(2,1)} %param.26, bf16[147,1536]{1,0:T(8,128)(2,1)S(1)} %reshape.157, bf16[1536,1536]{1,0:T(8,128)(2,1)} %param.24, f32[1536]{0:T(1024)S(1)} %copy-done.7), kind=kOutput, calls=%fused_computation.7 | convolution fusion | flops 1402619904 | bytes 10798080 | tf_op jit(solution)/shard_map/dot_general | solution.py:138
  33.3 2.4 %collective-permute-done = bf16[147,1536]{1,0:T(8,128)(2,1)S(1)} collective-permute-done((bf16[147,1536]{1,0:T(8,128)(2,1)S(1)}, bf16[147,1536]{1,0:T(8,128)(2,1)S(1)}, u32[]{:S(2)}, u32[]{:S(2)}) %collective-permute-start) | collective-permute-done | bytes 451616 | tf_op jit(solution)/shard_map/ppermute | solution.py:144
  35.7 8.2 %fusion = f32[147,1536]{1,0:T(8,128)} fusion(bf16[1536,1536]{1,0:T(8,128)(2,1)} %param.26, bf16[147,1536]{1,0:T(8,128)(2,1)S(1)} %collective-permute-done, bf16[1536,1536]{1,0:T(8,128)(2,1)} %param.24, f32[1536]{0:T(1024)S(1)} %copy-done.7), kind=kOutput, calls=%fused_computation.5 | convolution fusion | flops 1402619904 | bytes 10798080 | tf_op jit(solution)/shard_map/dot_general | solution.py:138
  43.9 1.3 %reshape.167 = f32[3,49,1536]{2,1,0:T(8,128)S(1)} reshape(f32[147,1536]{1,0:T(8,128)} %fusion) | data formatting | bytes 1806336 | tf_op jit(solution)/shard_map/reshape | solution.py:141
  45.4 1.8 %collective-permute-start.1 = (f32[3,1536]{1,0:T(4,128)S(1)}, f32[3,1536]{1,0:T(4,128)S(1)}, u32[]{:S(2)}, u32[]{:S(2)}) collective-permute-start(f32[3,1536]{1,0:T(4,128)S(1)} %broadcast_multiply_fusion), channel_id=1, source_target_pairs={{0,2},{2,0},{1,3},{3,1},{4,6},{6,4},{5,7},{7,5},{8,10},{10,8},{9,1... | collective-permute-start | bytes 55304 | tf_op jit(solution)/shard_map/ppermute | solution.py:153
  47.3 1.3 %reshape.165 = f32[3,49,1536]{2,1,0:T(8,128)S(1)} reshape(f32[147,1536]{1,0:T(8,128)} %fusion.1) | data formatting | bytes 1806336 | tf_op jit(solution)/shard_map/reshape | solution.py:141
  51.1 11.5 %all-gather.3.cloned.1.call-done = bf16[1536,512]{1,0:T(8,128)(2,1)} async-done(((bf16[384,512]{1,0:T(8,128)(2,1)}), bf16[1536,512]{1,0:T(8,128)(2,1)}) %all-gather.3.cloned.1.call-update) | async-done | bytes 1572880 | tf_op jit(solution)/shard_map/all_gather | solution.py:123
  62.8 1.8 %fusion.90 = f32[128,512]{1,0:T(8,128)S(1)} fusion(bf16[1536,512]{1,0:T(8,128)(2,1)} %all-gather.3.cloned.1.call-done, bf16[125,1536]{1,0:T(8,128)(2,1)S(1)} %slice_bitcast_fusion, bf16[3,1536]{1,0:T(4,128)(2,1)S(1)} %add_convert_fusion), kind=kOutput, calls=%fused_computation.127 | convolution fusion | flops 202113024 | bytes 2228224 | tf_op jit(solution)/shard_map/dot_general | solution.py:86
  64.6 1.7 %collective-permute-done.2 = bf16[1536,512]{1,0:T(8,128)(2,1)S(1)} collective-permute-done((bf16[1536,512]{1,0:T(8,128)(2,1)}, bf16[1536,512]{1,0:T(8,128)(2,1)S(1)}, u32[]{:S(2)}, u32[]{:S(2)}) %collective-permute-start.2) | collective-permute-done | bytes 1572896 | tf_op jit(solution)/shard_map/ppermute | solution.py:161
  68.9 25.9 %all-gather.5.cloned.1.call-done = bf16[512,1024]{1,0:T(8,128)(2,1)} async-done(((bf16[128,1024]{1,0:T(8,128)(2,1)}), bf16[512,1024]{1,0:T(8,128)(2,1)}) %all-gather.5.cloned.1.call-update) | async-done | bytes 1048592 | tf_op jit(solution)/shard_map/all_gather | solution.py:169
  94.8 2.2 %fusion.155 = f32[512,768]{0,1:T(8,128)S(1)} fusion(bf16[512,1024]{1,0:T(8,128)(2,1)} %all-gather.5.cloned.1.call-done, bf16[1024,768]{1,0:T(8,128)(2,1)S(1)} %copy-done), kind=kOutput, calls=%fused_computation.215 | convolution fusion | flops 805306368 | bytes 4194304 | tf_op jit(solution)/shard_map/dot_general | solution.py:171
  97.4 1.5 %convert_reduce_fusion = (f32[4,512]{1,0:T(4,128)S(1)}, bf16[4,512,512]{1,2,0:T(8,128)(2,1)S(1)}) fusion(f32[512,512]{0,1:T(8,128)S(1)} %abs_add_fusion, f32[4]{0:T(128)S(1)} %dynamic_slice.19, bf16[512,4,2,64]{0,3,1,2:T(8,128)(2,1)S(1)} %multiply_convert_fusion, pred[512]{0:T(512)(128)(4,1)S(1)} %iota_compare_fusion), kind=kOutput, calls=%fused_computation | convolution fusion | flops 141555712 | bytes 3678736 | tf_op jit(solution)/shard_map/qhd,khd->hqk/dot_general | solution.py:193
  99.5 2.0 %collective-permute-start.3 = (bf16[128,256]{1,0:T(8,128)(2,1)S(1)}, bf16[128,256]{1,0:T(8,128)(2,1)S(1)}, u32[]{:S(2)}, u32[]{:S(2)}) collective-permute-start(bf16[128,256]{1,0:T(8,128)(2,1)S(1)} %copy.38), channel_id=1, source_target_pairs={{0,12},{4,0},{8,4},{12,8},{1,13},{5,1},{9,5},{13,9},{2,14},{6,2},{... | collective-permute-start | bytes 196616 | tf_op jit(solution)/shard_map/ppermute | solution.py:208
  101.6 1.1 collective-permute-start.4
  102.8 1.1 collective-permute-start.5
  104.0 4.3 %collective-permute-done.4 = bf16[128,256]{1,0:T(8,128)(2,1)S(1)} collective-permute-done((bf16[128,256]{1,0:T(8,128)(2,1)S(1)}, bf16[128,256]{1,0:T(8,128)(2,1)S(1)}, u32[]{:S(2)}, u32[]{:S(2)}) %collective-permute-start.4) | collective-permute-done | bytes 65568 | tf_op jit(solution)/shard_map/ppermute | solution.py:208
  (60 shorter events, 8.5 us)
Async XLA Ops:
  7.2 87.7 %copy-start = (bf16[1024,768]{1,0:T(8,128)(2,1)S(1)}, bf16[1024,768]{1,0:T(8,128)(2,1)}, u32[]{:S(2)}) copy-start(bf16[1024,768]{1,0:T(8,128)(2,1)} %param.34) | copy-start | bytes 4718596
  7.2 17.9 %copy-start.7 = (f32[1536]{0:T(1024)S(1)}, f32[1536]{0:T(1024)}, u32[]{:S(2)}) copy-start(f32[1536]{0:T(1024)} %param.25) | copy-start | bytes 18436
  7.2 55.4 %all-gather.3.cloned.1.call-start = ((), (), s32[]{:S(2)}) async-start(), calls=%async_computation | async-start | bytes 1966080 | tf_op jit(solution)/shard_map/all_gather | solution.py:123
  22.0 13.7 %collective-permute-start = (bf16[147,1536]{1,0:T(8,128)(2,1)S(1)}, bf16[147,1536]{1,0:T(8,128)(2,1)S(1)}, u32[]{:S(2)}, u32[]{:S(2)}) collective-permute-start(bf16[147,1536]{1,0:T(8,128)(2,1)S(1)} %reshape.157), channel_id=1, source_target_pairs={{0,2},{2,0},{1,3},{3,1},{4,6},{6,4},{5,7},{7,5},{8,10},{10,8},{9,1... | collective-permute-start | bytes 1354760 | tf_op jit(solution)/shard_map/ppermute | solution.py:144
  25.1 8.3 %copy-start.4 = (f32[1536]{0:T(1024)S(1)}, f32[1536]{0:T(1024)}, u32[]{:S(2)}) copy-start(f32[1536]{0:T(1024)} %param.28) | copy-start | bytes 18436
  25.1 69.8 %all-gather.5.cloned.1.call-start = ((), (), s32[]{:S(2)}) async-start(), calls=%async_computation.1 | async-start | bytes 1310720 | tf_op jit(solution)/shard_map/all_gather | solution.py:169
  33.3 13.9 %copy-start.1 = (bf16[1,3,49,1536]{3,2,1,0:T(8,128)(2,1)S(1)}, bf16[1,3,49,1536]{3,2,1,0:T(8,128)(2,1)}, u32[]{:S(2)}) copy-start(bf16[1,3,49,1536]{3,2,1,0:T(8,128)(2,1)} %param.19) | copy-start | bytes 1354756
  43.9 18.7 %copy-start.2 = (bf16[1,128,1536]{2,1,0:T(8,128)(2,1)S(1)}, bf16[1,128,1536]{2,1,0:T(8,128)(2,1)}, u32[]{:S(2)}) copy-start(bf16[1,128,1536]{2,1,0:T(8,128)(2,1)} %param.31) | copy-start | bytes 1179652
  45.4 3.9 %collective-permute-start.1 = (f32[3,1536]{1,0:T(4,128)S(1)}, f32[3,1536]{1,0:T(4,128)S(1)}, u32[]{:S(2)}, u32[]{:S(2)}) collective-permute-start(f32[3,1536]{1,0:T(4,128)S(1)} %broadcast_multiply_fusion), channel_id=1, source_target_pairs={{0,2},{2,0},{1,3},{3,1},{4,6},{6,4},{5,7},{7,5},{8,10},{10,8},{9,1... | collective-permute-start | bytes 55304 | tf_op jit(solution)/shard_map/ppermute | solution.py:153
  48.6 18.4 %copy-start.5 = (f32[1024]{0:T(1024)S(1)}, f32[1024]{0:T(1024)}, u32[]{:S(2)}) copy-start(f32[1024]{0:T(1024)} %param.33) | copy-start | bytes 12292
  51.1 17.8 %copy-start.3 = (bf16[3,1536]{1,0:T(4,128)(2,1)}, bf16[3,1536]{1,0:T(4,128)(2,1)S(1)}, u32[]{:S(2)}) copy-start(bf16[3,1536]{1,0:T(4,128)(2,1)S(1)} %add_convert_fusion) | copy-start | bytes 27652
  62.6 3.6 %collective-permute-start.2 = (bf16[1536,512]{1,0:T(8,128)(2,1)}, bf16[1536,512]{1,0:T(8,128)(2,1)S(1)}, u32[]{:S(2)}, u32[]{:S(2)}) collective-permute-start(bf16[1536,512]{1,0:T(8,128)(2,1)} %all-gather.3.cloned.1.call-done), channel_id=1, source_target_pairs={{0,1},{1,0},{2,3},{3,2},{4,5},{5,4},{6,7},{7,6},{8,9},{9,8},{10,11... | collective-permute-start | bytes 4718600 | tf_op jit(solution)/shard_map/ppermute | solution.py:161
  62.7 5.8 %copy-start.8 = (f32[16]{0:T(128)S(1)}, f32[16]{0:T(128)}, u32[]{:S(2)}) copy-start(f32[16]{0:T(128)} %param.35) | copy-start | bytes 196
  62.7 5.9 %copy-start.6 = (s32[1,2,512]{2,1,0:T(2,128)S(1)}, s32[1,2,512]{2,1,0:T(2,128)}, u32[]{:S(2)}) copy-start(s32[1,2,512]{2,1,0:T(2,128)} %param.36) | copy-start | bytes 12292
  99.5 4.4 %collective-permute-start.3 = (bf16[128,256]{1,0:T(8,128)(2,1)S(1)}, bf16[128,256]{1,0:T(8,128)(2,1)S(1)}, u32[]{:S(2)}, u32[]{:S(2)}) collective-permute-start(bf16[128,256]{1,0:T(8,128)(2,1)S(1)} %copy.38), channel_id=1, source_target_pairs={{0,12},{4,0},{8,4},{12,8},{1,13},{5,1},{9,5},{13,9},{2,14},{6,2},{... | collective-permute-start | bytes 196616 | tf_op jit(solution)/shard_map/ppermute | solution.py:208
  101.6 6.6 %collective-permute-start.4 = (bf16[128,256]{1,0:T(8,128)(2,1)S(1)}, bf16[128,256]{1,0:T(8,128)(2,1)S(1)}, u32[]{:S(2)}, u32[]{:S(2)}) collective-permute-start(bf16[128,256]{1,0:T(8,128)(2,1)S(1)} %copy.39), channel_id=1, source_target_pairs={{0,8},{4,12},{8,0},{12,4},{1,9},{5,13},{9,1},{13,5},{2,10},{6,14},... | collective-permute-start | bytes 196616 | tf_op jit(solution)/shard_map/ppermute | solution.py:208
  102.8 6.2 %collective-permute-start.5 = (bf16[128,256]{1,0:T(8,128)(2,1)S(1)}, bf16[128,256]{1,0:T(8,128)(2,1)S(1)}, u32[]{:S(2)}, u32[]{:S(2)}) collective-permute-start(bf16[128,256]{1,0:T(8,128)(2,1)S(1)} %copy.40), channel_id=1, source_target_pairs={{0,4},{4,8},{8,12},{12,0},{1,5},{5,9},{9,13},{13,1},{2,6},{6,10},{... | collective-permute-start | bytes 196616 | tf_op jit(solution)/shard_map/ppermute | solution.py:208
Sparse Core Ops, SparseCore 0:
  25.2 37.4 all-gather.2
  68.0 26.7 all-gather.4

commit v11 on v5

--- a/solution.py
+++ b/solution.py
@@ -20,14 +20,14 @@
     return centered * lax.rsqrt(spread + epsilon) * gain + shift
 
 
-def dw_ln_kernel(x_ref, w_ref, b_ref, g_ref, nb_ref, o_ref, conv_ref):
+def dw_ln_kernel(x_ref, w_ref, o_ref, conv_ref):
     C = x_ref.shape[-1]
     jrow = lax.broadcasted_iota(jnp.int32, (8, LANES), 0)
     masks = [((jrow + (bb - 3)) >= 0) & ((jrow + (bb - 3)) < SIDE) for bb in range(KER)]
     def chunk(ci, carry):
         c0 = pl.multiple_of(ci * LANES, LANES)
         rows = [x_ref[0, i, :, pl.ds(c0, LANES)].astype(jnp.float32) for i in range(SIDE)]
-        bias = jnp.broadcast_to(b_ref[:, pl.ds(c0, LANES)], (8, LANES))
+        bias = jnp.broadcast_to(w_ref[pl.ds(KER * KER, 1), pl.ds(c0, LANES)], (8, LANES))
         acc = [bias for _ in range(SIDE)]
         for ip in range(SIDE):
             for bb in range(KER):
@@ -43,8 +43,8 @@
             conv_ref[i, :, pl.ds(c0, LANES)] = acc[i]
         return carry
     lax.fori_loop(0, C // LANES, chunk, 0)
-    g = g_ref[...]
-    nb = nb_ref[...]
+    g = w_ref[pl.ds(KER * KER + 1, 1), :]
+    nb = w_ref[pl.ds(KER * KER + 2, 1), :]
     for i in range(SIDE):
         v = conv_ref[i]
         mean = jnp.mean(v, axis=-1, keepdims=True)
@@ -60,15 +60,12 @@
         grid=(T,),
         in_specs=[
             pl.BlockSpec((1, SIDE, 8, C), lambda t: (t, 0, 0, 0)),
-            pl.BlockSpec((KER * KER, C), lambda t: (0, 0)),
-            pl.BlockSpec((1, C), lambda t: (0, 0)),
-            pl.BlockSpec((1, C), lambda t: (0, 0)),
-            pl.BlockSpec((1, C), lambda t: (0, 0)),
+            pl.BlockSpec((KER * KER + 3, C), lambda t: (0, 0)),
         ],
         out_specs=pl.BlockSpec((1, SIDE, 8, C), lambda t: (t, 0, 0, 0)),
         out_shape=jax.ShapeDtypeStruct((T, SIDE, 8, C), jnp.bfloat16),
         scratch_shapes=[pltpu.VMEM((SIDE, 8, C), jnp.float32)],
-    )(x, depth_weight, depth_bias[None], norm_gain[None], norm_bias[None])
+    )(x, jnp.concatenate([depth_weight, depth_bias[None], norm_gain[None], norm_bias[None]]))
     return out[:, :, :SIDE].reshape(T * SIDE * SIDE, C)
 
 
@@ -81,10 +78,21 @@
     return joined.astype(jnp.bfloat16).reshape(lead + (-1,))
 
 
-def project(rows, weight_parts, slide_gain):
-    projected = jnp.einsum(
-        "nk,skc->nsc", rows, weight_parts, preferred_element_type=jnp.float32
-    ).reshape(rows.shape[0], -1)
+def project(rows, partner_rows, cols, slide_gain):
+    n_sec = lax.axis_size("section")
+    both = jnp.dot(
+        jnp.concatenate([rows, partner_rows], axis=0), cols, preferred_element_type=jnp.float32
+    )
+    count = rows.shape[0]
+    mine = both[:count]
+    from_partner = lax.ppermute(
+        both[count:], "section", perm=[(c, (c + 1) % n_sec) for c in range(n_sec)]
+    )
+    projected = jnp.where(
+        lax.axis_index("section") == 0,
+        jnp.concatenate([mine, from_partner], axis=-1),
+        jnp.concatenate([from_partner, mine], axis=-1),
+    )
     return layer_norm(projected, slide_gain, 0.0, 1e-05).astype(jnp.bfloat16)
 
 
@@ -116,6 +124,10 @@
     )
     cols_full = lax.all_gather(my_cols, "slide", axis=0, tiled=True)
 
+    sec_swap = [(c, (c + 1) % n_sec) for c in range(n_sec)]
+    fresh_count = tile_features.shape[1]
+    partner_stored = lax.ppermute(embed_store[0, fresh_count:], "section", perm=sec_swap)
+
     tile_data = tile_features[0].astype(jnp.float32)
     fresh_count = tile_data.shape[0]
     n_rep = lax.axis_size("rep")
@@ -143,10 +155,6 @@
         block_sums(normed) / positions + down_bias
     )
     peer_terms = [layer_scale * (block_sums(rows) / positions) for rows in received]
-    cols_full, own_term, peer_terms = lax.optimization_barrier(
-        (cols_full, own_term, peer_terms)
-    )
-    weight_parts = lax.all_gather(cols_full, "section", axis=0, tiled=False)
     returned = [
         lax.ppermute(term, "rep", perm=[(r, (r - k) % n_rep) for r in range(n_rep)])
         for k, term in enumerate(peer_terms, start=1)
@@ -155,9 +163,12 @@
     for term in returned:
         pooled = pooled + term
     embedded = layer_norm(pooled, head_gain, head_bias, 1e-06).astype(jnp.bfloat16)
+    cols_full, embedded = lax.optimization_barrier((cols_full, embedded))
+    partner_embedded = lax.ppermute(embedded, "section", perm=sec_swap)
 
     seq_rows = jnp.concatenate([embedded, embed_store[0, fresh_count:]], axis=0)
-    normed_seq = project(seq_rows, weight_parts, slide_gain)
+    partner_rows = jnp.concatenate([partner_embedded, partner_stored], axis=0)
+    normed_seq = project(seq_rows, partner_rows, cols_full, slide_gain)
     normed_all = lax.all_gather(normed_seq, "slide", axis=0, tiled=True)
     local_heads = normalize_heads(
         jnp.dot(normed_all, qkv_weight, preferred_element_type=jnp.float32)

time: 122 us -> 110 us (0.902)
  waiting for transfers between devices: 49.3 us -> 34.9 us
  blocking collectives: 0 us -> 11.8 us
  starting transfers between devices: 8.59 us -> 5.27 us
  local copies, waits for them, and re-layouts: 14.3 us -> 11.1 us
  other arithmetic: 5.79 us -> 3.24 us
    all_to_all x0 -> x1, blocking collectives: none -> 11.8 us  [on_device(): lax.all_to_all(attended, 'slide', split_axis=0, concat_axis=1, tiled=True)]
    all_gather x1 -> x0, waiting for transfers between devices: 7.25 us -> none  [on_device(): weight_parts = lax.all_gather(cols_full, 'section', axis=0, tiled=False)]
    all_to_all x1 -> x0, waiting for transfers between devices: 6.2 us -> none  [on_device(): lax.all_to_all(attended, 'slide', split_axis=0, concat_axis=1, tiled=True)]
    all_gather x1, waiting for transfers between devices: 4 us -> 0.02 us  [on_device(): cols_full = lax.all_gather(my_cols, 'slide', axis=0, tiled=True)]
    all_to_all x1 -> x0, starting transfers between devices: 3.81 us -> none  [on_device(): lax.all_to_all(attended, 'slide', split_axis=0, concat_axis=1, tiled=True)]
    ppermute x1, waiting for transfers between devices: 0.01 us -> 3.11 us  [on_device(): lax.ppermute(normed, 'rep', perm=[(r, (r + k) % n_rep) for r in range(n_r...]
    ppermute x0 -> x3, waiting for transfers between devices: none -> 2.53 us  [the longest x1 1.37 us: project(): lax.ppermute(both[count:], 'section', perm=[(c, (c + 1) % n_sec) for c in...]
    all_gather x1, waiting for transfers between devices: 30.5 us -> 28.6 us  [on_device(): normed_all = lax.all_gather(normed_seq, 'slide', axis=0, tiled=True)]
  transfers between devices with their start and end apart: 6 -> 7, of which waited for: 5 -> 5; matrix products, arithmetic and copies ran while one was open for 25% -> 24% of each run, Pallas kernels for 5% -> 5%
where the time goes in v11:
time: 110 us
  waiting for transfers between devices  34.9 us (32%)
  matrix products  22.8 us (21%)
  between operations  15 us (14%)
  blocking collectives  11.8 us (11%)
  local copies, waits for them, and re-layouts  11.1 us (10%)
  Pallas kernels  5.77 us (5%)
  starting transfers between devices  5.27 us (5%)
  other arithmetic  3.24 us (3%)
    all_gather x1, waiting for transfers between devices, on_device(): normed_all = lax.all_gather(normed_seq, 'slide', axis=0, tiled=True)  28.6 us
    dot_general x2, matrix products, block_sums(): jnp.dot(hidden, down_weight, preferred_element_type=jnp.float32)  16.5 us
    all_to_all x1, blocking collectives, on_device(): lax.all_to_all(attended, 'slide', split_axis=0, concat_axis=1, tiled=True)  11.8 us
    pallas_call x1, Pallas kernels, dw_ln(): pl.pallas_call(dw_ln_kernel, grid=(T,), in_specs=[pl.BlockSpec((1, SIDE,...  5.77 us
    ppermute x1, waiting for transfers between devices, on_device(): lax.ppermute(normed, 'rep', perm=[(r, (r + k) % n_rep) for r in range(n_r...  3.11 us
    reshape x2, local copies, waits for them, and re-layouts, block_sums(): return jnp.sum(part.astype(jnp.float32).reshape(tile_data.shape), axis=1)  2.57 us
    ppermute x1, starting transfers between devices, on_device(): lax.ppermute(normed, 'rep', perm=[(r, (r + k) % n_rep) for r in range(n_r...  2.57 us
    dot_general x1, matrix products, on_device(): jnp.dot(normed_all, qkv_weight, preferred_element_type=jnp.float32)  2.24 us
  transfers between devices with their start and end apart: 7, of which 5 were waited for; matrix products, arithmetic and copies ran while one was open for 24% of the time, Pallas kernels for 5%

profile of v11, /device:TPU:0, one launch (start us, length us, event | category | flops | bytes accessed | tf_op | source)
XLA Modules:
  0.0 109.9 jit_solution(5520885220029903430)
XLA Ops:
  7.3 1.9 %constant_dynamic-slice_fusion = bf16[384,512]{1,0:T(8,128)(2,1)} fusion(bf16[384,1024]{1,0:T(8,128)(2,1)} %param.32, s32[]{:T(128)S(6)} %select_n.30), kind=kLoop, calls=%fused_computation.148 | loop fusion | bytes 786436 | tf_op jit(solution)/shard_map/dynamic_slice | solution.py:122
  9.3 1.1 slice_bitcast_fusion
  10.9 0.7 broadcast_in_dim.42
  11.6 0.7 broadcast_in_dim.43
  13.2 0.9 pad.4.x_ref
  14.1 0.8 pad_maximum_fusion.w_ref
  14.8 5.8 %shard_map.194 = bf16[3,7,8,1536]{3,2,1,0:T(8,128)(2,1)} custom-call(bf16[3,7,8,1536]{3,2,1,0:T(8,128)(2,1)} %pad.4.x_ref, f32[52,1536]{1,0:T(8,128)} %pad_maximum_fusion.w_ref), custom_call_target="tpu_custom_call" | custom-call | tf_op jit(solution)/shard_map/pallas_call | solution.py:58
  20.6 1.2 %reshape.160 = bf16[147,1536]{1,0:T(8,128)(2,1)S(1)} reshape(bf16[3,7,7,1536]{3,2,1,0:T(8,128)(2,1)} %bitcast.50) | data formatting | bytes 903168 | tf_op jit(solution)/shard_map/reshape | solution.py:69
  21.8 2.6 %collective-permute-start = (bf16[147,1536]{1,0:T(8,128)(2,1)S(1)}, bf16[147,1536]{1,0:T(8,128)(2,1)S(1)}, u32[]{:S(2)}, u32[]{:S(2)}) collective-permute-start(bf16[147,1536]{1,0:T(8,128)(2,1)S(1)} %reshape.160), channel_id=1, source_target_pairs={{0,2},{2,0},{1,3},{3,1},{4,6},{6,4},{5,7},{7,5},{8,10},{10,8},{9,1... | collective-permute-start | bytes 1354760 | tf_op jit(solution)/shard_map/ppermute | solution.py:150
  24.4 8.2 %fusion.1 = f32[147,1536]{1,0:T(8,128)} fusion(bf16[1536,1536]{1,0:T(8,128)(2,1)} %param.26, bf16[147,1536]{1,0:T(8,128)(2,1)S(1)} %reshape.160, bf16[1536,1536]{1,0:T(8,128)(2,1)} %param.24, f32[1536]{0:T(1024)S(1)} %copy-done.10), kind=kOutput, calls=%fused_computation.7 | convolution fusion | flops 1402619904 | bytes 10798080 | tf_op jit(solution)/shard_map/dot_general | solution.py:144
  32.6 3.1 %collective-permute-done = bf16[147,1536]{1,0:T(8,128)(2,1)S(1)} collective-permute-done((bf16[147,1536]{1,0:T(8,128)(2,1)S(1)}, bf16[147,1536]{1,0:T(8,128)(2,1)S(1)}, u32[]{:S(2)}, u32[]{:S(2)}) %collective-permute-start) | collective-permute-done | bytes 451616 | tf_op jit(solution)/shard_map/ppermute | solution.py:150
  35.7 8.3 %fusion = f32[147,1536]{1,0:T(8,128)} fusion(bf16[1536,1536]{1,0:T(8,128)(2,1)} %param.26, bf16[147,1536]{1,0:T(8,128)(2,1)S(1)} %collective-permute-done, bf16[1536,1536]{1,0:T(8,128)(2,1)} %param.24, f32[1536]{0:T(1024)S(1)} %copy-done.10), kind=kOutput, calls=%fused_computation.5 | convolution fusion | flops 1402619904 | bytes 10798080 | tf_op jit(solution)/shard_map/dot_general | solution.py:144
  44.0 1.3 %reshape.169 = f32[3,49,1536]{2,1,0:T(8,128)S(1)} reshape(f32[147,1536]{1,0:T(8,128)} %fusion) | data formatting | bytes 1806336 | tf_op jit(solution)/shard_map/reshape | solution.py:147
  45.4 1.8 %collective-permute-start.1 = (f32[3,1536]{1,0:T(4,128)S(1)}, f32[3,1536]{1,0:T(4,128)S(1)}, u32[]{:S(2)}, u32[]{:S(2)}) collective-permute-start(f32[3,1536]{1,0:T(4,128)S(1)} %broadcast_multiply_fusion), channel_id=1, source_target_pairs={{0,2},{2,0},{1,3},{3,1},{4,6},{6,4},{5,7},{7,5},{8,10},{10,8},{9,1... | collective-permute-start | bytes 55304 | tf_op jit(solution)/shard_map/ppermute | solution.py:159
  47.3 1.3 %reshape.167 = f32[3,49,1536]{2,1,0:T(8,128)S(1)} reshape(f32[147,1536]{1,0:T(8,128)} %fusion.1) | data formatting | bytes 1806336 | tf_op jit(solution)/shard_map/reshape | solution.py:147
  49.9 1.2 %collective-permute-done.2 = bf16[3,1536]{1,0:T(4,128)(2,1)S(1)} collective-permute-done((bf16[3,1536]{1,0:T(4,128)(2,1)S(1)}, bf16[3,1536]{1,0:T(4,128)(2,1)S(1)}, u32[]{:S(2)}, u32[]{:S(2)}) %collective-permute-start.2) | collective-permute-done | bytes 9248 | tf_op jit(solution)/shard_map/ppermute | solution.py:167
  51.1 2.1 %fusion.25 = f32[256,512]{1,0:T(8,128)S(1)} fusion(bf16[1536,512]{1,0:T(8,128)(2,1)} %all-gather.3.cloned.1.call-done, bf16[125,1536]{1,0:T(8,128)(2,1)} %collective-permute-done.3, bf16[3,1536]{1,0:T(4,128)(2,1)S(1)} %collective-permute-done.2, bf16[125,1536]{1,0:T(8,128)(2,1)S(1)} %slice_bitcast_fusion, bf16[3,1536]{1,0:T(4,128)(2,1)S(1)} %add_convert_fusion), kind=kOutput, calls=%fused_computation.54 | convolution fusion | flops 405798912 | bytes 2883584 | tf_op jit(solution)/shard_map/dot_general | solution.py:83
  53.5 1.4 %collective-permute-done.4 = f32[128,512]{1,0:T(8,128)S(1)} collective-permute-done((f32[128,512]{1,0:T(8,128)S(1)}, f32[128,512]{1,0:T(8,128)S(1)}, u32[]{:S(2)}, u32[]{:S(2)}) %collective-permute-start.4) | collective-permute-done | bytes 262176 | tf_op jit(solution)/shard_map/ppermute | solution.py:88
  55.2 0.8 multiply_convert_fusion.1
  57.1 28.6 %all-gather.5.cloned.1.call-done = bf16[512,1024]{1,0:T(8,128)(2,1)} async-done(((bf16[128,1024]{1,0:T(8,128)(2,1)}), bf16[512,1024]{1,0:T(8,128)(2,1)}) %all-gather.5.cloned.1.call-update) | async-done | bytes 1048592 | tf_op jit(solution)/shard_map/all_gather | solution.py:172
  85.7 2.2 %fusion.161 = f32[512,768]{0,1:T(8,128)S(1)} fusion(bf16[512,1024]{1,0:T(8,128)(2,1)} %all-gather.5.cloned.1.call-done, bf16[1024,768]{1,0:T(8,128)(2,1)S(1)} %copy-done), kind=kOutput, calls=%fused_computation.212 | convolution fusion | flops 805306368 | bytes 4194304 | tf_op jit(solution)/shard_map/dot_general | solution.py:174
  88.3 1.5 %convert_reduce_fusion = (f32[4,512]{1,0:T(4,128)S(1)}, bf16[4,512,512]{1,2,0:T(8,128)(2,1)S(1)}) fusion(f32[512,512]{0,1:T(8,128)S(1)} %abs_add_fusion, f32[4]{0:T(128)S(1)} %dynamic_slice.7, bf16[512,4,2,64]{0,3,1,2:T(8,128)(2,1)S(1)} %multiply_convert_fusion, pred[512]{0:T(512)(128)(4,1)S(1)} %iota_compare_fusion), kind=kOutput, calls=%fused_computation | convolution fusion | flops 141555712 | bytes 3678736 | tf_op jit(solution)/shard_map/qhd,khd->hqk/dot_general | solution.py:196
  90.3 11.8 %all_to_all.16 = bf16[4,128,256]{1,2,0:T(8,128)(2,1)S(1)} all-to-all(bf16[4,128,256]{1,2,0:T(8,128)(2,1)S(1)} %copy.34), channel_id=1, replica_groups=mesh['groups'=2,'slide'=4,'rep'=2,'section'=2] {'slide'}, dimensions={0} | all-to-all | bytes 524288 | tf_op jit(solution)/shard_map/all_to_all | solution.py:206
  102.2 0.8 copy.35
  (62 shorter events, 4.8 us)
Async XLA Ops:
  7.2 78.5 %copy-start = (bf16[1024,768]{1,0:T(8,128)(2,1)S(1)}, bf16[1024,768]{1,0:T(8,128)(2,1)}, u32[]{:S(2)}) copy-start(bf16[1024,768]{1,0:T(8,128)(2,1)} %param.34) | copy-start | bytes 4718596
  7.2 5.8 %copy-start.1 = (bf16[1,3,49,1536]{3,2,1,0:T(8,128)(2,1)S(1)}, bf16[1,3,49,1536]{3,2,1,0:T(8,128)(2,1)}, u32[]{:S(2)}) copy-start(bf16[1,3,49,1536]{3,2,1,0:T(8,128)(2,1)} %param.19) | copy-start | bytes 1354756
  7.2 6.9 %copy-start.2 = (f32[49,1536]{1,0:T(8,128)S(1)}, f32[49,1536]{1,0:T(8,128)}, u32[]{:S(2)}) copy-start(f32[49,1536]{1,0:T(8,128)} %param.20) | copy-start | bytes 903172
  7.2 42.6 %all-gather.3.cloned.1.call-start = ((), (), s32[]{:S(2)}) async-start(), calls=%async_computation.1 | async-start | bytes 1966080 | tf_op jit(solution)/shard_map/all_gather | solution.py:125
  9.2 76.5 %all-gather.5.cloned.1.call-start = ((), (), s32[]{:S(2)}) async-start(), calls=%async_computation.2 | async-start | bytes 1310720 | tf_op jit(solution)/shard_map/all_gather | solution.py:172
  10.4 39.5 %collective-permute-start.3 = (bf16[125,1536]{1,0:T(8,128)(2,1)S(1)}, bf16[125,1536]{1,0:T(8,128)(2,1)}, u32[]{:S(2)}, u32[]{:S(2)}) collective-permute-start(bf16[125,1536]{1,0:T(8,128)(2,1)S(1)} %slice_bitcast_fusion), channel_id=1, source_target_pairs={{0,1},{1,0},{2,3},{3,2},{4,5},{5,4},{6,7},{7,6},{8,9},{9,8},{10,11... | collective-permute-start | bytes 1152008 | tf_op jit(solution)/shard_map/ppermute | solution.py:129
  13.2 11.2 %copy-start.10 = (f32[1536]{0:T(1024)S(1)}, f32[1536]{0:T(1024)}, u32[]{:S(2)}) copy-start(f32[1536]{0:T(1024)} %param.25) | copy-start | bytes 18436
  21.8 10.8 %copy-start.3 = (f32[1536]{0:T(1024)S(1)}, f32[1536]{0:T(1024)}, u32[]{:S(2)}) copy-start(f32[1536]{0:T(1024)} %param.28) | copy-start | bytes 18436
  21.8 13.9 %collective-permute-start = (bf16[147,1536]{1,0:T(8,128)(2,1)S(1)}, bf16[147,1536]{1,0:T(8,128)(2,1)S(1)}, u32[]{:S(2)}, u32[]{:S(2)}) collective-permute-start(bf16[147,1536]{1,0:T(8,128)(2,1)S(1)} %reshape.160), channel_id=1, source_target_pairs={{0,2},{2,0},{1,3},{3,1},{4,6},{6,4},{5,7},{7,5},{8,10},{10,8},{9,1... | collective-permute-start | bytes 1354760 | tf_op jit(solution)/shard_map/ppermute | solution.py:150
  45.4 3.9 %copy-start.5 = (f32[1536]{0:T(1024)S(1)}, f32[1536]{0:T(1024)}, u32[]{:S(2)}) copy-start(f32[1536]{0:T(1024)} %param.27) | copy-start | bytes 18436
  45.4 4.3 %copy-start.6 = (f32[1536]{0:T(1024)S(1)}, f32[1536]{0:T(1024)}, u32[]{:S(2)}) copy-start(f32[1536]{0:T(1024)} %param.30) | copy-start | bytes 18436
  45.4 4.3 %copy-start.7 = (f32[1536]{0:T(1024)S(1)}, f32[1536]{0:T(1024)}, u32[]{:S(2)}) copy-start(f32[1536]{0:T(1024)} %param.29) | copy-start | bytes 18436
  45.4 3.9 %collective-permute-start.1 = (f32[3,1536]{1,0:T(4,128)S(1)}, f32[3,1536]{1,0:T(4,128)S(1)}, u32[]{:S(2)}, u32[]{:S(2)}) collective-permute-start(f32[3,1536]{1,0:T(4,128)S(1)} %broadcast_multiply_fusion), channel_id=1, source_target_pairs={{0,2},{2,0},{1,3},{3,1},{4,6},{6,4},{5,7},{7,5},{8,10},{10,8},{9,1... | collective-permute-start | bytes 55304 | tf_op jit(solution)/shard_map/ppermute | solution.py:159
  49.8 3.4 %copy-start.4 = (bf16[3,1536]{1,0:T(4,128)(2,1)}, bf16[3,1536]{1,0:T(4,128)(2,1)S(1)}, u32[]{:S(2)}) copy-start(bf16[3,1536]{1,0:T(4,128)(2,1)S(1)} %add_convert_fusion) | copy-start | bytes 27652
  49.8 1.2 %collective-permute-start.2 = (bf16[3,1536]{1,0:T(4,128)(2,1)S(1)}, bf16[3,1536]{1,0:T(4,128)(2,1)S(1)}, u32[]{:S(2)}, u32[]{:S(2)}) collective-permute-start(bf16[3,1536]{1,0:T(4,128)(2,1)S(1)} %add_convert_fusion), channel_id=1, source_target_pairs={{0,1},{1,0},{2,3},{3,2},{4,5},{5,4},{6,7},{7,6},{8,9},{9,8},{10,11... | collective-permute-start | bytes 27656 | tf_op jit(solution)/shard_map/ppermute | solution.py:167
  53.2 2.0 %copy-start.8 = (f32[1024]{0:T(1024)S(1)}, f32[1024]{0:T(1024)}, u32[]{:S(2)}) copy-start(f32[1024]{0:T(1024)} %param.33) | copy-start | bytes 12292
  53.2 3.5 %copy-start.11 = (f32[16]{0:T(128)S(1)}, f32[16]{0:T(128)}, u32[]{:S(2)}) copy-start(f32[16]{0:T(128)} %param.35) | copy-start | bytes 196
  53.2 3.6 %copy-start.9 = (s32[1,2,512]{2,1,0:T(2,128)S(1)}, s32[1,2,512]{2,1,0:T(2,128)}, u32[]{:S(2)}) copy-start(s32[1,2,512]{2,1,0:T(2,128)} %param.36) | copy-start | bytes 12292
  53.3 1.6 %collective-permute-start.4 = (f32[128,512]{1,0:T(8,128)S(1)}, f32[128,512]{1,0:T(8,128)S(1)}, u32[]{:S(2)}, u32[]{:S(2)}) collective-permute-start(f32[128,512]{1,0:T(8,128)S(1)} %get-tuple-element.10), channel_id=1, source_target_pairs={{0,1},{1,0},{2,3},{3,2},{4,5},{5,4},{6,7},{7,6},{8,9},{9,8},{10,11... | collective-permute-start | bytes 786440 | tf_op jit(solution)/shard_map/ppermute | solution.py:88
Sparse Core Ops, SparseCore 0:
  9.6 39.7 all-gather.2
  56.2 29.4 all-gather.4

commit v12 on v11

--- a/solution.py
+++ b/solution.py
@@ -80,9 +80,14 @@
 
 def project(rows, partner_rows, cols, slide_gain):
     n_sec = lax.axis_size("section")
-    both = jnp.dot(
-        jnp.concatenate([rows, partner_rows], axis=0), cols, preferred_element_type=jnp.float32
-    )
+    joined = jnp.concatenate([rows, partner_rows], axis=0)
+    n_blocks, n_grp, block_rows, _ = cols.shape
+    both = jnp.einsum(
+        "njk,jgkc->ngc",
+        joined.reshape(joined.shape[0], n_blocks, block_rows),
+        cols,
+        preferred_element_type=jnp.float32,
+    ).reshape(joined.shape[0], -1)
     count = rows.shape[0]
     mine = both[:count]
     from_partner = lax.ppermute(
@@ -119,10 +124,16 @@
 ):
     n_sec = lax.axis_size("section")
     col_part = in_weight.shape[1] // n_sec
+    n_grp = lax.axis_size("groups")
+    sub_part = col_part // n_grp
     my_cols = lax.dynamic_slice_in_dim(
-        in_weight, lax.axis_index("section") * col_part, col_part, 1
-    )
-    cols_full = lax.all_gather(my_cols, "slide", axis=0, tiled=True)
+        in_weight,
+        lax.axis_index("section") * col_part + lax.axis_index("groups") * sub_part,
+        sub_part,
+        1,
+    )
+    cols_full = lax.all_gather(my_cols, ("slide", "groups"), axis=0, tiled=False)
+    cols_full = cols_full.reshape((-1, n_grp) + my_cols.shape)
 
     sec_swap = [(c, (c + 1) % n_sec) for c in range(n_sec)]
     fresh_count = tile_features.shape[1]

time: 110 us -> 118 us (1.073)
  waiting for transfers between devices: 34.9 us -> 40.4 us
  local copies, waits for them, and re-layouts: 11.1 us -> 13.8 us
    all_gather x1, waiting for transfers between devices: 0.02 us -> 8.88 us  [on_device(): lax.all_gather(my_cols, ('slide', 'groups'), axis=0, tiled=False)]
    ppermute x1, waiting for transfers between devices: 3.11 us -> 1.59 us  [on_device(): lax.ppermute(normed, 'rep', perm=[(r, (r + k) % n_rep) for r in range(n_r...]
    ppermute x0 -> x1, local copies, waits for them, and re-layouts: none -> 1.24 us  [on_device(): lax.ppermute(embed_store[0, fresh_count:], 'section', perm=sec_swap)]
  transfers between devices with their start and end apart: 7 -> 7, of which waited for: 5 -> 5; matrix products, arithmetic and copies ran while one was open for 24% -> 25% of each run, Pallas kernels for 5% -> 5%
where the time goes in v12:
time: 118 us; the launch traced here: 117 us
  waiting for transfers between devices  40.4 us (34%)
  matrix products  22.8 us (19%)
  between operations  14.9 us (13%)
  local copies, waits for them, and re-layouts  13.8 us (12%)
  blocking collectives  10.7 us (9%)
  Pallas kernels  5.77 us (5%)
  starting transfers between devices  5.47 us (5%)
  other arithmetic  3.29 us (3%)
    all_gather x1, waiting for transfers between devices, on_device(): normed_all = lax.all_gather(normed_seq, 'slide', axis=0, tiled=True)  28.2 us
    dot_general x2, matrix products, block_sums(): jnp.dot(hidden, down_weight, preferred_element_type=jnp.float32)  16.4 us
    all_to_all x1, blocking collectives, on_device(): lax.all_to_all(attended, 'slide', split_axis=0, concat_axis=1, tiled=True)  10.7 us
    all_gather x1, waiting for transfers between devices, on_device(): lax.all_gather(my_cols, ('slide', 'groups'), axis=0, tiled=False)  8.88 us
    pallas_call x1, Pallas kernels, dw_ln(): pl.pallas_call(dw_ln_kernel, grid=(T,), in_specs=[pl.BlockSpec((1, SIDE,...  5.77 us
    ppermute x1, starting transfers between devices, on_device(): lax.ppermute(normed, 'rep', perm=[(r, (r + k) % n_rep) for r in range(n_r...  3 us
    reshape x2, local copies, waits for them, and re-layouts, block_sums(): return jnp.sum(part.astype(jnp.float32).reshape(tile_data.shape), axis=1)  2.64 us
  transfers between devices with their start and end apart: 7, of which 5 were waited for; matrix products, arithmetic and copies ran while one was open for 25% of the time, Pallas kernels for 5%

profile of v12, /device:TPU:0, one launch (start us, length us, event | category | flops | bytes accessed | tf_op | source)
XLA Modules:
  0.0 117.2 jit_solution(13637162879148142221)
XLA Ops:
  7.2 1.8 %constant_dynamic-slice_fusion = bf16[384,256]{1,0:T(8,128)(2,1)} fusion(bf16[384,1024]{1,0:T(8,128)(2,1)} %param.32, s32[]{:T(128)S(6)} %select_n.30), kind=kLoop, calls=%fused_computation.148 | loop fusion | bytes 393220 | tf_op jit(solution)/shard_map/dynamic_slice | solution.py:129
  11.2 1.2 %reshape_squeeze.3 = bf16[3,7,7,1536]{3,2,1,0:T(8,128)(2,1)S(1)} reshape(bf16[1,3,49,1536]{3,2,1,0:T(8,128)(2,1)} %param.19) | data formatting | bytes 903168 | tf_op jit(solution)/shard_map/reshape;squeeze | solution.py:57
  12.4 0.9 pad.4.x_ref
  13.3 0.8 pad_maximum_fusion.w_ref
  14.1 5.8 %shard_map.194 = bf16[3,7,8,1536]{3,2,1,0:T(8,128)(2,1)} custom-call(bf16[3,7,8,1536]{3,2,1,0:T(8,128)(2,1)} %pad.4.x_ref, f32[52,1536]{1,0:T(8,128)} %pad_maximum_fusion.w_ref), custom_call_target="tpu_custom_call" | custom-call | tf_op jit(solution)/shard_map/pallas_call | solution.py:58
  19.8 1.2 %reshape.173 = bf16[147,1536]{1,0:T(8,128)(2,1)S(1)} reshape(bf16[3,7,7,1536]{3,2,1,0:T(8,128)(2,1)} %bitcast.70) | data formatting | bytes 903168 | tf_op jit(solution)/shard_map/reshape | solution.py:69
  21.1 3.0 %collective-permute-start = (bf16[147,1536]{1,0:T(8,128)(2,1)S(1)}, bf16[147,1536]{1,0:T(8,128)(2,1)S(1)}, u32[]{:S(2)}, u32[]{:S(2)}) collective-permute-start(bf16[147,1536]{1,0:T(8,128)(2,1)S(1)} %reshape.173), channel_id=1, source_target_pairs={{0,2},{2,0},{1,3},{3,1},{4,6},{6,4},{5,7},{7,5},{8,10},{10,8},{9,1... | collective-permute-start | bytes 1354760 | tf_op jit(solution)/shard_map/ppermute | solution.py:161
  24.1 0.9 fusion.161
  24.9 8.2 %fusion.1 = f32[147,1536]{1,0:T(8,128)} fusion(bf16[1536,1536]{1,0:T(8,128)(2,1)} %param.26, bf16[147,1536]{1,0:T(8,128)(2,1)S(1)} %reshape.173, bf16[1536,1536]{1,0:T(8,128)(2,1)} %param.24, f32[1536]{0:T(1024)S(1)} %copy-done.11), kind=kOutput, calls=%fused_computation.7 | convolution fusion | flops 1402619904 | bytes 10798080 | tf_op jit(solution)/shard_map/dot_general | solution.py:155
  33.2 1.6 %collective-permute-done = bf16[147,1536]{1,0:T(8,128)(2,1)S(1)} collective-permute-done((bf16[147,1536]{1,0:T(8,128)(2,1)S(1)}, bf16[147,1536]{1,0:T(8,128)(2,1)S(1)}, u32[]{:S(2)}, u32[]{:S(2)}) %collective-permute-start) | collective-permute-done | bytes 451616 | tf_op jit(solution)/shard_map/ppermute | solution.py:161
  34.8 8.2 %fusion = f32[147,1536]{1,0:T(8,128)} fusion(bf16[1536,1536]{1,0:T(8,128)(2,1)} %param.26, bf16[147,1536]{1,0:T(8,128)(2,1)S(1)} %collective-permute-done, bf16[1536,1536]{1,0:T(8,128)(2,1)} %param.24, f32[1536]{0:T(1024)S(1)} %copy-done.11), kind=kOutput, calls=%fused_computation.5 | convolution fusion | flops 1402619904 | bytes 10798080 | tf_op jit(solution)/shard_map/dot_general | solution.py:155
  43.0 1.3 %reshape.182 = f32[3,49,1536]{2,1,0:T(8,128)S(1)} reshape(f32[147,1536]{1,0:T(8,128)} %fusion) | data formatting | bytes 1806336 | tf_op jit(solution)/shard_map/reshape | solution.py:158
  44.5 1.8 %collective-permute-start.1 = (f32[3,1536]{1,0:T(4,128)S(1)}, f32[3,1536]{1,0:T(4,128)S(1)}, u32[]{:S(2)}, u32[]{:S(2)}) collective-permute-start(f32[3,1536]{1,0:T(4,128)S(1)} %broadcast_multiply_fusion), channel_id=1, source_target_pairs={{0,2},{2,0},{1,3},{3,1},{4,6},{6,4},{5,7},{7,5},{8,10},{10,8},{9,1... | collective-permute-start | bytes 55304 | tf_op jit(solution)/shard_map/ppermute | solution.py:170
  46.4 1.3 %reshape.180 = f32[3,49,1536]{2,1,0:T(8,128)S(1)} reshape(f32[147,1536]{1,0:T(8,128)} %fusion.1) | data formatting | bytes 1806336 | tf_op jit(solution)/shard_map/reshape | solution.py:158
  48.8 8.9 %all-gather.6.cloned.1.call-done = bf16[3072,256]{1,0:T(8,128)(2,1)} async-done(((bf16[384,256]{1,0:T(8,128)(2,1)}), bf16[3072,256]{1,0:T(8,128)(2,1)}) %all-gather.6.cloned.1.call-update) | async-done | bytes 1572880 | tf_op jit(solution)/shard_map/all_gather | solution.py:135
  58.2 1.2 %copy.37 = bf16[125,1536]{0,1:T(8,128)(2,1)S(1)} copy(bf16[125,1536]{1,0:T(8,128)(2,1)} %collective-permute-done.3) | data formatting | bytes 768000 | tf_op jit(solution)/shard_map/ppermute | solution.py:140
  59.7 2.2 %convolution_bitcast_fusion = f32[256,2,256]{0,2,1:T(8,128)S(1)} fusion(bf16[4,2,384,256]{3,2,1,0:T(8,128)(2,1)} %bitcast.79, bf16[125,4,384]{2,0,1:T(8,128)(2,1)S(1)} %copy.39, bf16[3,4,384]{2,0,1:T(4,128)(2,1)S(1)} %bitcast.80, bf16[125,4,384]{2,0,1:T(8,128)(2,1)S(1)} %copy.38, bf16[3,4,384]{2,0,1:T(4,128)(2,1)S(1)} %bitcast.77), kind=kOutput, calls=%fused_computation.10 | convolution fusion | flops 405798912 | bytes 2883584 | tf_op jit(solution)/shard_map/njk,jgkc->ngc/dot_general | solution.py:85
  62.5 1.2 collective-permute-done.4
  64.0 0.9 multiply_convert_fusion.1
  66.0 28.2 %all-gather.4.cloned.1.call-done = bf16[512,1024]{0,1:T(8,128)(2,1)} async-done(((bf16[128,1024]{0,1:T(8,128)(2,1)}), bf16[512,1024]{0,1:T(8,128)(2,1)}) %all-gather.4.cloned.1.call-update) | async-done | bytes 1048592 | tf_op jit(solution)/shard_map/all_gather | solution.py:183
  94.1 2.2 %fusion.162 = f32[512,768]{0,1:T(8,128)S(1)} fusion(bf16[512,1024]{0,1:T(8,128)(2,1)} %all-gather.4.cloned.1.call-done, bf16[1024,768]{1,0:T(8,128)(2,1)S(1)} %copy-done), kind=kOutput, calls=%fused_computation.214 | convolution fusion | flops 805306368 | bytes 4194304 | tf_op jit(solution)/shard_map/dot_general | solution.py:185
  96.7 1.5 %convert_reduce_fusion = (f32[4,512]{1,0:T(4,128)S(1)}, bf16[4,512,512]{1,2,0:T(8,128)(2,1)S(1)}) fusion(f32[512,512]{0,1:T(8,128)S(1)} %abs_add_fusion, f32[4]{0:T(128)S(1)} %dynamic_slice.7, bf16[512,4,2,64]{0,3,1,2:T(8,128)(2,1)S(1)} %multiply_convert_fusion, pred[512]{0:T(512)(128)(4,1)S(1)} %iota_compare_fusion), kind=kOutput, calls=%fused_computation | convolution fusion | flops 141555712 | bytes 3678736 | tf_op jit(solution)/shard_map/qhd,khd->hqk/dot_general | solution.py:207
  98.8 10.7 %all_to_all.16 = bf16[4,128,256]{1,2,0:T(8,128)(2,1)S(1)} all-to-all(bf16[4,128,256]{1,2,0:T(8,128)(2,1)S(1)} %copy.45), channel_id=1, replica_groups=mesh['groups'=2,'slide'=4,'rep'=2,'section'=2] {'slide'}, dimensions={0} | all-to-all | bytes 524288 | tf_op jit(solution)/shard_map/all_to_all | solution.py:217
  109.5 0.8 copy.46
  (68 shorter events, 6.5 us)
Async XLA Ops:
  7.2 87.0 %copy-start = (bf16[1024,768]{1,0:T(8,128)(2,1)S(1)}, bf16[1024,768]{1,0:T(8,128)(2,1)}, u32[]{:S(2)}) copy-start(bf16[1024,768]{1,0:T(8,128)(2,1)} %param.34) | copy-start | bytes 4718596
  7.2 6.1 %copy-start.3 = (f32[49,1536]{1,0:T(8,128)S(1)}, f32[49,1536]{1,0:T(8,128)}, u32[]{:S(2)}) copy-start(f32[49,1536]{1,0:T(8,128)} %param.20) | copy-start | bytes 903172
  7.2 50.5 %all-gather.6.cloned.1.call-start = ((), (), s32[]{:S(2)}) async-start(), calls=%async_computation.2 | async-start | bytes 1769472 | tf_op jit(solution)/shard_map/all_gather | solution.py:135
  9.0 85.1 %all-gather.4.cloned.1.call-start = ((), (), s32[]{:S(2)}) async-start(), calls=%async_computation.1 | async-start | bytes 1310720 | tf_op jit(solution)/shard_map/all_gather | solution.py:183
  12.4 11.7 %copy-start.2 = (bf16[1,128,1536]{2,1,0:T(8,128)(2,1)S(1)}, bf16[1,128,1536]{2,1,0:T(8,128)(2,1)}, u32[]{:S(2)}) copy-start(bf16[1,128,1536]{2,1,0:T(8,128)(2,1)} %param.31) | copy-start | bytes 1179652
  13.3 11.6 %copy-start.11 = (f32[1536]{0:T(1024)S(1)}, f32[1536]{0:T(1024)}, u32[]{:S(2)}) copy-start(f32[1536]{0:T(1024)} %param.25) | copy-start | bytes 18436
  21.1 13.7 %collective-permute-start = (bf16[147,1536]{1,0:T(8,128)(2,1)S(1)}, bf16[147,1536]{1,0:T(8,128)(2,1)S(1)}, u32[]{:S(2)}, u32[]{:S(2)}) collective-permute-start(bf16[147,1536]{1,0:T(8,128)(2,1)S(1)} %reshape.173), channel_id=1, source_target_pairs={{0,2},{2,0},{1,3},{3,1},{4,6},{6,4},{5,7},{7,5},{8,10},{10,8},{9,1... | collective-permute-start | bytes 1354760 | tf_op jit(solution)/shard_map/ppermute | solution.py:161
  24.9 8.2 %copy-start.4 = (f32[1536]{0:T(1024)S(1)}, f32[1536]{0:T(1024)}, u32[]{:S(2)}) copy-start(f32[1536]{0:T(1024)} %param.28) | copy-start | bytes 18436
  24.9 33.3 %collective-permute-start.3 = (bf16[125,1536]{1,0:T(8,128)(2,1)}, bf16[125,1536]{1,0:T(8,128)(2,1)}, u32[]{:S(2)}, u32[]{:S(2)}) collective-permute-start(bf16[125,1536]{1,0:T(8,128)(2,1)} %get-tuple-element.13), channel_id=1, source_target_pairs={{0,1},{1,0},{2,3},{3,2},{4,5},{5,4},{6,7},{7,6},{8,9},{9,8},{10,11... | collective-permute-start | bytes 1152008 | tf_op jit(solution)/shard_map/ppermute | solution.py:140
  43.0 3.3 %copy-start.1 = (bf16[1,3,49,1536]{3,2,1,0:T(8,128)(2,1)S(1)}, bf16[1,3,49,1536]{3,2,1,0:T(8,128)(2,1)}, u32[]{:S(2)}) copy-start(bf16[1,3,49,1536]{3,2,1,0:T(8,128)(2,1)} %param.19) | copy-start | bytes 1354756
  44.4 3.9 %copy-start.6 = (f32[1536]{0:T(1024)S(1)}, f32[1536]{0:T(1024)}, u32[]{:S(2)}) copy-start(f32[1536]{0:T(1024)} %param.27) | copy-start | bytes 18436
  44.4 4.3 %copy-start.7 = (f32[1536]{0:T(1024)S(1)}, f32[1536]{0:T(1024)}, u32[]{:S(2)}) copy-start(f32[1536]{0:T(1024)} %param.30) | copy-start | bytes 18436
  44.4 4.3 %copy-start.8 = (f32[1536]{0:T(1024)S(1)}, f32[1536]{0:T(1024)}, u32[]{:S(2)}) copy-start(f32[1536]{0:T(1024)} %param.29) | copy-start | bytes 18436
  44.5 3.9 %collective-permute-start.1 = (f32[3,1536]{1,0:T(4,128)S(1)}, f32[3,1536]{1,0:T(4,128)S(1)}, u32[]{:S(2)}, u32[]{:S(2)}) collective-permute-start(f32[3,1536]{1,0:T(4,128)S(1)} %broadcast_multiply_fusion), channel_id=1, source_target_pairs={{0,2},{2,0},{1,3},{3,1},{4,6},{6,4},{5,7},{7,5},{8,10},{10,8},{9,1... | collective-permute-start | bytes 55304 | tf_op jit(solution)/shard_map/ppermute | solution.py:170
  48.8 13.1 %copy-start.5 = (bf16[3,1536]{1,0:T(4,128)(2,1)}, bf16[3,1536]{1,0:T(4,128)(2,1)S(1)}, u32[]{:S(2)}) copy-start(bf16[3,1536]{1,0:T(4,128)(2,1)S(1)} %add_convert_fusion) | copy-start | bytes 27652
  57.7 2.0 %collective-permute-start.2 = (bf16[3,1536]{1,0:T(4,128)(2,1)S(1)}, bf16[3,1536]{1,0:T(4,128)(2,1)S(1)}, u32[]{:S(2)}, u32[]{:S(2)}) collective-permute-start(bf16[3,1536]{1,0:T(4,128)(2,1)S(1)} %add_convert_fusion), channel_id=1, source_target_pairs={{0,1},{1,0},{2,3},{3,2},{4,5},{5,4},{6,7},{7,6},{8,9},{9,8},{10,11... | collective-permute-start | bytes 27656 | tf_op jit(solution)/shard_map/ppermute | solution.py:178
  61.9 2.1 %copy-start.9 = (f32[1024]{0:T(1024)S(1)}, f32[1024]{0:T(1024)}, u32[]{:S(2)}) copy-start(f32[1024]{0:T(1024)} %param.33) | copy-start | bytes 12292
  61.9 3.7 %copy-start.12 = (f32[16]{0:T(128)S(1)}, f32[16]{0:T(128)}, u32[]{:S(2)}) copy-start(f32[16]{0:T(128)} %param.35) | copy-start | bytes 196
  61.9 3.8 %copy-start.10 = (s32[1,2,512]{2,1,0:T(2,128)S(1)}, s32[1,2,512]{2,1,0:T(2,128)}, u32[]{:S(2)}) copy-start(s32[1,2,512]{2,1,0:T(2,128)} %param.36) | copy-start | bytes 12292
  62.0 1.7 %collective-permute-start.4 = (f32[128,512]{0,1:T(8,128)S(1)}, f32[128,512]{0,1:T(8,128)S(1)}, u32[]{:S(2)}, u32[]{:S(2)}) collective-permute-start(f32[128,512]{0,1:T(8,128)S(1)} %bitcast.74), channel_id=1, source_target_pairs={{0,1},{1,0},{2,3},{3,2},{4,5},{5,4},{6,7},{7,6},{8,9},{9,8},{10,11... | collective-permute-start | bytes 786440 | tf_op jit(solution)/shard_map/ppermute | solution.py:93
Sparse Core Ops, SparseCore 0:
  10.8 46.8 all-gather.5
  65.1 29.0 all-gather.3

commit v13 on v11

--- a/solution.py
+++ b/solution.py
@@ -163,8 +163,10 @@
     for term in returned:
         pooled = pooled + term
     embedded = layer_norm(pooled, head_gain, head_bias, 1e-06).astype(jnp.bfloat16)
-    cols_full, embedded = lax.optimization_barrier((cols_full, embedded))
     partner_embedded = lax.ppermute(embedded, "section", perm=sec_swap)
+    cols_full, embedded, partner_embedded = lax.optimization_barrier(
+        (cols_full, embedded, partner_embedded)
+    )
 
     seq_rows = jnp.concatenate([embedded, embed_store[0, fresh_count:]], axis=0)
     partner_rows = jnp.concatenate([partner_embedded, partner_stored], axis=0)

time: 110 us -> 110 us (level)
  no operation moved by 1% of the time
where the time goes in v13:
time: 110 us
  waiting for transfers between devices  34.9 us (32%)
  matrix products  22.8 us (21%)
  between operations  15 us (14%)
  blocking collectives  11.9 us (11%)
  local copies, waits for them, and re-layouts  11.1 us (10%)
  Pallas kernels  5.77 us (5%)
  starting transfers between devices  5.27 us (5%)
  other arithmetic  3.24 us (3%)
    all_gather x1, waiting for transfers between devices, on_device(): normed_all = lax.all_gather(normed_seq, 'slide', axis=0, tiled=True)  28.6 us
    dot_general x2, matrix products, block_sums(): jnp.dot(hidden, down_weight, preferred_element_type=jnp.float32)  16.5 us
    all_to_all x1, blocking collectives, on_device(): lax.all_to_all(attended, 'slide', split_axis=0, concat_axis=1, tiled=True)  11.9 us
    pallas_call x1, Pallas kernels, dw_ln(): pl.pallas_call(dw_ln_kernel, grid=(T,), in_specs=[pl.BlockSpec((1, SIDE,...  5.77 us
    ppermute x1, waiting for transfers between devices, on_device(): lax.ppermute(normed, 'rep', perm=[(r, (r + k) % n_rep) for r in range(n_r...  3.11 us
    reshape x2, local copies, waits for them, and re-layouts, block_sums(): return jnp.sum(part.astype(jnp.float32).reshape(tile_data.shape), axis=1)  2.57 us
    ppermute x1, starting transfers between devices, on_device(): lax.ppermute(normed, 'rep', perm=[(r, (r + k) % n_rep) for r in range(n_r...  2.57 us
    dot_general x1, matrix products, on_device(): jnp.dot(normed_all, qkv_weight, preferred_element_type=jnp.float32)  2.24 us
  transfers between devices with their start and end apart: 7, of which 5 were waited for; matrix products, arithmetic and copies ran while one was open for 24% of the time, Pallas kernels for 5%

profile of v13, /device:TPU:0, one launch (start us, length us, event | category | flops | bytes accessed | tf_op | source)
XLA Modules:
  0.0 109.9 jit_solution(18006556241037978347)
XLA Ops:
  7.3 1.9 %constant_dynamic-slice_fusion = bf16[384,512]{1,0:T(8,128)(2,1)} fusion(bf16[384,1024]{1,0:T(8,128)(2,1)} %param.32, s32[]{:T(128)S(6)} %select_n.30), kind=kLoop, calls=%fused_computation.148 | loop fusion | bytes 786436 | tf_op jit(solution)/shard_map/dynamic_slice | solution.py:122
  9.3 1.1 slice_bitcast_fusion
  11.6 0.7 broadcast_in_dim.43
  12.3 0.7 broadcast_in_dim.44
  13.2 0.9 pad.4.x_ref
  14.1 0.8 pad_maximum_fusion.w_ref
  14.8 5.8 %shard_map.194 = bf16[3,7,8,1536]{3,2,1,0:T(8,128)(2,1)} custom-call(bf16[3,7,8,1536]{3,2,1,0:T(8,128)(2,1)} %pad.4.x_ref, f32[52,1536]{1,0:T(8,128)} %pad_maximum_fusion.w_ref), custom_call_target="tpu_custom_call" | custom-call | tf_op jit(solution)/shard_map/pallas_call | solution.py:58
  20.6 1.2 %reshape.160 = bf16[147,1536]{1,0:T(8,128)(2,1)S(1)} reshape(bf16[3,7,7,1536]{3,2,1,0:T(8,128)(2,1)} %bitcast.50) | data formatting | bytes 903168 | tf_op jit(solution)/shard_map/reshape | solution.py:69
  21.8 2.6 %collective-permute-start = (bf16[147,1536]{1,0:T(8,128)(2,1)S(1)}, bf16[147,1536]{1,0:T(8,128)(2,1)S(1)}, u32[]{:S(2)}, u32[]{:S(2)}) collective-permute-start(bf16[147,1536]{1,0:T(8,128)(2,1)S(1)} %reshape.160), channel_id=1, source_target_pairs={{0,2},{2,0},{1,3},{3,1},{4,6},{6,4},{5,7},{7,5},{8,10},{10,8},{9,1... | collective-permute-start | bytes 1354760 | tf_op jit(solution)/shard_map/ppermute | solution.py:150
  24.4 8.2 %fusion.1 = f32[147,1536]{1,0:T(8,128)} fusion(bf16[1536,1536]{1,0:T(8,128)(2,1)} %param.26, bf16[147,1536]{1,0:T(8,128)(2,1)S(1)} %reshape.160, bf16[1536,1536]{1,0:T(8,128)(2,1)} %param.24, f32[1536]{0:T(1024)S(1)} %copy-done.10), kind=kOutput, calls=%fused_computation.7 | convolution fusion | flops 1402619904 | bytes 10798080 | tf_op jit(solution)/shard_map/dot_general | solution.py:144
  32.6 3.1 %collective-permute-done = bf16[147,1536]{1,0:T(8,128)(2,1)S(1)} collective-permute-done((bf16[147,1536]{1,0:T(8,128)(2,1)S(1)}, bf16[147,1536]{1,0:T(8,128)(2,1)S(1)}, u32[]{:S(2)}, u32[]{:S(2)}) %collective-permute-start) | collective-permute-done | bytes 451616 | tf_op jit(solution)/shard_map/ppermute | solution.py:150
  35.7 8.3 %fusion = f32[147,1536]{1,0:T(8,128)} fusion(bf16[1536,1536]{1,0:T(8,128)(2,1)} %param.26, bf16[147,1536]{1,0:T(8,128)(2,1)S(1)} %collective-permute-done, bf16[1536,1536]{1,0:T(8,128)(2,1)} %param.24, f32[1536]{0:T(1024)S(1)} %copy-done.10), kind=kOutput, calls=%fused_computation.5 | convolution fusion | flops 1402619904 | bytes 10798080 | tf_op jit(solution)/shard_map/dot_general | solution.py:144
  44.0 1.3 %reshape.169 = f32[3,49,1536]{2,1,0:T(8,128)S(1)} reshape(f32[147,1536]{1,0:T(8,128)} %fusion) | data formatting | bytes 1806336 | tf_op jit(solution)/shard_map/reshape | solution.py:147
  45.4 1.8 %collective-permute-start.1 = (f32[3,1536]{1,0:T(4,128)S(1)}, f32[3,1536]{1,0:T(4,128)S(1)}, u32[]{:S(2)}, u32[]{:S(2)}) collective-permute-start(f32[3,1536]{1,0:T(4,128)S(1)} %broadcast_multiply_fusion), channel_id=1, source_target_pairs={{0,2},{2,0},{1,3},{3,1},{4,6},{6,4},{5,7},{7,5},{8,10},{10,8},{9,1... | collective-permute-start | bytes 55304 | tf_op jit(solution)/shard_map/ppermute | solution.py:159
  47.3 1.3 %reshape.167 = f32[3,49,1536]{2,1,0:T(8,128)S(1)} reshape(f32[147,1536]{1,0:T(8,128)} %fusion.1) | data formatting | bytes 1806336 | tf_op jit(solution)/shard_map/reshape | solution.py:147
  49.9 1.2 %collective-permute-done.2 = bf16[3,1536]{1,0:T(4,128)(2,1)S(1)} collective-permute-done((bf16[3,1536]{1,0:T(4,128)(2,1)S(1)}, bf16[3,1536]{1,0:T(4,128)(2,1)S(1)}, u32[]{:S(2)}, u32[]{:S(2)}) %collective-permute-start.2) | collective-permute-done | bytes 9248 | tf_op jit(solution)/shard_map/ppermute | solution.py:166
  51.0 2.1 %fusion.25 = f32[256,512]{1,0:T(8,128)S(1)} fusion(bf16[1536,512]{1,0:T(8,128)(2,1)} %all-gather.3.cloned.1.call-done, bf16[125,1536]{1,0:T(8,128)(2,1)} %collective-permute-done.3, bf16[3,1536]{1,0:T(4,128)(2,1)S(1)} %collective-permute-done.2, bf16[125,1536]{1,0:T(8,128)(2,1)S(1)} %slice_bitcast_fusion, bf16[3,1536]{1,0:T(4,128)(2,1)S(1)} %add_convert_fusion), kind=kOutput, calls=%fused_computation.54 | convolution fusion | flops 405798912 | bytes 2883584 | tf_op jit(solution)/shard_map/dot_general | solution.py:83
  53.5 1.4 %collective-permute-done.4 = f32[128,512]{1,0:T(8,128)S(1)} collective-permute-done((f32[128,512]{1,0:T(8,128)S(1)}, f32[128,512]{1,0:T(8,128)S(1)}, u32[]{:S(2)}, u32[]{:S(2)}) %collective-permute-start.4) | collective-permute-done | bytes 262176 | tf_op jit(solution)/shard_map/ppermute | solution.py:88
  55.2 0.8 multiply_convert_fusion.1
  57.1 28.6 %all-gather.5.cloned.1.call-done = bf16[512,1024]{1,0:T(8,128)(2,1)} async-done(((bf16[128,1024]{1,0:T(8,128)(2,1)}), bf16[512,1024]{1,0:T(8,128)(2,1)}) %all-gather.5.cloned.1.call-update) | async-done | bytes 1048592 | tf_op jit(solution)/shard_map/all_gather | solution.py:174
  85.7 2.2 %fusion.161 = f32[512,768]{0,1:T(8,128)S(1)} fusion(bf16[512,1024]{1,0:T(8,128)(2,1)} %all-gather.5.cloned.1.call-done, bf16[1024,768]{1,0:T(8,128)(2,1)S(1)} %copy-done), kind=kOutput, calls=%fused_computation.212 | convolution fusion | flops 805306368 | bytes 4194304 | tf_op jit(solution)/shard_map/dot_general | solution.py:176
  88.2 1.5 %convert_reduce_fusion = (f32[4,512]{1,0:T(4,128)S(1)}, bf16[4,512,512]{1,2,0:T(8,128)(2,1)S(1)}) fusion(f32[512,512]{0,1:T(8,128)S(1)} %abs_add_fusion, f32[4]{0:T(128)S(1)} %dynamic_slice.7, bf16[512,4,2,64]{0,3,1,2:T(8,128)(2,1)S(1)} %multiply_convert_fusion, pred[512]{0:T(512)(128)(4,1)S(1)} %iota_compare_fusion), kind=kOutput, calls=%fused_computation | convolution fusion | flops 141555712 | bytes 3678736 | tf_op jit(solution)/shard_map/qhd,khd->hqk/dot_general | solution.py:198
  90.3 11.9 %all_to_all.16 = bf16[4,128,256]{1,2,0:T(8,128)(2,1)S(1)} all-to-all(bf16[4,128,256]{1,2,0:T(8,128)(2,1)S(1)} %copy.34), channel_id=1, replica_groups=mesh['groups'=2,'slide'=4,'rep'=2,'section'=2] {'slide'}, dimensions={0} | all-to-all | bytes 524288 | tf_op jit(solution)/shard_map/all_to_all | solution.py:208
  102.2 0.8 copy.35
  (62 shorter events, 4.8 us)
Async XLA Ops:
  7.2 78.5 %copy-start = (bf16[1024,768]{1,0:T(8,128)(2,1)S(1)}, bf16[1024,768]{1,0:T(8,128)(2,1)}, u32[]{:S(2)}) copy-start(bf16[1024,768]{1,0:T(8,128)(2,1)} %param.34) | copy-start | bytes 4718596
  7.2 5.8 %copy-start.1 = (bf16[1,3,49,1536]{3,2,1,0:T(8,128)(2,1)S(1)}, bf16[1,3,49,1536]{3,2,1,0:T(8,128)(2,1)}, u32[]{:S(2)}) copy-start(bf16[1,3,49,1536]{3,2,1,0:T(8,128)(2,1)} %param.19) | copy-start | bytes 1354756
  7.2 6.9 %copy-start.2 = (f32[49,1536]{1,0:T(8,128)S(1)}, f32[49,1536]{1,0:T(8,128)}, u32[]{:S(2)}) copy-start(f32[49,1536]{1,0:T(8,128)} %param.20) | copy-start | bytes 903172
  7.2 43.8 %all-gather.3.cloned.1.call-start = ((), (), s32[]{:S(2)}) async-start(), calls=%async_computation.1 | async-start | bytes 1966080 | tf_op jit(solution)/shard_map/all_gather | solution.py:125
  9.2 76.5 %all-gather.5.cloned.1.call-start = ((), (), s32[]{:S(2)}) async-start(), calls=%async_computation.2 | async-start | bytes 1310720 | tf_op jit(solution)/shard_map/all_gather | solution.py:174
  10.4 40.7 %collective-permute-start.3 = (bf16[125,1536]{1,0:T(8,128)(2,1)S(1)}, bf16[125,1536]{1,0:T(8,128)(2,1)}, u32[]{:S(2)}, u32[]{:S(2)}) collective-permute-start(bf16[125,1536]{1,0:T(8,128)(2,1)S(1)} %slice_bitcast_fusion), channel_id=1, source_target_pairs={{0,1},{1,0},{2,3},{3,2},{4,5},{5,4},{6,7},{7,6},{8,9},{9,8},{10,11... | collective-permute-start | bytes 1152008 | tf_op jit(solution)/shard_map/ppermute | solution.py:129
  13.2 11.2 %copy-start.10 = (f32[1536]{0:T(1024)S(1)}, f32[1536]{0:T(1024)}, u32[]{:S(2)}) copy-start(f32[1536]{0:T(1024)} %param.25) | copy-start | bytes 18436
  21.8 10.8 %copy-start.3 = (f32[1536]{0:T(1024)S(1)}, f32[1536]{0:T(1024)}, u32[]{:S(2)}) copy-start(f32[1536]{0:T(1024)} %param.28) | copy-start | bytes 18436
  21.8 13.9 %collective-permute-start = (bf16[147,1536]{1,0:T(8,128)(2,1)S(1)}, bf16[147,1536]{1,0:T(8,128)(2,1)S(1)}, u32[]{:S(2)}, u32[]{:S(2)}) collective-permute-start(bf16[147,1536]{1,0:T(8,128)(2,1)S(1)} %reshape.160), channel_id=1, source_target_pairs={{0,2},{2,0},{1,3},{3,1},{4,6},{6,4},{5,7},{7,5},{8,10},{10,8},{9,1... | collective-permute-start | bytes 1354760 | tf_op jit(solution)/shard_map/ppermute | solution.py:150
  45.4 3.9 %copy-start.5 = (f32[1536]{0:T(1024)S(1)}, f32[1536]{0:T(1024)}, u32[]{:S(2)}) copy-start(f32[1536]{0:T(1024)} %param.27) | copy-start | bytes 18436
  45.4 4.3 %copy-start.6 = (f32[1536]{0:T(1024)S(1)}, f32[1536]{0:T(1024)}, u32[]{:S(2)}) copy-start(f32[1536]{0:T(1024)} %param.30) | copy-start | bytes 18436
  45.4 4.3 %copy-start.7 = (f32[1536]{0:T(1024)S(1)}, f32[1536]{0:T(1024)}, u32[]{:S(2)}) copy-start(f32[1536]{0:T(1024)} %param.29) | copy-start | bytes 18436
  45.4 3.9 %collective-permute-start.1 = (f32[3,1536]{1,0:T(4,128)S(1)}, f32[3,1536]{1,0:T(4,128)S(1)}, u32[]{:S(2)}, u32[]{:S(2)}) collective-permute-start(f32[3,1536]{1,0:T(4,128)S(1)} %broadcast_multiply_fusion), channel_id=1, source_target_pairs={{0,2},{2,0},{1,3},{3,1},{4,6},{6,4},{5,7},{7,5},{8,10},{10,8},{9,1... | collective-permute-start | bytes 55304 | tf_op jit(solution)/shard_map/ppermute | solution.py:159
  49.8 3.4 %copy-start.4 = (bf16[3,1536]{1,0:T(4,128)(2,1)}, bf16[3,1536]{1,0:T(4,128)(2,1)S(1)}, u32[]{:S(2)}) copy-start(bf16[3,1536]{1,0:T(4,128)(2,1)S(1)} %add_convert_fusion) | copy-start | bytes 27652
  49.8 1.2 %collective-permute-start.2 = (bf16[3,1536]{1,0:T(4,128)(2,1)S(1)}, bf16[3,1536]{1,0:T(4,128)(2,1)S(1)}, u32[]{:S(2)}, u32[]{:S(2)}) collective-permute-start(bf16[3,1536]{1,0:T(4,128)(2,1)S(1)} %add_convert_fusion), channel_id=1, source_target_pairs={{0,1},{1,0},{2,3},{3,2},{4,5},{5,4},{6,7},{7,6},{8,9},{9,8},{10,11... | collective-permute-start | bytes 27656 | tf_op jit(solution)/shard_map/ppermute | solution.py:166
  53.2 2.0 %copy-start.8 = (f32[1024]{0:T(1024)S(1)}, f32[1024]{0:T(1024)}, u32[]{:S(2)}) copy-start(f32[1024]{0:T(1024)} %param.33) | copy-start | bytes 12292
  53.2 3.5 %copy-start.11 = (f32[16]{0:T(128)S(1)}, f32[16]{0:T(128)}, u32[]{:S(2)}) copy-start(f32[16]{0:T(128)} %param.35) | copy-start | bytes 196
  53.2 3.6 %copy-start.9 = (s32[1,2,512]{2,1,0:T(2,128)S(1)}, s32[1,2,512]{2,1,0:T(2,128)}, u32[]{:S(2)}) copy-start(s32[1,2,512]{2,1,0:T(2,128)} %param.36) | copy-start | bytes 12292
  53.3 1.6 %collective-permute-start.4 = (f32[128,512]{1,0:T(8,128)S(1)}, f32[128,512]{1,0:T(8,128)S(1)}, u32[]{:S(2)}, u32[]{:S(2)}) collective-permute-start(f32[128,512]{1,0:T(8,128)S(1)} %get-tuple-element.12), channel_id=1, source_target_pairs={{0,1},{1,0},{2,3},{3,2},{4,5},{5,4},{6,7},{7,6},{8,9},{9,8},{10,11... | collective-permute-start | bytes 786440 | tf_op jit(solution)/shard_map/ppermute | solution.py:88
Sparse Core Ops, SparseCore 0:
  9.6 39.7 all-gather.2
  56.2 29.4 all-gather.4

commit v14 on v13

--- a/solution.py
+++ b/solution.py
@@ -78,21 +78,22 @@
     return joined.astype(jnp.bfloat16).reshape(lead + (-1,))
 
 
-def project(rows, partner_rows, cols, slide_gain):
+def project(rows, partner_rows, weight_rows, slide_gain):
     n_sec = lax.axis_size("section")
-    both = jnp.dot(
-        jnp.concatenate([rows, partner_rows], axis=0), cols, preferred_element_type=jnp.float32
-    )
+    joined = jnp.concatenate([rows, partner_rows], axis=0)
+    n_blocks, part_rows, _ = weight_rows.shape
+    picked = lax.dynamic_index_in_dim(
+        joined.reshape(joined.shape[0], n_blocks, n_sec, part_rows),
+        lax.axis_index("section"),
+        2,
+        keepdims=False,
+    )
+    both = jnp.einsum("njk,jkc->nc", picked, weight_rows, preferred_element_type=jnp.float32)
     count = rows.shape[0]
-    mine = both[:count]
     from_partner = lax.ppermute(
         both[count:], "section", perm=[(c, (c + 1) % n_sec) for c in range(n_sec)]
     )
-    projected = jnp.where(
-        lax.axis_index("section") == 0,
-        jnp.concatenate([mine, from_partner], axis=-1),
-        jnp.concatenate([from_partner, mine], axis=-1),
-    )
+    projected = both[:count] + from_partner
     return layer_norm(projected, slide_gain, 0.0, 1e-05).astype(jnp.bfloat16)
 
 
@@ -118,11 +119,11 @@
     valid_counts,
 ):
     n_sec = lax.axis_size("section")
-    col_part = in_weight.shape[1] // n_sec
-    my_cols = lax.dynamic_slice_in_dim(
-        in_weight, lax.axis_index("section") * col_part, col_part, 1
-    )
-    cols_full = lax.all_gather(my_cols, "slide", axis=0, tiled=True)
+    row_part = in_weight.shape[0] // n_sec
+    my_rows = lax.dynamic_slice_in_dim(
+        in_weight, lax.axis_index("section") * row_part, row_part, 0
+    )
+    cols_full = lax.all_gather(my_rows, "slide", axis=0, tiled=False)
 
     sec_swap = [(c, (c + 1) % n_sec) for c in range(n_sec)]
     fresh_count = tile_features.shape[1]

time: 110 us -> 114 us (1.036)
  local copies, waits for them, and re-layouts: 11.1 us -> 12.8 us
  other arithmetic: 3.24 us -> 4.67 us
  transfers between devices with their start and end apart: 7 -> 7, of which waited for: 5 -> 5; matrix products, arithmetic and copies ran while one was open for 24% -> 26% of each run, Pallas kernels for 5% -> 5%
where the time goes in v14:
time: 114 us; the launch traced here: 113 us
  waiting for transfers between devices  35.2 us (31%)
  matrix products  22.9 us (20%)
  between operations  14.9 us (13%)
  local copies, waits for them, and re-layouts  12.8 us (11%)
  blocking collectives  11.9 us (10%)
  Pallas kernels  5.77 us (5%)
  starting transfers between devices  5.28 us (5%)
  other arithmetic  4.67 us (4%)
    all_gather x1, waiting for transfers between devices, on_device(): normed_all = lax.all_gather(normed_seq, 'slide', axis=0, tiled=True)  28.6 us
    dot_general x2, matrix products, block_sums(): jnp.dot(hidden, down_weight, preferred_element_type=jnp.float32)  16.5 us
    all_to_all x1, blocking collectives, on_device(): lax.all_to_all(attended, 'slide', split_axis=0, concat_axis=1, tiled=True)  11.9 us
    pallas_call x1, Pallas kernels, dw_ln(): pl.pallas_call(dw_ln_kernel, grid=(T,), in_specs=[pl.BlockSpec((1, SIDE,...  5.77 us
    ppermute x1, waiting for transfers between devices, on_device(): lax.ppermute(normed, 'rep', perm=[(r, (r + k) % n_rep) for r in range(n_r...  3.11 us
    reshape x2, local copies, waits for them, and re-layouts, block_sums(): return jnp.sum(part.astype(jnp.float32).reshape(tile_data.shape), axis=1)  2.57 us
    ppermute x1, starting transfers between devices, on_device(): lax.ppermute(normed, 'rep', perm=[(r, (r + k) % n_rep) for r in range(n_r...  2.57 us
  transfers between devices with their start and end apart: 7, of which 5 were waited for; matrix products, arithmetic and copies ran while one was open for 26% of the time, Pallas kernels for 5%

profile of v14, /device:TPU:0, one launch (start us, length us, event | category | flops | bytes accessed | tf_op | source)
XLA Modules:
  0.0 113.4 jit_solution(182507692424012911)
XLA Ops:
  7.3 1.9 %constant_dynamic-slice_fusion = bf16[192,1024]{1,0:T(8,128)(2,1)} fusion(bf16[384,1024]{1,0:T(8,128)(2,1)} %param.32, s32[]{:T(128)S(6)} %select_n.26), kind=kLoop, calls=%fused_computation.144 | loop fusion | bytes 786436 | tf_op jit(solution)/shard_map/dynamic_slice | solution.py:123
  9.2 1.1 slice.36
  13.2 1.2 %reshape_squeeze.3 = bf16[3,7,7,1536]{3,2,1,0:T(8,128)(2,1)S(1)} reshape(bf16[1,3,49,1536]{3,2,1,0:T(8,128)(2,1)} %param.19) | data formatting | bytes 903168 | tf_op jit(solution)/shard_map/reshape;squeeze | solution.py:57
  14.4 0.9 pad.4.x_ref
  16.0 5.8 %shard_map.194 = bf16[3,7,8,1536]{3,2,1,0:T(8,128)(2,1)} custom-call(bf16[3,7,8,1536]{3,2,1,0:T(8,128)(2,1)} %pad.4.x_ref, f32[52,1536]{1,0:T(8,128)} %pad_maximum_fusion.w_ref), custom_call_target="tpu_custom_call" | custom-call | tf_op jit(solution)/shard_map/pallas_call | solution.py:58
  21.8 1.2 %reshape.166 = bf16[147,1536]{1,0:T(8,128)(2,1)S(1)} reshape(bf16[3,7,7,1536]{3,2,1,0:T(8,128)(2,1)} %bitcast.59) | data formatting | bytes 903168 | tf_op jit(solution)/shard_map/reshape | solution.py:69
  23.0 2.6 %collective-permute-start = (bf16[147,1536]{1,0:T(8,128)(2,1)S(1)}, bf16[147,1536]{1,0:T(8,128)(2,1)S(1)}, u32[]{:S(2)}, u32[]{:S(2)}) collective-permute-start(bf16[147,1536]{1,0:T(8,128)(2,1)S(1)} %reshape.166), channel_id=1, source_target_pairs={{0,2},{2,0},{1,3},{3,1},{4,6},{6,4},{5,7},{7,5},{8,10},{10,8},{9,1... | collective-permute-start | bytes 1354760 | tf_op jit(solution)/shard_map/ppermute | solution.py:151
  25.6 8.2 %fusion.1 = f32[147,1536]{1,0:T(8,128)} fusion(bf16[1536,1536]{1,0:T(8,128)(2,1)} %param.26, bf16[147,1536]{1,0:T(8,128)(2,1)S(1)} %reshape.166, bf16[1536,1536]{1,0:T(8,128)(2,1)} %param.24, f32[1536]{0:T(1024)S(1)} %copy-done.7), kind=kOutput, calls=%fused_computation.7 | convolution fusion | flops 1402619904 | bytes 10798080 | tf_op jit(solution)/shard_map/dot_general | solution.py:145
  33.8 3.1 %collective-permute-done = bf16[147,1536]{1,0:T(8,128)(2,1)S(1)} collective-permute-done((bf16[147,1536]{1,0:T(8,128)(2,1)S(1)}, bf16[147,1536]{1,0:T(8,128)(2,1)S(1)}, u32[]{:S(2)}, u32[]{:S(2)}) %collective-permute-start) | collective-permute-done | bytes 451616 | tf_op jit(solution)/shard_map/ppermute | solution.py:151
  36.9 8.3 %fusion = f32[147,1536]{1,0:T(8,128)} fusion(bf16[1536,1536]{1,0:T(8,128)(2,1)} %param.26, bf16[147,1536]{1,0:T(8,128)(2,1)S(1)} %collective-permute-done, bf16[1536,1536]{1,0:T(8,128)(2,1)} %param.24, f32[1536]{0:T(1024)S(1)} %copy-done.7), kind=kOutput, calls=%fused_computation.5 | convolution fusion | flops 1402619904 | bytes 10798080 | tf_op jit(solution)/shard_map/dot_general | solution.py:145
  45.2 1.3 %reshape.175 = f32[3,49,1536]{2,1,0:T(8,128)S(1)} reshape(f32[147,1536]{1,0:T(8,128)} %fusion) | data formatting | bytes 1806336 | tf_op jit(solution)/shard_map/reshape | solution.py:148
  46.6 1.8 %collective-permute-start.1 = (f32[3,1536]{1,0:T(4,128)S(1)}, f32[3,1536]{1,0:T(4,128)S(1)}, u32[]{:S(2)}, u32[]{:S(2)}) collective-permute-start(f32[3,1536]{1,0:T(4,128)S(1)} %broadcast_multiply_fusion), channel_id=1, source_target_pairs={{0,2},{2,0},{1,3},{3,1},{4,6},{6,4},{5,7},{7,5},{8,10},{10,8},{9,1... | collective-permute-start | bytes 55304 | tf_op jit(solution)/shard_map/ppermute | solution.py:160
  48.5 1.3 %reshape.173 = f32[3,49,1536]{2,1,0:T(8,128)S(1)} reshape(f32[147,1536]{1,0:T(8,128)} %fusion.1) | data formatting | bytes 1806336 | tf_op jit(solution)/shard_map/reshape | solution.py:148
  50.5 0.8 fusion.157
  51.5 0.8 add_convert_fusion
  52.4 1.2 %collective-permute-done.2 = bf16[3,1536]{1,0:T(4,128)(2,1)S(1)} collective-permute-done((bf16[3,1536]{1,0:T(4,128)(2,1)S(1)}, bf16[3,1536]{1,0:T(4,128)(2,1)S(1)}, u32[]{:S(2)}, u32[]{:S(2)}) %collective-permute-start.2) | collective-permute-done | bytes 9248 | tf_op jit(solution)/shard_map/ppermute | solution.py:167
  54.2 2.2 %convolution_bitcast_fusion = f32[256,1024]{1,0:T(8,128)S(1)} fusion(bf16[4,192,1024]{2,1,0:T(8,128)(2,1)} %bitcast.60, s32[]{:T(128)S(6)} %select_n.27, bf16[3,4,2,192]{0,3,2,1:T(8,128)(2,1)S(1)} %bitcast.64, bf16[125,4,2,192]{0,3,2,1:T(8,128)(2,1)S(1)} %bitcast.62, bf16[3,4,2,192]{0,3,2,1:T(8,128)(2,1)S(1)} %bitcast.63, bf16[125,4,2,192]{0,3,2,1:T(8,128)(2,1)} %bitcast.7), kind=kOutput, calls=%fused_computation.10 | convolution fusion | flops 404226048 | bytes 3407876 | tf_op jit(solution)/shard_map/njk,jkc->nc/dot_general | solution.py:91
  56.6 1.7 %collective-permute-done.4 = f32[128,1024]{1,0:T(8,128)S(1)} collective-permute-done((f32[128,1024]{1,0:T(8,128)S(1)}, f32[128,1024]{1,0:T(8,128)S(1)}, u32[]{:S(2)}, u32[]{:S(2)}) %collective-permute-start.4) | collective-permute-done | bytes 524320 | tf_op jit(solution)/shard_map/ppermute | solution.py:93
  58.8 0.9 multiply_convert_fusion.1
  60.6 28.6 %all-gather.4.cloned.1.call-done = bf16[512,1024]{1,0:T(8,128)(2,1)} async-done(((bf16[128,1024]{1,0:T(8,128)(2,1)}), bf16[512,1024]{1,0:T(8,128)(2,1)}) %all-gather.4.cloned.1.call-update) | async-done | bytes 1048592 | tf_op jit(solution)/shard_map/all_gather | solution.py:175
  89.2 2.2 %fusion.158 = f32[512,768]{0,1:T(8,128)S(1)} fusion(bf16[512,1024]{1,0:T(8,128)(2,1)} %all-gather.4.cloned.1.call-done, bf16[1024,768]{1,0:T(8,128)(2,1)S(1)} %copy-done), kind=kOutput, calls=%fused_computation.212 | convolution fusion | flops 805306368 | bytes 4194304 | tf_op jit(solution)/shard_map/dot_general | solution.py:177
  91.8 1.5 %convert_reduce_fusion = (f32[4,512]{1,0:T(4,128)S(1)}, bf16[4,512,512]{1,2,0:T(8,128)(2,1)S(1)}) fusion(f32[512,512]{0,1:T(8,128)S(1)} %abs_add_fusion, f32[4]{0:T(128)S(1)} %dynamic_slice.12, bf16[512,4,2,64]{0,3,1,2:T(8,128)(2,1)S(1)} %multiply_convert_fusion, pred[512]{0:T(512)(128)(4,1)S(1)} %iota_compare_fusion), kind=kOutput, calls=%fused_computation | convolution fusion | flops 141555712 | bytes 3678736 | tf_op jit(solution)/shard_map/qhd,khd->hqk/dot_general | solution.py:199
  93.9 11.9 %all_to_all.16 = bf16[4,128,256]{1,2,0:T(8,128)(2,1)S(1)} all-to-all(bf16[4,128,256]{1,2,0:T(8,128)(2,1)S(1)} %copy.44), channel_id=1, replica_groups=mesh['groups'=2,'slide'=4,'rep'=2,'section'=2] {'slide'}, dimensions={0} | all-to-all | bytes 524288 | tf_op jit(solution)/shard_map/all_to_all | solution.py:209
  105.7 0.8 copy.45
  (59 shorter events, 7.3 us)
Async XLA Ops:
  7.2 82.1 %copy-start = (bf16[1024,768]{1,0:T(8,128)(2,1)S(1)}, bf16[1024,768]{1,0:T(8,128)(2,1)}, u32[]{:S(2)}) copy-start(bf16[1024,768]{1,0:T(8,128)(2,1)} %param.34) | copy-start | bytes 4718596
  7.2 8.1 %copy-start.2 = (f32[49,1536]{1,0:T(8,128)S(1)}, f32[49,1536]{1,0:T(8,128)}, u32[]{:S(2)}) copy-start(f32[49,1536]{1,0:T(8,128)} %param.20) | copy-start | bytes 903172
  7.2 18.4 %copy-start.7 = (f32[1536]{0:T(1024)S(1)}, f32[1536]{0:T(1024)}, u32[]{:S(2)}) copy-start(f32[1536]{0:T(1024)} %param.25) | copy-start | bytes 18436
  7.2 46.4 %all-gather.6.cloned.1.call-start = ((), (), s32[]{:S(2)}) async-start(), calls=%async_computation.2 | async-start | bytes 1966080 | tf_op jit(solution)/shard_map/all_gather | solution.py:126
  9.2 80.0 %all-gather.4.cloned.1.call-start = ((), (), s32[]{:S(2)}) async-start(), calls=%async_computation.1 | async-start | bytes 1310720 | tf_op jit(solution)/shard_map/all_gather | solution.py:175
  10.6 43.6 %collective-permute-start.3 = (bf16[125,1536]{0,1:T(8,128)(2,1)S(1)}, bf16[125,1536]{0,1:T(8,128)(2,1)}, u32[]{:S(2)}, u32[]{:S(2)}) collective-permute-start(bf16[125,1536]{0,1:T(8,128)(2,1)S(1)} %bitcast.61), channel_id=1, source_target_pairs={{0,1},{1,0},{2,3},{3,2},{4,5},{5,4},{6,7},{7,6},{8,9},{9,8},{10,11... | collective-permute-start | bytes 1152008 | tf_op jit(solution)/shard_map/ppermute | solution.py:130
  23.0 10.8 %copy-start.4 = (f32[1536]{0:T(1024)S(1)}, f32[1536]{0:T(1024)}, u32[]{:S(2)}) copy-start(f32[1536]{0:T(1024)} %param.28) | copy-start | bytes 18436
  23.0 13.9 %collective-permute-start = (bf16[147,1536]{1,0:T(8,128)(2,1)S(1)}, bf16[147,1536]{1,0:T(8,128)(2,1)S(1)}, u32[]{:S(2)}, u32[]{:S(2)}) collective-permute-start(bf16[147,1536]{1,0:T(8,128)(2,1)S(1)} %reshape.166), channel_id=1, source_target_pairs={{0,2},{2,0},{1,3},{3,1},{4,6},{6,4},{5,7},{7,5},{8,10},{10,8},{9,1... | collective-permute-start | bytes 1354760 | tf_op jit(solution)/shard_map/ppermute | solution.py:151
  33.8 14.6 %copy-start.1 = (bf16[1,3,49,1536]{3,2,1,0:T(8,128)(2,1)S(1)}, bf16[1,3,49,1536]{3,2,1,0:T(8,128)(2,1)}, u32[]{:S(2)}) copy-start(bf16[1,3,49,1536]{3,2,1,0:T(8,128)(2,1)} %param.19) | copy-start | bytes 1354756
  46.6 3.9 %collective-permute-start.1 = (f32[3,1536]{1,0:T(4,128)S(1)}, f32[3,1536]{1,0:T(4,128)S(1)}, u32[]{:S(2)}, u32[]{:S(2)}) collective-permute-start(f32[3,1536]{1,0:T(4,128)S(1)} %broadcast_multiply_fusion), channel_id=1, source_target_pairs={{0,2},{2,0},{1,3},{3,1},{4,6},{6,4},{5,7},{7,5},{8,10},{10,8},{9,1... | collective-permute-start | bytes 55304 | tf_op jit(solution)/shard_map/ppermute | solution.py:160
  49.9 8.8 %copy-start.5 = (f32[1024]{0:T(1024)S(1)}, f32[1024]{0:T(1024)}, u32[]{:S(2)}) copy-start(f32[1024]{0:T(1024)} %param.33) | copy-start | bytes 12292
  52.3 7.3 %copy-start.3 = (bf16[3,1536]{1,0:T(4,128)(2,1)}, bf16[3,1536]{1,0:T(4,128)(2,1)S(1)}, u32[]{:S(2)}) copy-start(bf16[3,1536]{1,0:T(4,128)(2,1)S(1)} %add_convert_fusion) | copy-start | bytes 27652
  52.3 1.2 %collective-permute-start.2 = (bf16[3,1536]{1,0:T(4,128)(2,1)S(1)}, bf16[3,1536]{1,0:T(4,128)(2,1)S(1)}, u32[]{:S(2)}, u32[]{:S(2)}) collective-permute-start(bf16[3,1536]{1,0:T(4,128)(2,1)S(1)} %add_convert_fusion), channel_id=1, source_target_pairs={{0,1},{1,0},{2,3},{3,2},{4,5},{5,4},{6,7},{7,6},{8,9},{9,8},{10,11... | collective-permute-start | bytes 27656 | tf_op jit(solution)/shard_map/ppermute | solution.py:167
  54.1 6.2 %copy-start.8 = (f32[16]{0:T(128)S(1)}, f32[16]{0:T(128)}, u32[]{:S(2)}) copy-start(f32[16]{0:T(128)} %param.35) | copy-start | bytes 196
  54.1 6.2 %copy-start.6 = (s32[1,2,512]{2,1,0:T(2,128)S(1)}, s32[1,2,512]{2,1,0:T(2,128)}, u32[]{:S(2)}) copy-start(s32[1,2,512]{2,1,0:T(2,128)} %param.36) | copy-start | bytes 12292
  56.4 2.0 %collective-permute-start.4 = (f32[128,1024]{1,0:T(8,128)S(1)}, f32[128,1024]{1,0:T(8,128)S(1)}, u32[]{:S(2)}, u32[]{:S(2)}) collective-permute-start(f32[128,1024]{1,0:T(8,128)S(1)} %slice.47), channel_id=1, source_target_pairs={{0,1},{1,0},{2,3},{3,2},{4,5},{5,4},{6,7},{7,6},{8,9},{9,8},{10,11... | collective-permute-start | bytes 1572872 | tf_op jit(solution)/shard_map/ppermute | solution.py:93
Sparse Core Ops, SparseCore 0:
  9.6 39.7 all-gather.5
  59.8 29.4 all-gather.3

commit v15 on v13

--- a/solution.py
+++ b/solution.py
@@ -144,7 +144,12 @@
         part = jnp.dot(hidden, down_weight, preferred_element_type=jnp.float32).astype(
             jnp.bfloat16
         )
-        return jnp.sum(part.astype(jnp.float32).reshape(tile_data.shape), axis=1)
+        tiles, per_tile = tile_data.shape[:2]
+        owner = jnp.arange(tiles * per_tile, dtype=jnp.int32) // per_tile
+        pool = (owner[None, :] == jnp.arange(tiles, dtype=jnp.int32)[:, None]).astype(
+            jnp.bfloat16
+        )
+        return jnp.dot(pool, part, preferred_element_type=jnp.float32)
 
     received = [
         lax.ppermute(normed, "rep", perm=[(r, (r + k) % n_rep) for r in range(n_rep)])

time: 110 us -> 113 us (1.027)
  waiting for transfers between devices: 34.9 us -> 39.3 us
  local copies, waits for them, and re-layouts: 11.1 us -> 8.5 us
    ppermute x1, waiting for transfers between devices: 3.11 us -> 6.21 us  [on_device(): lax.ppermute(normed, 'rep', perm=[(r, (r + k) % n_rep) for r in range(n_r...]
    reshape x2 -> x0, local copies, waits for them, and re-layouts: 2.57 us -> none  [block_sums(): return jnp.sum(part.astype(jnp.float32).reshape(tile_data.shape), axis=1)]
    ppermute x1, waiting for transfers between devices: 0.6 us -> 1.95 us  [on_device(): lax.ppermute(term, 'rep', perm=[(r, (r - k) % n_rep) for r in range(n_rep)])]
    dot_general x2 -> x4, matrix products: 16.5 us -> 17.1 us  [the longest x2 10.2 us: block_sums(): jnp.dot(rows, up_weight, preferred_element_type=jnp.float32) + up_bias]
  transfers between devices with their start and end apart: 7 -> 7, of which waited for: 5 -> 5; matrix products, arithmetic and copies ran while one was open for 24% -> 21% of each run, Pallas kernels for 5% -> 5%
where the time goes in v15:
time: 113 us; the launch traced here: 112 us
  waiting for transfers between devices  39.3 us (35%)
  matrix products  23.4 us (21%)
  between operations  15 us (13%)
  blocking collectives  11.9 us (11%)
  local copies, waits for them, and re-layouts  8.5 us (8%)
  Pallas kernels  5.77 us (5%)
  starting transfers between devices  5.21 us (5%)
  other arithmetic  2.95 us (3%)
    all_gather x1, waiting for transfers between devices, on_device(): normed_all = lax.all_gather(normed_seq, 'slide', axis=0, tiled=True)  28.6 us
    all_to_all x1, blocking collectives, on_device(): lax.all_to_all(attended, 'slide', split_axis=0, concat_axis=1, tiled=True)  11.9 us
    dot_general x2, matrix products, block_sums(): jnp.dot(rows, up_weight, preferred_element_type=jnp.float32) + up_bias  10.2 us
    dot_general x2, matrix products, block_sums(): return jnp.dot(pool, part, preferred_element_type=jnp.float32)  6.87 us
    ppermute x1, waiting for transfers between devices, on_device(): lax.ppermute(normed, 'rep', perm=[(r, (r + k) % n_rep) for r in range(n_r...  6.21 us
    pallas_call x1, Pallas kernels, dw_ln(): pl.pallas_call(dw_ln_kernel, grid=(T,), in_specs=[pl.BlockSpec((1, SIDE,...  5.77 us
    ppermute x1, starting transfers between devices, on_device(): lax.ppermute(normed, 'rep', perm=[(r, (r + k) % n_rep) for r in range(n_r...  2.57 us
  transfers between devices with their start and end apart: 7, of which 5 were waited for; matrix products, arithmetic and copies ran while one was open for 21% of the time, Pallas kernels for 5%

profile of v15, /device:TPU:0, one launch (start us, length us, event | category | flops | bytes accessed | tf_op | source)
XLA Modules:
  0.0 112.0 jit_solution(4730534674298640447)
XLA Ops:
  7.3 1.9 %constant_dynamic-slice_fusion = bf16[384,512]{1,0:T(8,128)(2,1)} fusion(bf16[384,1024]{1,0:T(8,128)(2,1)} %param.32, s32[]{:T(128)S(6)} %select_n.42), kind=kLoop, calls=%fused_computation.95 | loop fusion | bytes 786436 | tf_op jit(solution)/shard_map/dynamic_slice | solution.py:122
  9.3 1.1 slice_bitcast_fusion
  10.9 0.7 broadcast_in_dim.38
  13.2 0.9 pad.4.x_ref
  14.0 0.8 pad_maximum_fusion.w_ref
  14.8 5.8 %shard_map.194 = bf16[3,7,8,1536]{3,2,1,0:T(8,128)(2,1)} custom-call(bf16[3,7,8,1536]{3,2,1,0:T(8,128)(2,1)} %pad.4.x_ref, f32[52,1536]{1,0:T(8,128)} %pad_maximum_fusion.w_ref), custom_call_target="tpu_custom_call" | custom-call | tf_op jit(solution)/shard_map/pallas_call | solution.py:58
  20.6 1.2 %reshape.161 = bf16[147,1536]{1,0:T(8,128)(2,1)S(1)} reshape(bf16[3,7,7,1536]{3,2,1,0:T(8,128)(2,1)} %bitcast.52) | data formatting | bytes 903168 | tf_op jit(solution)/shard_map/reshape | solution.py:69
  21.8 2.6 %collective-permute-start = (bf16[147,1536]{1,0:T(8,128)(2,1)S(1)}, bf16[147,1536]{1,0:T(8,128)(2,1)S(1)}, u32[]{:S(2)}, u32[]{:S(2)}) collective-permute-start(bf16[147,1536]{1,0:T(8,128)(2,1)S(1)} %reshape.161), channel_id=1, source_target_pairs={{0,2},{2,0},{1,3},{3,1},{4,6},{6,4},{5,7},{7,5},{8,10},{10,8},{9,1... | collective-permute-start | bytes 1354760 | tf_op jit(solution)/shard_map/ppermute | solution.py:155
  24.4 5.1 %fusion.9 = bf16[147,1536]{1,0:T(8,128)(2,1)S(1)} fusion(bf16[147,1536]{1,0:T(8,128)(2,1)S(1)} %reshape.161, bf16[1536,1536]{1,0:T(8,128)(2,1)} %param.24, f32[1536]{0:T(1024)S(1)} %copy-done.10), kind=kOutput, calls=%fused_computation.24 | convolution fusion | flops 708535296 | bytes 5627904 | tf_op jit(solution)/shard_map/dot_general | solution.py:141
  29.5 6.2 %collective-permute-done = bf16[147,1536]{1,0:T(8,128)(2,1)S(1)} collective-permute-done((bf16[147,1536]{1,0:T(8,128)(2,1)S(1)}, bf16[147,1536]{1,0:T(8,128)(2,1)S(1)}, u32[]{:S(2)}, u32[]{:S(2)}) %collective-permute-start) | collective-permute-done | bytes 451616 | tf_op jit(solution)/shard_map/ppermute | solution.py:155
  35.7 5.1 %fusion.12 = bf16[147,1536]{1,0:T(8,128)(2,1)S(1)} fusion(bf16[147,1536]{1,0:T(8,128)(2,1)S(1)} %collective-permute-done, bf16[1536,1536]{1,0:T(8,128)(2,1)} %param.24, f32[1536]{0:T(1024)S(1)} %copy-done.10), kind=kOutput, calls=%fused_computation.27 | convolution fusion | flops 708535296 | bytes 5627904 | tf_op jit(solution)/shard_map/dot_general | solution.py:141
  40.8 3.4 %convolution_multiply_fusion = f32[3,1536]{1,0:T(4,128)S(1)} fusion(bf16[147,1536]{1,0:T(8,128)(2,1)S(1)} %fusion.12, bf16[1536,1536]{1,0:T(8,128)(2,1)} %param.26, f32[1536]{0:T(1024)S(1)} %broadcast_multiply_fusion, s32[147]{0:T(256)S(1)} %and_select_fusion), kind=kOutput, calls=%fused_computation.6 | convolution fusion | flops 695218624 | bytes 5195340 | tf_op jit(solution)/shard_map/dot_general | solution.py:152
  44.2 1.7 %collective-permute-start.1 = (f32[3,1536]{1,0:T(4,128)S(1)}, f32[3,1536]{1,0:T(4,128)S(1)}, u32[]{:S(2)}, u32[]{:S(2)}) collective-permute-start(f32[3,1536]{1,0:T(4,128)S(1)} %convolution_multiply_fusion), channel_id=1, source_target_pairs={{0,2},{2,0},{1,3},{3,1},{4,6},{6,4},{5,7},{7,5},{8,10},{10,8},{9,1... | collective-permute-start | bytes 55304 | tf_op jit(solution)/shard_map/ppermute | solution.py:164
  46.1 1.9 %collective-permute-done.1 = f32[3,1536]{1,0:T(4,128)S(1)} collective-permute-done((f32[3,1536]{1,0:T(4,128)S(1)}, f32[3,1536]{1,0:T(4,128)S(1)}, u32[]{:S(2)}, u32[]{:S(2)}) %collective-permute-start.1) | collective-permute-done | bytes 18464 | tf_op jit(solution)/shard_map/ppermute | solution.py:164
  48.1 3.5 %fusion.42 = (f32[3]{0:T(128)S(1)}, f32[3,1536]{1,0:T(4,128)S(1)}) fusion(f32[3,1536]{1,0:T(4,128)S(1)} %collective-permute-done.1, f32[1536]{0:T(1024)S(1)} %copy-done.5, bf16[147,1536]{1,0:T(8,128)(2,1)S(1)} %fusion.9, bf16[1536,1536]{1,0:T(8,128)(2,1)} %param.26, s32[147]{0:T(256)S(1)} %and_select_fusion, f32[1536]{0:T(1024)S(1)} %copy-done.3, ...), kind=kOutput, calls=%fused_computation.98 | convolution fusion | flops 695246272 | bytes 5238360 | tf_op jit(solution)/shard_map/dot_general | solution.py:152
  52.0 1.2 %collective-permute-done.2 = bf16[3,1536]{1,0:T(4,128)(2,1)S(1)} collective-permute-done((bf16[3,1536]{1,0:T(4,128)(2,1)S(1)}, bf16[3,1536]{1,0:T(4,128)(2,1)S(1)}, u32[]{:S(2)}, u32[]{:S(2)}) %collective-permute-start.2) | collective-permute-done | bytes 9248 | tf_op jit(solution)/shard_map/ppermute | solution.py:171
  53.1 2.1 %fusion.27 = f32[256,512]{1,0:T(8,128)S(1)} fusion(bf16[1536,512]{1,0:T(8,128)(2,1)} %all-gather.3.cloned.1.call-done, bf16[125,1536]{1,0:T(8,128)(2,1)} %collective-permute-done.3, bf16[3,1536]{1,0:T(4,128)(2,1)S(1)} %collective-permute-done.2, bf16[125,1536]{1,0:T(8,128)(2,1)S(1)} %slice_bitcast_fusion, bf16[3,1536]{1,0:T(4,128)(2,1)S(1)} %add_convert_fusion), kind=kOutput, calls=%fused_computation.58 | convolution fusion | flops 405798912 | bytes 2883584 | tf_op jit(solution)/shard_map/dot_general | solution.py:83
  55.6 1.4 %collective-permute-done.4 = f32[128,512]{1,0:T(8,128)S(1)} collective-permute-done((f32[128,512]{1,0:T(8,128)S(1)}, f32[128,512]{1,0:T(8,128)S(1)}, u32[]{:S(2)}, u32[]{:S(2)}) %collective-permute-start.4) | collective-permute-done | bytes 262176 | tf_op jit(solution)/shard_map/ppermute | solution.py:88
  57.3 0.8 multiply_convert_fusion.1
  59.2 28.6 %all-gather.5.cloned.1.call-done = bf16[512,1024]{1,0:T(8,128)(2,1)} async-done(((bf16[128,1024]{1,0:T(8,128)(2,1)}), bf16[512,1024]{1,0:T(8,128)(2,1)}) %all-gather.5.cloned.1.call-update) | async-done | bytes 1048592 | tf_op jit(solution)/shard_map/all_gather | solution.py:179
  87.8 2.2 %fusion.43 = f32[512,768]{0,1:T(8,128)S(1)} fusion(bf16[512,1024]{1,0:T(8,128)(2,1)} %all-gather.5.cloned.1.call-done, bf16[1024,768]{1,0:T(8,128)(2,1)S(1)} %copy-done), kind=kOutput, calls=%fused_computation.99 | convolution fusion | flops 805306368 | bytes 4194304 | tf_op jit(solution)/shard_map/dot_general | solution.py:181
  90.3 1.5 %convert_reduce_fusion = (f32[4,512]{1,0:T(4,128)S(1)}, bf16[4,512,512]{1,2,0:T(8,128)(2,1)S(1)}) fusion(f32[512,512]{0,1:T(8,128)S(1)} %abs_add_fusion, f32[4]{0:T(128)S(1)} %dynamic_slice.7, bf16[512,4,2,64]{0,3,1,2:T(8,128)(2,1)S(1)} %multiply_convert_fusion, pred[512]{0:T(512)(128)(4,1)S(1)} %iota_compare_fusion.3), kind=kOutput, calls=%fused_computation | convolution fusion | flops 141555712 | bytes 3678736 | tf_op jit(solution)/shard_map/qhd,khd->hqk/dot_general | solution.py:203
  92.4 11.9 %all_to_all.16 = bf16[4,128,256]{1,2,0:T(8,128)(2,1)S(1)} all-to-all(bf16[4,128,256]{1,2,0:T(8,128)(2,1)S(1)} %copy.34), channel_id=1, replica_groups=mesh['groups'=2,'slide'=4,'rep'=2,'section'=2] {'slide'}, dimensions={0} | all-to-all | bytes 524288 | tf_op jit(solution)/shard_map/all_to_all | solution.py:213
  104.3 0.8 copy.35
  (59 shorter events, 4.6 us)
Async XLA Ops:
  7.2 80.6 %copy-start = (bf16[1024,768]{1,0:T(8,128)(2,1)S(1)}, bf16[1024,768]{1,0:T(8,128)(2,1)}, u32[]{:S(2)}) copy-start(bf16[1024,768]{1,0:T(8,128)(2,1)} %param.34) | copy-start | bytes 4718596
  7.2 5.8 %copy-start.1 = (bf16[1,3,49,1536]{3,2,1,0:T(8,128)(2,1)S(1)}, bf16[1,3,49,1536]{3,2,1,0:T(8,128)(2,1)}, u32[]{:S(2)}) copy-start(bf16[1,3,49,1536]{3,2,1,0:T(8,128)(2,1)} %param.19) | copy-start | bytes 1354756
  7.2 6.8 %copy-start.2 = (f32[49,1536]{1,0:T(8,128)S(1)}, f32[49,1536]{1,0:T(8,128)}, u32[]{:S(2)}) copy-start(f32[49,1536]{1,0:T(8,128)} %param.20) | copy-start | bytes 903172
  7.2 45.9 %all-gather.3.cloned.1.call-start = ((), (), s32[]{:S(2)}) async-start(), calls=%async_computation.1 | async-start | bytes 1966080 | tf_op jit(solution)/shard_map/all_gather | solution.py:125
  9.2 78.6 %all-gather.5.cloned.1.call-start = ((), (), s32[]{:S(2)}) async-start(), calls=%async_computation.2 | async-start | bytes 1310720 | tf_op jit(solution)/shard_map/all_gather | solution.py:179
  10.4 42.8 %collective-permute-start.3 = (bf16[125,1536]{1,0:T(8,128)(2,1)S(1)}, bf16[125,1536]{1,0:T(8,128)(2,1)}, u32[]{:S(2)}, u32[]{:S(2)}) collective-permute-start(bf16[125,1536]{1,0:T(8,128)(2,1)S(1)} %slice_bitcast_fusion), channel_id=1, source_target_pairs={{0,1},{1,0},{2,3},{3,2},{4,5},{5,4},{6,7},{7,6},{8,9},{9,8},{10,11... | collective-permute-start | bytes 1152008 | tf_op jit(solution)/shard_map/ppermute | solution.py:129
  13.1 11.2 %copy-start.10 = (f32[1536]{0:T(1024)S(1)}, f32[1536]{0:T(1024)}, u32[]{:S(2)}) copy-start(f32[1536]{0:T(1024)} %param.25) | copy-start | bytes 18436
  21.8 7.7 %copy-start.3 = (f32[1536]{0:T(1024)S(1)}, f32[1536]{0:T(1024)}, u32[]{:S(2)}) copy-start(f32[1536]{0:T(1024)} %param.28) | copy-start | bytes 18436
  21.8 13.9 %collective-permute-start = (bf16[147,1536]{1,0:T(8,128)(2,1)S(1)}, bf16[147,1536]{1,0:T(8,128)(2,1)S(1)}, u32[]{:S(2)}, u32[]{:S(2)}) collective-permute-start(bf16[147,1536]{1,0:T(8,128)(2,1)S(1)} %reshape.161), channel_id=1, source_target_pairs={{0,2},{2,0},{1,3},{3,1},{4,6},{6,4},{5,7},{7,5},{8,10},{10,8},{9,1... | collective-permute-start | bytes 1354760 | tf_op jit(solution)/shard_map/ppermute | solution.py:155
  40.8 7.2 %copy-start.5 = (f32[1536]{0:T(1024)S(1)}, f32[1536]{0:T(1024)}, u32[]{:S(2)}) copy-start(f32[1536]{0:T(1024)} %param.27) | copy-start | bytes 18436
  44.2 3.8 %collective-permute-start.1 = (f32[3,1536]{1,0:T(4,128)S(1)}, f32[3,1536]{1,0:T(4,128)S(1)}, u32[]{:S(2)}, u32[]{:S(2)}) collective-permute-start(f32[3,1536]{1,0:T(4,128)S(1)} %convolution_multiply_fusion), channel_id=1, source_target_pairs={{0,2},{2,0},{1,3},{3,1},{4,6},{6,4},{5,7},{7,5},{8,10},{10,8},{9,1... | collective-permute-start | bytes 55304 | tf_op jit(solution)/shard_map/ppermute | solution.py:164
  46.1 5.7 %copy-start.6 = (f32[1536]{0:T(1024)S(1)}, f32[1536]{0:T(1024)}, u32[]{:S(2)}) copy-start(f32[1536]{0:T(1024)} %param.30) | copy-start | bytes 18436
  46.1 5.7 %copy-start.7 = (f32[1536]{0:T(1024)S(1)}, f32[1536]{0:T(1024)}, u32[]{:S(2)}) copy-start(f32[1536]{0:T(1024)} %param.29) | copy-start | bytes 18436
  51.9 3.4 %copy-start.4 = (bf16[3,1536]{1,0:T(4,128)(2,1)}, bf16[3,1536]{1,0:T(4,128)(2,1)S(1)}, u32[]{:S(2)}) copy-start(bf16[3,1536]{1,0:T(4,128)(2,1)S(1)} %add_convert_fusion) | copy-start | bytes 27652
  51.9 1.2 %collective-permute-start.2 = (bf16[3,1536]{1,0:T(4,128)(2,1)S(1)}, bf16[3,1536]{1,0:T(4,128)(2,1)S(1)}, u32[]{:S(2)}, u32[]{:S(2)}) collective-permute-start(bf16[3,1536]{1,0:T(4,128)(2,1)S(1)} %add_convert_fusion), channel_id=1, source_target_pairs={{0,1},{1,0},{2,3},{3,2},{4,5},{5,4},{6,7},{7,6},{8,9},{9,8},{10,11... | collective-permute-start | bytes 27656 | tf_op jit(solution)/shard_map/ppermute | solution.py:171
  55.3 2.0 %copy-start.8 = (f32[1024]{0:T(1024)S(1)}, f32[1024]{0:T(1024)}, u32[]{:S(2)}) copy-start(f32[1024]{0:T(1024)} %param.33) | copy-start | bytes 12292
  55.3 3.5 %copy-start.11 = (f32[16]{0:T(128)S(1)}, f32[16]{0:T(128)}, u32[]{:S(2)}) copy-start(f32[16]{0:T(128)} %param.35) | copy-start | bytes 196
  55.3 3.6 %copy-start.9 = (s32[1,2,512]{2,1,0:T(2,128)S(1)}, s32[1,2,512]{2,1,0:T(2,128)}, u32[]{:S(2)}) copy-start(s32[1,2,512]{2,1,0:T(2,128)} %param.36) | copy-start | bytes 12292
  55.4 1.6 %collective-permute-start.4 = (f32[128,512]{1,0:T(8,128)S(1)}, f32[128,512]{1,0:T(8,128)S(1)}, u32[]{:S(2)}, u32[]{:S(2)}) collective-permute-start(f32[128,512]{1,0:T(8,128)S(1)} %get-tuple-element.10), channel_id=1, source_target_pairs={{0,1},{1,0},{2,3},{3,2},{4,5},{5,4},{6,7},{7,6},{8,9},{9,8},{10,11... | collective-permute-start | bytes 786440 | tf_op jit(solution)/shard_map/ppermute | solution.py:88
Sparse Core Ops, SparseCore 0:
  9.6 39.7 all-gather.2
  58.3 29.4 all-gather.4

commit v16 on v13

--- a/solution.py
+++ b/solution.py
@@ -126,7 +126,6 @@
 
     sec_swap = [(c, (c + 1) % n_sec) for c in range(n_sec)]
     fresh_count = tile_features.shape[1]
-    partner_stored = lax.ppermute(embed_store[0, fresh_count:], "section", perm=sec_swap)
 
     tile_data = tile_features[0].astype(jnp.float32)
     fresh_count = tile_data.shape[0]
@@ -154,6 +153,8 @@
     own_term = jnp.mean(tile_data, axis=1) + layer_scale * (
         block_sums(normed) / positions + down_bias
     )
+    stored, own_term = lax.optimization_barrier((embed_store[0, fresh_count:], own_term))
+    partner_stored = lax.ppermute(stored, "section", perm=sec_swap)
     peer_terms = [layer_scale * (block_sums(rows) / positions) for rows in received]
     returned = [
         lax.ppermute(term, "rep", perm=[(r, (r - k) % n_rep) for r in range(n_rep)])

time: 110 us -> 109 us (level)
  other arithmetic: 3.24 us -> 5.92 us
  waiting for transfers between devices: 34.9 us -> 32.6 us
  matrix products: 22.8 us -> 21.2 us
    ppermute x1, waiting for transfers between devices: 3.11 us -> 0.17 us  [on_device(): lax.ppermute(normed, 'rep', perm=[(r, (r + k) % n_rep) for r in range(n_r...]
    reshape x2, local copies, waits for them, and re-layouts: 2.57 us -> 0.21 us  [block_sums(): return jnp.sum(part.astype(jnp.float32).reshape(tile_data.shape), axis=1)]
    dot_general x2, matrix products: 16.5 us -> 14.9 us  [block_sums(): jnp.dot(hidden, down_weight, preferred_element_type=jnp.float32)]
  transfers between devices with their start and end apart: 7 -> 7, of which waited for: 5 -> 5; matrix products, arithmetic and copies ran while one was open for 24% -> 25% of each run, Pallas kernels for 5% -> 5%
where the time goes in v16:
time: 109 us
  waiting for transfers between devices  32.6 us (30%)
  matrix products  21.2 us (19%)
  between operations  15 us (14%)
  blocking collectives  11.9 us (11%)
  local copies, waits for them, and re-layouts  11.3 us (10%)
  other arithmetic  5.92 us (5%)
  Pallas kernels  5.76 us (5%)
  starting transfers between devices  5.15 us (5%)
    all_gather x1, waiting for transfers between devices, on_device(): normed_all = lax.all_gather(normed_seq, 'slide', axis=0, tiled=True)  28.6 us
    dot_general x2, matrix products, block_sums(): jnp.dot(hidden, down_weight, preferred_element_type=jnp.float32)  14.9 us
    all_to_all x1, blocking collectives, on_device(): lax.all_to_all(attended, 'slide', split_axis=0, concat_axis=1, tiled=True)  11.9 us
    pallas_call x1, Pallas kernels, dw_ln(): pl.pallas_call(dw_ln_kernel, grid=(T,), in_specs=[pl.BlockSpec((1, SIDE,...  5.76 us
    ppermute x1, starting transfers between devices, on_device(): lax.ppermute(normed, 'rep', perm=[(r, (r + k) % n_rep) for r in range(n_r...  2.89 us
    dot_general x1, matrix products, on_device(): jnp.dot(normed_all, qkv_weight, preferred_element_type=jnp.float32)  2.24 us
  transfers between devices with their start and end apart: 7, of which 5 were waited for; matrix products, arithmetic and copies ran while one was open for 25% of the time, Pallas kernels for 5%

profile of v16, /device:TPU:0, one launch (start us, length us, event | category | flops | bytes accessed | tf_op | source)
XLA Modules:
  0.0 108.7 jit_solution(3680275187694525302)
XLA Ops:
  7.2 1.9 %constant_dynamic-slice_fusion = bf16[384,512]{1,0:T(8,128)(2,1)} fusion(bf16[384,1024]{1,0:T(8,128)(2,1)} %param.32, s32[]{:T(128)S(6)} %select_n.30), kind=kLoop, calls=%fused_computation.148 | loop fusion | bytes 786436 | tf_op jit(solution)/shard_map/dynamic_slice | solution.py:122
  11.3 1.2 %reshape_squeeze.3 = bf16[3,7,7,1536]{3,2,1,0:T(8,128)(2,1)S(1)} reshape(bf16[1,3,49,1536]{3,2,1,0:T(8,128)(2,1)} %param.19) | data formatting | bytes 903168 | tf_op jit(solution)/shard_map/reshape;squeeze | solution.py:57
  12.6 0.9 pad.4.x_ref
  13.5 0.8 pad_maximum_fusion.w_ref
  14.2 5.8 %shard_map.194 = bf16[3,7,8,1536]{3,2,1,0:T(8,128)(2,1)} custom-call(bf16[3,7,8,1536]{3,2,1,0:T(8,128)(2,1)} %pad.4.x_ref, f32[52,1536]{1,0:T(8,128)} %pad_maximum_fusion.w_ref), custom_call_target="tpu_custom_call" | custom-call | tf_op jit(solution)/shard_map/pallas_call | solution.py:58
  20.0 2.0 %reshape.160 = bf16[147,1536]{1,0:T(8,128)(2,1)} reshape(bf16[3,7,7,1536]{3,2,1,0:T(8,128)(2,1)} %bitcast.50) | data formatting | bytes 903168 | tf_op jit(solution)/shard_map/reshape | solution.py:69
  22.0 2.9 %collective-permute-start = (bf16[147,1536]{1,0:T(8,128)(2,1)}, bf16[147,1536]{1,0:T(8,128)(2,1)}, u32[]{:S(2)}, u32[]{:S(2)}) collective-permute-start(bf16[147,1536]{1,0:T(8,128)(2,1)} %reshape.160), channel_id=1, source_target_pairs={{0,2},{2,0},{1,3},{3,1},{4,6},{6,4},{5,7},{7,5},{8,10},{10,8},{9,1... | collective-permute-start | bytes 1354760 | tf_op jit(solution)/shard_map/ppermute | solution.py:149
  24.9 0.7 convert_reduce_fusion.1
  25.6 7.4 %fusion.1 = f32[147,1536]{1,0:T(8,128)S(1)} fusion(bf16[1536,1536]{1,0:T(8,128)(2,1)} %param.26, bf16[147,1536]{1,0:T(8,128)(2,1)} %reshape.160, bf16[1536,1536]{1,0:T(8,128)(2,1)} %param.24, f32[1536]{0:T(1024)S(1)} %copy-done.7), kind=kOutput, calls=%fused_computation.7 | convolution fusion | flops 1402619904 | bytes 10798080 | tf_op jit(solution)/shard_map/dot_general | solution.py:143
  33.9 1.9 %slice_bitcast_fusion = bf16[125,1536]{1,0:T(8,128)(2,1)} fusion(bf16[1,128,1536]{2,1,0:T(8,128)(2,1)} %param.31), kind=kLoop, calls=%fused_computation.128 | loop fusion | bytes 768000 | tf_op jit(solution)/shard_map/squeeze | solution.py:156
  35.9 7.5 %fusion = f32[147,1536]{1,0:T(8,128)S(1)} fusion(bf16[1536,1536]{1,0:T(8,128)(2,1)} %param.26, bf16[147,1536]{1,0:T(8,128)(2,1)} %collective-permute-done, bf16[1536,1536]{1,0:T(8,128)(2,1)} %param.24, f32[1536]{0:T(1024)} %param.25), kind=kOutput, calls=%fused_computation.5 | convolution fusion | flops 1402619904 | bytes 10798080 | tf_op jit(solution)/shard_map/dot_general | solution.py:143
  43.6 1.8 %collective-permute-start.1 = (f32[3,1536]{1,0:T(4,128)S(1)}, f32[3,1536]{1,0:T(4,128)S(1)}, u32[]{:S(2)}, u32[]{:S(2)}) collective-permute-start(f32[3,1536]{1,0:T(4,128)S(1)} %broadcast_multiply_fusion), channel_id=1, source_target_pairs={{0,2},{2,0},{1,3},{3,1},{4,6},{6,4},{5,7},{7,5},{8,10},{10,8},{9,1... | collective-permute-start | bytes 55304 | tf_op jit(solution)/shard_map/ppermute | solution.py:160
  45.4 0.8 multiply_add_fusion
  46.3 1.2 %collective-permute-done.1 = f32[3,1536]{1,0:T(4,128)S(1)} collective-permute-done((f32[3,1536]{1,0:T(4,128)S(1)}, f32[3,1536]{1,0:T(4,128)S(1)}, u32[]{:S(2)}, u32[]{:S(2)}) %collective-permute-start.1) | collective-permute-done | bytes 18464 | tf_op jit(solution)/shard_map/ppermute | solution.py:160
  47.8 0.8 add_convert_fusion
  48.7 1.2 %collective-permute-done.2 = bf16[3,1536]{1,0:T(4,128)(2,1)S(1)} collective-permute-done((bf16[3,1536]{1,0:T(4,128)(2,1)S(1)}, bf16[3,1536]{1,0:T(4,128)(2,1)S(1)}, u32[]{:S(2)}, u32[]{:S(2)}) %collective-permute-start.2) | collective-permute-done | bytes 9248 | tf_op jit(solution)/shard_map/ppermute | solution.py:167
  49.9 2.1 %fusion.25 = f32[256,512]{1,0:T(8,128)S(1)} fusion(bf16[1536,512]{1,0:T(8,128)(2,1)} %all-gather.3.cloned.1.call-done, bf16[125,1536]{1,0:T(8,128)(2,1)S(1)} %collective-permute-done.3, bf16[3,1536]{1,0:T(4,128)(2,1)S(1)} %collective-permute-done.2, bf16[125,1536]{1,0:T(8,128)(2,1)} %slice_bitcast_fusion, bf16[3,1536]{1,0:T(4,128)(2,1)S(1)} %add_convert_fusion), kind=kOutput, calls=%fused_computation.54 | convolution fusion | flops 405798912 | bytes 2883584 | tf_op jit(solution)/shard_map/dot_general | solution.py:83
  52.3 1.4 %collective-permute-done.4 = f32[128,512]{1,0:T(8,128)S(1)} collective-permute-done((f32[128,512]{1,0:T(8,128)S(1)}, f32[128,512]{1,0:T(8,128)S(1)}, u32[]{:S(2)}, u32[]{:S(2)}) %collective-permute-start.4) | collective-permute-done | bytes 262176 | tf_op jit(solution)/shard_map/ppermute | solution.py:88
  54.1 0.8 multiply_convert_fusion.1
  55.9 28.6 %all-gather.5.cloned.1.call-done = bf16[512,1024]{1,0:T(8,128)(2,1)} async-done(((bf16[128,1024]{1,0:T(8,128)(2,1)}), bf16[512,1024]{1,0:T(8,128)(2,1)}) %all-gather.5.cloned.1.call-update) | async-done | bytes 1048592 | tf_op jit(solution)/shard_map/all_gather | solution.py:175
  84.5 2.2 %fusion.161 = f32[512,768]{0,1:T(8,128)S(1)} fusion(bf16[512,1024]{1,0:T(8,128)(2,1)} %all-gather.5.cloned.1.call-done, bf16[1024,768]{1,0:T(8,128)(2,1)S(1)} %copy-done), kind=kOutput, calls=%fused_computation.212 | convolution fusion | flops 805306368 | bytes 4194304 | tf_op jit(solution)/shard_map/dot_general | solution.py:177
  87.1 1.5 %convert_reduce_fusion = (f32[4,512]{1,0:T(4,128)S(1)}, bf16[4,512,512]{1,2,0:T(8,128)(2,1)S(1)}) fusion(f32[512,512]{0,1:T(8,128)S(1)} %abs_add_fusion, f32[4]{0:T(128)S(1)} %dynamic_slice.7, bf16[512,4,2,64]{0,3,1,2:T(8,128)(2,1)S(1)} %multiply_convert_fusion, pred[512]{0:T(512)(128)(4,1)S(1)} %iota_compare_fusion), kind=kOutput, calls=%fused_computation | convolution fusion | flops 141555712 | bytes 3678736 | tf_op jit(solution)/shard_map/qhd,khd->hqk/dot_general | solution.py:199
  89.2 11.9 %all_to_all.16 = bf16[4,128,256]{1,2,0:T(8,128)(2,1)S(1)} all-to-all(bf16[4,128,256]{1,2,0:T(8,128)(2,1)S(1)} %copy.34), channel_id=1, replica_groups=mesh['groups'=2,'slide'=4,'rep'=2,'section'=2] {'slide'}, dimensions={0} | all-to-all | bytes 524288 | tf_op jit(solution)/shard_map/all_to_all | solution.py:209
  101.0 0.8 copy.35
  (57 shorter events, 5.7 us)
Async XLA Ops:
  7.2 77.4 %copy-start = (bf16[1024,768]{1,0:T(8,128)(2,1)S(1)}, bf16[1024,768]{1,0:T(8,128)(2,1)}, u32[]{:S(2)}) copy-start(bf16[1024,768]{1,0:T(8,128)(2,1)} %param.34) | copy-start | bytes 4718596
  7.2 6.3 %copy-start.2 = (f32[49,1536]{1,0:T(8,128)S(1)}, f32[49,1536]{1,0:T(8,128)}, u32[]{:S(2)}) copy-start(f32[49,1536]{1,0:T(8,128)} %param.20) | copy-start | bytes 903172
  7.2 42.7 %all-gather.3.cloned.1.call-start = ((), (), s32[]{:S(2)}) async-start(), calls=%async_computation.1 | async-start | bytes 1966080 | tf_op jit(solution)/shard_map/all_gather | solution.py:125
  9.2 75.4 %all-gather.5.cloned.1.call-start = ((), (), s32[]{:S(2)}) async-start(), calls=%async_computation.2 | async-start | bytes 1310720 | tf_op jit(solution)/shard_map/all_gather | solution.py:175
  12.5 12.4 %copy-start.1 = (bf16[1,3,49,1536]{3,2,1,0:T(8,128)(2,1)S(1)}, bf16[1,3,49,1536]{3,2,1,0:T(8,128)(2,1)}, u32[]{:S(2)}) copy-start(bf16[1,3,49,1536]{3,2,1,0:T(8,128)(2,1)} %param.19) | copy-start | bytes 1354756
  12.5 13.1 %copy-start.3 = (f32[1536]{0:T(1024)S(1)}, f32[1536]{0:T(1024)}, u32[]{:S(2)}) copy-start(f32[1536]{0:T(1024)} %param.28) | copy-start | bytes 18436
  13.5 12.2 %copy-start.7 = (f32[1536]{0:T(1024)S(1)}, f32[1536]{0:T(1024)}, u32[]{:S(2)}) copy-start(f32[1536]{0:T(1024)} %param.25) | copy-start | bytes 18436
  22.0 13.9 %collective-permute-start = (bf16[147,1536]{1,0:T(8,128)(2,1)}, bf16[147,1536]{1,0:T(8,128)(2,1)}, u32[]{:S(2)}, u32[]{:S(2)}) collective-permute-start(bf16[147,1536]{1,0:T(8,128)(2,1)} %reshape.160), channel_id=1, source_target_pairs={{0,2},{2,0},{1,3},{3,1},{4,6},{6,4},{5,7},{7,5},{8,10},{10,8},{9,1... | collective-permute-start | bytes 1354760 | tf_op jit(solution)/shard_map/ppermute | solution.py:149
  43.6 3.9 %collective-permute-start.1 = (f32[3,1536]{1,0:T(4,128)S(1)}, f32[3,1536]{1,0:T(4,128)S(1)}, u32[]{:S(2)}, u32[]{:S(2)}) collective-permute-start(f32[3,1536]{1,0:T(4,128)S(1)} %broadcast_multiply_fusion), channel_id=1, source_target_pairs={{0,2},{2,0},{1,3},{3,1},{4,6},{6,4},{5,7},{7,5},{8,10},{10,8},{9,1... | collective-permute-start | bytes 55304 | tf_op jit(solution)/shard_map/ppermute | solution.py:160
  46.2 3.7 %collective-permute-start.3 = (bf16[125,1536]{1,0:T(8,128)(2,1)}, bf16[125,1536]{1,0:T(8,128)(2,1)S(1)}, u32[]{:S(2)}, u32[]{:S(2)}) collective-permute-start(bf16[125,1536]{1,0:T(8,128)(2,1)} %slice_bitcast_fusion), channel_id=1, source_target_pairs={{0,1},{1,0},{2,3},{3,2},{4,5},{5,4},{6,7},{7,6},{8,9},{9,8},{10,11... | collective-permute-start | bytes 1152008 | tf_op jit(solution)/shard_map/ppermute | solution.py:157
  48.6 3.4 %copy-start.4 = (bf16[3,1536]{1,0:T(4,128)(2,1)}, bf16[3,1536]{1,0:T(4,128)(2,1)S(1)}, u32[]{:S(2)}) copy-start(bf16[3,1536]{1,0:T(4,128)(2,1)S(1)} %add_convert_fusion) | copy-start | bytes 27652
  48.6 1.2 %collective-permute-start.2 = (bf16[3,1536]{1,0:T(4,128)(2,1)S(1)}, bf16[3,1536]{1,0:T(4,128)(2,1)S(1)}, u32[]{:S(2)}, u32[]{:S(2)}) collective-permute-start(bf16[3,1536]{1,0:T(4,128)(2,1)S(1)} %add_convert_fusion), channel_id=1, source_target_pairs={{0,1},{1,0},{2,3},{3,2},{4,5},{5,4},{6,7},{7,6},{8,9},{9,8},{10,11... | collective-permute-start | bytes 27656 | tf_op jit(solution)/shard_map/ppermute | solution.py:167
  52.0 2.0 %copy-start.5 = (f32[1024]{0:T(1024)S(1)}, f32[1024]{0:T(1024)}, u32[]{:S(2)}) copy-start(f32[1024]{0:T(1024)} %param.33) | copy-start | bytes 12292
  52.0 3.5 %copy-start.8 = (f32[16]{0:T(128)S(1)}, f32[16]{0:T(128)}, u32[]{:S(2)}) copy-start(f32[16]{0:T(128)} %param.35) | copy-start | bytes 196
  52.1 3.6 %copy-start.6 = (s32[1,2,512]{2,1,0:T(2,128)S(1)}, s32[1,2,512]{2,1,0:T(2,128)}, u32[]{:S(2)}) copy-start(s32[1,2,512]{2,1,0:T(2,128)} %param.36) | copy-start | bytes 12292
  52.1 1.6 %collective-permute-start.4 = (f32[128,512]{1,0:T(8,128)S(1)}, f32[128,512]{1,0:T(8,128)S(1)}, u32[]{:S(2)}, u32[]{:S(2)}) collective-permute-start(f32[128,512]{1,0:T(8,128)S(1)} %get-tuple-element.16), channel_id=1, source_target_pairs={{0,1},{1,0},{2,3},{3,2},{4,5},{5,4},{6,7},{7,6},{8,9},{9,8},{10,11... | collective-permute-start | bytes 786440 | tf_op jit(solution)/shard_map/ppermute | solution.py:88
Sparse Core Ops, SparseCore 0:
  9.6 39.7 all-gather.2
  55.1 29.4 all-gather.4

commit v17 on v16

--- a/solution.py
+++ b/solution.py
@@ -80,14 +80,11 @@
 
 def project(rows, partner_rows, cols, slide_gain):
     n_sec = lax.axis_size("section")
-    both = jnp.dot(
-        jnp.concatenate([rows, partner_rows], axis=0), cols, preferred_element_type=jnp.float32
-    )
-    count = rows.shape[0]
-    mine = both[:count]
+    for_partner = jnp.dot(partner_rows, cols, preferred_element_type=jnp.float32)
     from_partner = lax.ppermute(
-        both[count:], "section", perm=[(c, (c + 1) % n_sec) for c in range(n_sec)]
-    )
+        for_partner, "section", perm=[(c, (c + 1) % n_sec) for c in range(n_sec)]
+    )
+    mine = jnp.dot(rows, cols, preferred_element_type=jnp.float32)
     projected = jnp.where(
         lax.axis_index("section") == 0,
         jnp.concatenate([mine, from_partner], axis=-1),

time: 109 us -> 112 us (1.028)
  matrix products: 21.2 us -> 23.6 us
    dot_general x1 -> x2, matrix products: 2.12 us -> 3.57 us  [the longest x1 1.79 us: project(): jnp.dot(partner_rows, cols, preferred_element_type=jnp.float32)]
    ppermute x1, waiting for transfers between devices: 1.37 us -> 0.01 us  [project(): lax.ppermute(for_partner, 'section', perm=[(c, (c + 1) % n_sec) for c in...]
    ppermute x1, waiting for transfers between devices: 0.17 us -> 1.45 us  [on_device(): lax.ppermute(normed, 'rep', perm=[(r, (r + k) % n_rep) for r in range(n_r...]
    reshape x2, local copies, waits for them, and re-layouts: 0.21 us -> 1.4 us  [block_sums(): return jnp.sum(part.astype(jnp.float32).reshape(tile_data.shape), axis=1)]
  transfers between devices with their start and end apart: 7 -> 7, of which waited for: 5 -> 4; matrix products, arithmetic and copies ran while one was open for 25% -> 27% of each run, Pallas kernels for 5% -> 5%
where the time goes in v17:
time: 112 us; the launch traced here: 111 us
  waiting for transfers between devices  33.2 us (30%)
  matrix products  23.6 us (21%)
  between operations  15 us (13%)
  blocking collectives  11.9 us (11%)
  local copies, waits for them, and re-layouts  11.6 us (10%)
  Pallas kernels  5.76 us (5%)
  starting transfers between devices  5.21 us (5%)
  other arithmetic  4.86 us (4%)
    all_gather x1, waiting for transfers between devices, on_device(): normed_all = lax.all_gather(normed_seq, 'slide', axis=0, tiled=True)  28.6 us
    dot_general x2, matrix products, block_sums(): jnp.dot(hidden, down_weight, preferred_element_type=jnp.float32)  15.9 us
    all_to_all x1, blocking collectives, on_device(): lax.all_to_all(attended, 'slide', split_axis=0, concat_axis=1, tiled=True)  11.9 us
    pallas_call x1, Pallas kernels, dw_ln(): pl.pallas_call(dw_ln_kernel, grid=(T,), in_specs=[pl.BlockSpec((1, SIDE,...  5.76 us
    ppermute x1, starting transfers between devices, on_device(): lax.ppermute(normed, 'rep', perm=[(r, (r + k) % n_rep) for r in range(n_r...  2.94 us
    dot_general x1, matrix products, on_device(): jnp.dot(normed_all, qkv_weight, preferred_element_type=jnp.float32)  2.24 us
  transfers between devices with their start and end apart: 7, of which 4 were waited for; matrix products, arithmetic and copies ran while one was open for 27% of the time, Pallas kernels for 5%

profile of v17, /device:TPU:0, one launch (start us, length us, event | category | flops | bytes accessed | tf_op | source)
XLA Modules:
  0.0 111.1 jit_solution(1373328841676220328)
XLA Ops:
  7.3 1.9 %constant_dynamic-slice_fusion = bf16[384,512]{1,0:T(8,128)(2,1)} fusion(bf16[384,1024]{1,0:T(8,128)(2,1)} %param.32, s32[]{:T(128)S(6)} %select_n.30), kind=kLoop, calls=%fused_computation.148 | loop fusion | bytes 786436 | tf_op jit(solution)/shard_map/dynamic_slice | solution.py:119
  11.3 1.2 %reshape_squeeze.3 = bf16[3,7,7,1536]{3,2,1,0:T(8,128)(2,1)S(1)} reshape(bf16[1,3,49,1536]{3,2,1,0:T(8,128)(2,1)} %param.19) | data formatting | bytes 903168 | tf_op jit(solution)/shard_map/reshape;squeeze | solution.py:57
  12.5 0.9 pad.4.x_ref
  13.4 1.8 %pad_maximum_fusion.w_ref = f32[52,1536]{1,0:T(8,128)} fusion(f32[1,1536]{1,0:T(1,128)S(1)} %broadcast_in_dim.44, f32[1,1536]{1,0:T(1,128)S(1)} %broadcast_in_dim.43, f32[1,1536]{1,0:T(1,128)S(1)} %broadcast_in_dim.42, f32[49,1536]{1,0:T(8,128)} %param.20), kind=kLoop, calls=%fused_computation.129 | loop fusion | flops 239616 | bytes 638976 | tf_op jit(solution)/shard_map/concatenate | solution.py:68
  15.2 5.8 %shard_map.194 = bf16[3,7,8,1536]{3,2,1,0:T(8,128)(2,1)} custom-call(bf16[3,7,8,1536]{3,2,1,0:T(8,128)(2,1)} %pad.4.x_ref, f32[52,1536]{1,0:T(8,128)} %pad_maximum_fusion.w_ref), custom_call_target="tpu_custom_call" | custom-call | tf_op jit(solution)/shard_map/pallas_call | solution.py:58
  20.9 2.0 %reshape.160 = bf16[147,1536]{1,0:T(8,128)(2,1)} reshape(bf16[3,7,7,1536]{3,2,1,0:T(8,128)(2,1)} %bitcast.51) | data formatting | bytes 903168 | tf_op jit(solution)/shard_map/reshape | solution.py:69
  22.9 2.9 %collective-permute-start = (bf16[147,1536]{1,0:T(8,128)(2,1)}, bf16[147,1536]{1,0:T(8,128)(2,1)}, u32[]{:S(2)}, u32[]{:S(2)}) collective-permute-start(bf16[147,1536]{1,0:T(8,128)(2,1)} %reshape.160), channel_id=1, source_target_pairs={{0,2},{2,0},{1,3},{3,1},{4,6},{6,4},{5,7},{7,5},{8,10},{10,8},{9,1... | collective-permute-start | bytes 1354760 | tf_op jit(solution)/shard_map/ppermute | solution.py:146
  25.8 0.7 convert_reduce_fusion.1
  26.6 7.5 %fusion.1 = f32[147,1536]{1,0:T(8,128)S(1)} fusion(bf16[1536,1536]{1,0:T(8,128)(2,1)} %param.26, bf16[147,1536]{1,0:T(8,128)(2,1)} %reshape.160, bf16[1536,1536]{1,0:T(8,128)(2,1)} %param.24, f32[1536]{0:T(1024)} %param.25), kind=kOutput, calls=%fused_computation.7 | convolution fusion | flops 1402619904 | bytes 10798080 | tf_op jit(solution)/shard_map/dot_general | solution.py:140
  34.2 1.1 slice_bitcast_fusion
  35.4 1.4 %collective-permute-done = bf16[147,1536]{1,0:T(8,128)(2,1)} collective-permute-done((bf16[147,1536]{1,0:T(8,128)(2,1)}, bf16[147,1536]{1,0:T(8,128)(2,1)}, u32[]{:S(2)}, u32[]{:S(2)}) %collective-permute-start) | collective-permute-done | bytes 451616 | tf_op jit(solution)/shard_map/ppermute | solution.py:146
  36.8 8.4 %fusion = f32[147,1536]{1,0:T(8,128)} fusion(bf16[1536,1536]{1,0:T(8,128)(2,1)} %param.26, bf16[147,1536]{1,0:T(8,128)(2,1)} %collective-permute-done, bf16[1536,1536]{1,0:T(8,128)(2,1)} %param.24, f32[1536]{0:T(1024)} %param.25), kind=kOutput, calls=%fused_computation.5 | convolution fusion | flops 1402619904 | bytes 10798080 | tf_op jit(solution)/shard_map/dot_general | solution.py:140
  45.3 1.3 %reshape.169 = f32[3,49,1536]{2,1,0:T(8,128)S(1)} reshape(f32[147,1536]{1,0:T(8,128)} %fusion) | data formatting | bytes 1806336 | tf_op jit(solution)/shard_map/reshape | solution.py:143
  46.7 1.8 %collective-permute-start.1 = (f32[3,1536]{1,0:T(4,128)S(1)}, f32[3,1536]{1,0:T(4,128)S(1)}, u32[]{:S(2)}, u32[]{:S(2)}) collective-permute-start(f32[3,1536]{1,0:T(4,128)S(1)} %broadcast_multiply_fusion), channel_id=1, source_target_pairs={{0,2},{2,0},{1,3},{3,1},{4,6},{6,4},{5,7},{7,5},{8,10},{10,8},{9,1... | collective-permute-start | bytes 55304 | tf_op jit(solution)/shard_map/ppermute | solution.py:157
  48.6 2.0 %collective-permute-done.1 = f32[3,1536]{1,0:T(4,128)S(1)} collective-permute-done((f32[3,1536]{1,0:T(4,128)S(1)}, f32[3,1536]{1,0:T(4,128)S(1)}, u32[]{:S(2)}, u32[]{:S(2)}) %collective-permute-start.1) | collective-permute-done | bytes 18464 | tf_op jit(solution)/shard_map/ppermute | solution.py:157
  51.1 1.2 %collective-permute-done.2 = bf16[3,1536]{1,0:T(4,128)(2,1)S(1)} collective-permute-done((bf16[3,1536]{1,0:T(4,128)(2,1)S(1)}, bf16[3,1536]{1,0:T(4,128)(2,1)S(1)}, u32[]{:S(2)}, u32[]{:S(2)}) %collective-permute-start.2) | collective-permute-done | bytes 9248 | tf_op jit(solution)/shard_map/ppermute | solution.py:164
  52.3 1.8 %fusion.91 = f32[128,512]{1,0:T(8,128)S(1)} fusion(bf16[1536,512]{1,0:T(8,128)(2,1)} %all-gather.3.cloned.1.call-done, bf16[125,1536]{1,0:T(8,128)(2,1)S(1)} %collective-permute-done.3, bf16[3,1536]{1,0:T(4,128)(2,1)S(1)} %collective-permute-done.2), kind=kOutput, calls=%fused_computation.124 | convolution fusion | flops 202113024 | bytes 2228224 | tf_op jit(solution)/shard_map/dot_general | solution.py:83
  54.3 1.8 %fusion.87 = f32[128,512]{1,0:T(8,128)S(1)} fusion(bf16[1536,512]{1,0:T(8,128)(2,1)} %all-gather.3.cloned.1.call-done, bf16[125,1536]{1,0:T(8,128)(2,1)S(1)} %slice_bitcast_fusion, bf16[3,1536]{1,0:T(4,128)(2,1)S(1)} %add_convert_fusion), kind=kOutput, calls=%fused_computation.120 | convolution fusion | flops 202113024 | bytes 2228224 | tf_op jit(solution)/shard_map/dot_general | solution.py:87
  56.5 0.8 multiply_convert_fusion.1
  58.3 28.6 %all-gather.5.cloned.1.call-done = bf16[512,1024]{1,0:T(8,128)(2,1)} async-done(((bf16[128,1024]{1,0:T(8,128)(2,1)}), bf16[512,1024]{1,0:T(8,128)(2,1)}) %all-gather.5.cloned.1.call-update) | async-done | bytes 1048592 | tf_op jit(solution)/shard_map/all_gather | solution.py:172
  86.9 2.2 %fusion.161 = f32[512,768]{0,1:T(8,128)S(1)} fusion(bf16[512,1024]{1,0:T(8,128)(2,1)} %all-gather.5.cloned.1.call-done, bf16[1024,768]{1,0:T(8,128)(2,1)S(1)} %copy-done), kind=kOutput, calls=%fused_computation.212 | convolution fusion | flops 805306368 | bytes 4194304 | tf_op jit(solution)/shard_map/dot_general | solution.py:174
  89.5 1.5 %convert_reduce_fusion = (f32[4,512]{1,0:T(4,128)S(1)}, bf16[4,512,512]{1,2,0:T(8,128)(2,1)S(1)}) fusion(f32[512,512]{0,1:T(8,128)S(1)} %abs_add_fusion, f32[4]{0:T(128)S(1)} %dynamic_slice.7, bf16[512,4,2,64]{0,3,1,2:T(8,128)(2,1)S(1)} %multiply_convert_fusion, pred[512]{0:T(512)(128)(4,1)S(1)} %iota_compare_fusion), kind=kOutput, calls=%fused_computation | convolution fusion | flops 141555712 | bytes 3678736 | tf_op jit(solution)/shard_map/qhd,khd->hqk/dot_general | solution.py:196
  91.6 11.9 %all_to_all.16 = bf16[4,128,256]{1,2,0:T(8,128)(2,1)S(1)} all-to-all(bf16[4,128,256]{1,2,0:T(8,128)(2,1)S(1)} %copy.34), channel_id=1, replica_groups=mesh['groups'=2,'slide'=4,'rep'=2,'section'=2] {'slide'}, dimensions={0} | all-to-all | bytes 524288 | tf_op jit(solution)/shard_map/all_to_all | solution.py:206
  103.5 0.8 copy.35
  (61 shorter events, 4.9 us)
Async XLA Ops:
  7.2 79.8 %copy-start = (bf16[1024,768]{1,0:T(8,128)(2,1)S(1)}, bf16[1024,768]{1,0:T(8,128)(2,1)}, u32[]{:S(2)}) copy-start(bf16[1024,768]{1,0:T(8,128)(2,1)} %param.34) | copy-start | bytes 4718596
  7.2 18.7 %copy-start.1 = (bf16[1,3,49,1536]{3,2,1,0:T(8,128)(2,1)S(1)}, bf16[1,3,49,1536]{3,2,1,0:T(8,128)(2,1)}, u32[]{:S(2)}) copy-start(bf16[1,3,49,1536]{3,2,1,0:T(8,128)(2,1)} %param.19) | copy-start | bytes 1354756
  7.2 19.4 %copy-start.4 = (f32[1536]{0:T(1024)S(1)}, f32[1536]{0:T(1024)}, u32[]{:S(2)}) copy-start(f32[1536]{0:T(1024)} %param.28) | copy-start | bytes 18436
  7.2 45.1 %all-gather.3.cloned.1.call-start = ((), (), s32[]{:S(2)}) async-start(), calls=%async_computation.1 | async-start | bytes 1966080 | tf_op jit(solution)/shard_map/all_gather | solution.py:122
  9.2 77.8 %all-gather.5.cloned.1.call-start = ((), (), s32[]{:S(2)}) async-start(), calls=%async_computation.2 | async-start | bytes 1310720 | tf_op jit(solution)/shard_map/all_gather | solution.py:172
  22.9 13.9 %collective-permute-start = (bf16[147,1536]{1,0:T(8,128)(2,1)}, bf16[147,1536]{1,0:T(8,128)(2,1)}, u32[]{:S(2)}, u32[]{:S(2)}) collective-permute-start(bf16[147,1536]{1,0:T(8,128)(2,1)} %reshape.160), channel_id=1, source_target_pairs={{0,2},{2,0},{1,3},{3,1},{4,6},{6,4},{5,7},{7,5},{8,10},{10,8},{9,1... | collective-permute-start | bytes 1354760 | tf_op jit(solution)/shard_map/ppermute | solution.py:146
  35.3 13.2 %copy-start.2 = (f32[3,1536]{1,0:T(4,128)S(1)}, f32[3,1536]{1,0:T(4,128)}, u32[]{:S(2)}) copy-start(f32[3,1536]{1,0:T(4,128)} %convert_reduce_fusion.1) | copy-start | bytes 55300
  35.4 13.2 %copy-start.7 = (f32[1536]{0:T(1024)S(1)}, f32[1536]{0:T(1024)}, u32[]{:S(2)}) copy-start(f32[1536]{0:T(1024)} %param.27) | copy-start | bytes 18436
  35.4 15.6 %copy-start.5 = (f32[1536]{0:T(1024)S(1)}, f32[1536]{0:T(1024)}, u32[]{:S(2)}) copy-start(f32[1536]{0:T(1024)} %param.30) | copy-start | bytes 18436
  35.4 15.6 %copy-start.6 = (f32[1536]{0:T(1024)S(1)}, f32[1536]{0:T(1024)}, u32[]{:S(2)}) copy-start(f32[1536]{0:T(1024)} %param.29) | copy-start | bytes 18436
  45.2 11.2 %copy-start.8 = (f32[1024]{0:T(1024)S(1)}, f32[1024]{0:T(1024)}, u32[]{:S(2)}) copy-start(f32[1024]{0:T(1024)} %param.33) | copy-start | bytes 12292
  46.6 11.4 %copy-start.10 = (f32[16]{0:T(128)S(1)}, f32[16]{0:T(128)}, u32[]{:S(2)}) copy-start(f32[16]{0:T(128)} %param.35) | copy-start | bytes 196
  46.6 11.5 %copy-start.9 = (s32[1,2,512]{2,1,0:T(2,128)S(1)}, s32[1,2,512]{2,1,0:T(2,128)}, u32[]{:S(2)}) copy-start(s32[1,2,512]{2,1,0:T(2,128)} %param.36) | copy-start | bytes 12292
  46.7 3.9 %collective-permute-start.1 = (f32[3,1536]{1,0:T(4,128)S(1)}, f32[3,1536]{1,0:T(4,128)S(1)}, u32[]{:S(2)}, u32[]{:S(2)}) collective-permute-start(f32[3,1536]{1,0:T(4,128)S(1)} %broadcast_multiply_fusion), channel_id=1, source_target_pairs={{0,2},{2,0},{1,3},{3,1},{4,6},{6,4},{5,7},{7,5},{8,10},{10,8},{9,1... | collective-permute-start | bytes 55304 | tf_op jit(solution)/shard_map/ppermute | solution.py:157
  48.5 3.8 %collective-permute-start.3 = (bf16[125,1536]{1,0:T(8,128)(2,1)S(1)}, bf16[125,1536]{1,0:T(8,128)(2,1)S(1)}, u32[]{:S(2)}, u32[]{:S(2)}) collective-permute-start(bf16[125,1536]{1,0:T(8,128)(2,1)S(1)} %slice_bitcast_fusion), channel_id=1, source_target_pairs={{0,1},{1,0},{2,3},{3,2},{4,5},{5,4},{6,7},{7,6},{8,9},{9,8},{10,11... | collective-permute-start | bytes 1152008 | tf_op jit(solution)/shard_map/ppermute | solution.py:154
  51.0 38.2 %copy-start.3 = (bf16[3,1536]{1,0:T(4,128)(2,1)}, bf16[3,1536]{1,0:T(4,128)(2,1)S(1)}, u32[]{:S(2)}) copy-start(bf16[3,1536]{1,0:T(4,128)(2,1)S(1)} %add_convert_fusion) | copy-start | bytes 27652
  51.0 1.2 %collective-permute-start.2 = (bf16[3,1536]{1,0:T(4,128)(2,1)S(1)}, bf16[3,1536]{1,0:T(4,128)(2,1)S(1)}, u32[]{:S(2)}, u32[]{:S(2)}) collective-permute-start(bf16[3,1536]{1,0:T(4,128)(2,1)S(1)} %add_convert_fusion), channel_id=1, source_target_pairs={{0,1},{1,0},{2,3},{3,2},{4,5},{5,4},{6,7},{7,6},{8,9},{9,8},{10,11... | collective-permute-start | bytes 27656 | tf_op jit(solution)/shard_map/ppermute | solution.py:164
  54.1 2.0 %collective-permute-start.4 = (f32[128,512]{1,0:T(8,128)S(1)}, f32[128,512]{1,0:T(8,128)S(1)}, u32[]{:S(2)}, u32[]{:S(2)}) collective-permute-start(f32[128,512]{1,0:T(8,128)S(1)} %fusion.91), channel_id=1, source_target_pairs={{0,1},{1,0},{2,3},{3,2},{4,5},{5,4},{6,7},{7,6},{8,9},{9,8},{10,11... | collective-permute-start | bytes 786440 | tf_op jit(solution)/shard_map/ppermute | solution.py:84
Sparse Core Ops, SparseCore 0:
  9.6 39.7 all-gather.2
  57.5 29.4 all-gather.4
